TPU v7x, 256 devices: a whole 4x4x8 slice. The times are simulated.
256 devices in a mesh: dp: 32 (over y, z), mp: 8 (over x, core).
Axes of the slice: x: 4, y: 4, z: 8, core: 2. Of those that a mesh axis runs over, the one named last changes fastest.
Arguments:
- hidden: bfloat16 [512, 32, 1024], P(('dp', 'mp')), may hold values from -96 to 96, as said below
- query_weight: bfloat16 [1024, 1024], P('dp', 'mp'), may hold values from -0.1875 to 0.1875
- w_key: bfloat16 [1024, 1024], P('dp', 'mp'), may hold values from -0.1875 to 0.1875
- w_value: bfloat16 [1024, 1024], P('dp', 'mp'), may hold values from -0.1875 to 0.1875
- rel_table: bfloat16 [512, 1024], P('dp'), may hold values from -6 to 6
- rel_bucket: int32 [32, 32], replicated, may hold values from 0 to 511
- w_out: bfloat16 [1024, 1024], P('mp', 'dp'), may hold values from -0.1875 to 0.1875
- w_up: bfloat16 [1024, 4096], P('dp', 'mp'), may hold values from -0.1875 to 0.1875
- w_down: bfloat16 [4096, 1024], P('mp', 'dp'), may hold values from -0.09375 to 0.09375
- w_proj: bfloat16 [1024, 128], P(('dp', 'mp')), may hold values from -0.1875 to 0.1875
- pages: bfloat16 [8192, 128, 128], P('dp'), may hold values from -0.59765625 to 0.59765625
- page_len: int32 [8192], P('dp'), may hold values from 1 to 128
- slot_per_page: int32 [8192], replicated, may hold values from 0 to 8191, as said below
- candidates: int32 [512, 16, 4], P(('dp', 'mp')), may hold values from 0 to 8191, as said below
Outputs:
- query_vectors: bfloat16 [512, 32, 128], P(('dp', 'mp'))
- scores: float32 [512, 16], P(('dp', 'mp'))
Inputs may be any that keep to these rules, and one draw needn't show every extreme that they name: slot_per_page is a permutation of the slots; the page in slot s is held by index s // 256 of dp. `candidates`: among the 128 page ids of the 2 queries of one device (queries in aligned blocks of 2), at most 8 have slots held by any one index of dp, and in every such block some index of dp holds exactly 8 of them. `hidden`: token states are finite.
All inputs are finite; a program needn't handle non-finite values.
Results may differ from a plain program's by a relative error of at most 0.025.
Values may be sent and summed in bfloat16 or wider, within the bound.
No kernel may reach another device: no remote copies, remote signals or barrier semaphores. Data moves between devices by JAX's collectives and lax.ppermute only.
A program may use at most 64 MiB of HBM per device.

v0:
```python
import jax
import jax.numpy as jnp
from jax import lax
from jax.sharding import PartitionSpec as P

HD = 64


def layer_norm(value):
    mean = jnp.mean(value, axis=-1, keepdims=True)
    centered = value - mean
    var = jnp.mean(centered * centered, axis=-1, keepdims=True)
    return centered / jnp.sqrt(var + 1e-07)


def add_rows(left, piece):
    return jnp.dot(left, piece, preferred_element_type=jnp.float32)


def return_maxima(maxima):
    return lax.all_to_all(
        maxima.astype(jnp.bfloat16), "dp", split_axis=0, concat_axis=0, tiled=True
    ).astype(maxima.dtype)


def body(
    hidden,
    query_weight,
    w_key,
    w_value,
    rel_table,
    rel_bucket,
    w_out,
    w_up,
    w_down,
    w_proj,
    pages,
    page_len,
    slot_per_page,
    candidates,
):
    qry_dev, qlen, width = hidden.shape
    heads_local = query_weight.shape[1] // HD
    cols = query_weight.shape[1]
    tokens = lax.all_gather(hidden, "mp", axis=0, tiled=True)
    group = tokens.shape[0]
    flat = tokens.reshape(group * qlen, width)
    left_rel = lax.all_gather(rel_table, "dp", axis=0, tiled=True)
    pieces = (
        lax.all_gather(query_weight, "dp", axis=0, tiled=True),
        lax.all_gather(w_key, "dp", axis=0, tiled=True),
        lax.all_gather(w_value, "dp", axis=0, tiled=True),
    )
    qsum = add_rows(flat, pieces[0])
    ksum = add_rows(flat, pieces[1])
    vsum = add_rows(flat, pieces[2])
    qrsum = add_rows(left_rel, pieces[0])
    krsum = add_rows(left_rel, pieces[1])
    rel_q = qrsum.astype(jnp.bfloat16)
    rel_k = krsum.astype(jnp.bfloat16)
    nbuck = rel_q.shape[0]
    qx = qsum.astype(jnp.bfloat16).reshape(group, qlen, heads_local, HD)
    kx = ksum.astype(jnp.bfloat16).reshape(group, qlen, heads_local, HD)
    vx = vsum.astype(jnp.bfloat16).reshape(group, qlen, heads_local, HD)
    rel_q = rel_q.reshape(nbuck, heads_local, HD)
    rel_k = rel_k.reshape(nbuck, heads_local, HD)
    onehot = (rel_bucket[:, :, None] == jnp.arange(nbuck, dtype=jnp.int32)[None, None, :]).astype(
        jnp.float32
    )
    scale = 1.0 / jnp.sqrt(jnp.float32(3 * HD))
    content = jnp.einsum("qihd,qjhd->qhij", qx, kx, preferred_element_type=jnp.float32)
    along_axis_name = jnp.einsum("qihd,bhd->qhib", qx, rel_k, preferred_element_type=jnp.float32)
    c2p = jnp.einsum("qhib,ijb->qhij", along_axis_name, onehot, precision=lax.Precision.HIGHEST)
    back = jnp.einsum("qjhd,bhd->qhjb", kx, rel_q, preferred_element_type=jnp.float32)
    p2c = jnp.einsum("qhjb,jib->qhij", back, onehot, precision=lax.Precision.HIGHEST)
    logits = (content + c2p + p2c) * scale
    probs = jax.nn.softmax(logits, axis=-1).astype(jnp.bfloat16)
    context_rows = jnp.einsum("qhij,qjhd->qihd", probs, vx, preferred_element_type=jnp.float32)
    context_rows = context_rows.astype(jnp.bfloat16).reshape(group * qlen, cols)
    attn_terms = jnp.dot(
        context_rows,
        lax.all_gather(w_out, "dp", axis=1, tiled=True),
        preferred_element_type=jnp.float32,
    )
    attn = lax.psum_scatter(
        attn_terms.astype(jnp.bfloat16), "mp", scatter_dimension=0, tiled=True
    ).astype(jnp.float32)
    own = hidden.reshape(qry_dev * qlen, width).astype(jnp.float32)
    mid = layer_norm(own + attn).astype(jnp.bfloat16)
    mid_all = lax.all_gather(mid, "mp", axis=0, tiled=True)
    up = add_rows(mid_all, lax.all_gather(w_up, "dp", axis=0, tiled=True))
    inner = jax.nn.gelu(up, approximate=False).astype(jnp.bfloat16)
    down_terms = jnp.dot(
        inner, lax.all_gather(w_down, "dp", axis=1, tiled=True), preferred_element_type=jnp.float32
    )
    mlp = lax.psum_scatter(
        down_terms.astype(jnp.bfloat16), "mp", scatter_dimension=0, tiled=True
    ).astype(jnp.float32)
    state = layer_norm(mid.astype(jnp.float32) + mlp).astype(jnp.bfloat16)
    width_out = w_proj.shape[1]
    proj = add_rows(state, lax.all_gather(w_proj, ("dp", "mp"), axis=0, tiled=True))
    vectors = (proj / jnp.sqrt(jnp.sum(proj * proj, axis=-1, keepdims=True) + 1e-06)).astype(
        jnp.bfloat16
    )
    vectors = vectors.reshape(qry_dev, qlen, width_out)
    page_owners = lax.axis_size("dp")
    pg_dev = pages.shape[0]
    ptok = pages.shape[1]
    ncand, ppc = (candidates.shape[1], candidates.shape[2])
    req = qry_dev * ncand * ppc
    cap = 2 * req // page_owners
    slots = slot_per_page[candidates.reshape(req)]
    dest = slots // pg_dev
    local = slots % pg_dev
    query_of = jnp.arange(req, dtype=jnp.int32) // (ncand * ppc)
    member = (dest[:, None] == jnp.arange(page_owners, dtype=jnp.int32)[None, :]).astype(jnp.int32)
    place = jnp.sum((jnp.cumsum(member, axis=0) - 1) * member, axis=1)
    index = dest * cap + place
    codes = jnp.full((page_owners * cap,), -1, jnp.int32).at[index].set(query_of * pg_dev + local)
    codes = codes.reshape(page_owners, cap)
    token_positions = jnp.arange(ptok, dtype=jnp.int32)
    rows_out = (
        jnp.zeros((page_owners * cap, qlen, width_out), jnp.bfloat16)
        .at[index]
        .set(vectors[query_of])
    )
    rows_out = rows_out.reshape(page_owners, cap, qlen, width_out)
    where_local = lax.all_to_all(codes, "dp", split_axis=0, concat_axis=0, tiled=True) % pg_dev
    chosen = pages[where_local]
    lens = page_len[where_local]
    sim = jnp.einsum(
        "snie,snte->snit",
        lax.all_to_all(rows_out, "dp", split_axis=0, concat_axis=0, tiled=True),
        chosen,
        preferred_element_type=jnp.float32,
    )
    valid = token_positions[None, None, None, :] < lens[:, :, None, None]
    returned = return_maxima(jnp.max(jnp.where(valid, sim, -1e30), axis=-1))
    best = returned.reshape(page_owners * cap, qlen)[index]
    best = best.reshape(qry_dev, ncand, ppc, qlen)
    scores = jnp.sum(jnp.max(best, axis=2), axis=-1)
    return (vectors, scores)


def solution(mesh):
    in_specs = (
        P(("dp", "mp"), None, None),
        P("dp", "mp"),
        P("dp", "mp"),
        P("dp", "mp"),
        P("dp", None),
        P(),
        P("mp", "dp"),
        P("dp", "mp"),
        P("mp", "dp"),
        P(("dp", "mp"), None),
        P("dp", None, None),
        P("dp"),
        P(),
        P(("dp", "mp"), None, None),
    )
    out_specs = (P(("dp", "mp"), None, None), P(("dp", "mp"), None))
    return jax.shard_map(body, mesh=mesh, in_specs=in_specs, out_specs=out_specs, check_vma=False)
```

profile of v0, /device:TPU:2, one launch (start us, length us, event | category | flops | bytes accessed | tf_op | source)
XLA Modules:
  0.0 620.8 jit_solution(7747046523202727993)
XLA Ops:
  8.7 52.7 %all_gather.32 = bf16[1024,128]{1,0:T(8,128)(2,1)S(1)} all-gather(bf16[32,128]{1,0:T(8,128)(2,1)} %param.15), channel_id=1, replica_groups=mesh['dp'=32,'mp'=8] {'dp'}, dimensions={0}, use_global_device_ids=true | all-gather | bytes 270336 | tf_op jit(solution)/shard_map/all_gather | solution.py:50
  61.4 48.4 %all_gather.33 = bf16[1024,128]{1,0:T(8,128)(2,1)S(1)} all-gather(bf16[32,128]{1,0:T(8,128)(2,1)} %param.16), channel_id=1, replica_groups=mesh['dp'=32,'mp'=8] {'dp'}, dimensions={0}, use_global_device_ids=true | all-gather | bytes 270336 | tf_op jit(solution)/shard_map/all_gather | solution.py:51
  109.8 47.0 %all_gather.31 = bf16[1024,128]{1,0:T(8,128)(2,1)S(1)} all-gather(bf16[32,128]{1,0:T(8,128)(2,1)} %param.17), channel_id=1, replica_groups=mesh['dp'=32,'mp'=8] {'dp'}, dimensions={0}, use_global_device_ids=true | all-gather | bytes 270336 | tf_op jit(solution)/shard_map/all_gather | solution.py:52
  156.8 48.2 %all_gather.35 = bf16[128,1024]{0,1:T(8,128)(2,1)S(1)} all-gather(bf16[128,32]{0,1:T(8,128)(2,1)} %param.20), channel_id=1, replica_groups=mesh['dp'=32,'mp'=8] {'dp'}, dimensions={1}, use_global_device_ids=true | all-gather | bytes 270336 | tf_op jit(solution)/shard_map/all_gather | solution.py:82
  205.1 1.7 convolution_convert_fusion.6
  206.9 1.7 convolution_convert_fusion.5
  209.4 1.7 convolution_convert_fusion.4
  219.7 27.9 %reduce-scatter.3.cloned.1.call-done = bf16[64,1024]{1,0:T(8,128)(2,1)} async-done(((bf16[512,1024]{1,0:T(8,128)(2,1)}), bf16[64,1024]{1,0:T(8,128)(2,1)}) %reduce-scatter.3.cloned.1.call-update) | async-done | bytes 131088 | tf_op jit(solution)/shard_map/reduce_scatter | solution.py:85
  249.8 1.7 divide_convert_fusion.3
  251.8 76.6 %all-gather.13.cloned.1.call-done = bf16[1024,512]{1,0:T(8,128)(2,1)} async-done(((bf16[32,512]{1,0:T(8,128)(2,1)}), bf16[1024,512]{1,0:T(8,128)(2,1)}) %all-gather.13.cloned.1.call-update) | async-done | bytes 1048592 | tf_op jit(solution)/shard_map/all_gather | solution.py:91
  328.4 76.3 %all-gather.15.cloned.1.call-done = bf16[512,1024]{0,1:T(8,128)(2,1)} async-done(((bf16[512,32]{0,1:T(8,128)(2,1)}), bf16[512,1024]{0,1:T(8,128)(2,1)}) %all-gather.15.cloned.1.call-update) | async-done | bytes 1048592 | tf_op jit(solution)/shard_map/all_gather | solution.py:94
  404.7 23.4 %all-gather.11.cloned.1.call-done = bf16[512,1024]{1,0:T(8,128)(2,1)} async-done(((bf16[64,1024]{1,0:T(8,128)(2,1)}), bf16[512,1024]{1,0:T(8,128)(2,1)}) %all-gather.11.cloned.1.call-update) | async-done | bytes 1048592 | tf_op jit(solution)/shard_map/all_gather | solution.py:90
  428.1 6.2 %convolution_convert_fusion.1 = bf16[512,1024]{1,0:T(8,128)(2,1)} fusion(bf16[512,1024]{0,1:T(8,128)(2,1)} %all-gather.15.cloned.1.call-done, bf16[512,1024]{1,0:T(8,128)(2,1)} %all-gather.11.cloned.1.call-done, bf16[1024,512]{1,0:T(8,128)(2,1)} %all-gather.13.cloned.1.call-done), kind=kOutput, calls=%fused_computation.17 | convolution fusion | flops 1091305472 | bytes 4194304 | tf_op jit(solution)/shard_map/dot_general | solution.py:93
  437.9 9.8 %all-to-all-start = ((s32[32,1,8]{2,1,0:T(1,128)}), s32[32,1,8]{2,1,0:T(1,128)S(1)}, u32[]{:S(2)}, u32[]{:S(2)}) async-start(s32[32,1,8]{2,1,0:T(1,128)} %bitcast.21), calls=%async_computation.2 | async-start | bytes 32768 | tf_op jit(solution)/shard_map/all_to_all | solution.py:128
  447.8 62.5 %all-gather = bf16[256,4,128]{2,1,0:T(4,128)(2,1)S(1)} all-gather(bf16[1,4,128]{2,1,0:T(4,128)(2,1)S(1)} %bitcast.96), channel_id=1, replica_groups=mesh['dp'=32,'mp'=8] {'dp','mp'}, dimensions={0}, use_global_device_ids=true | all-gather | bytes 263168 | tf_op jit(solution)/shard_map/all_gather | solution.py:101
  514.6 1.7 broadcast_in_dim.14
  516.3 13.7 %scatter_fusion = bf16[256,32,128]{2,1,0:T(8,128)(2,1)} fusion(bf16[256,32,128]{2,1,0:T(8,128)(2,1)} %broadcast_in_dim.14, s32[128]{0:T(128)S(1)} %fusion.75, bf16[128,32,128]{2,1,0:T(8,128)(2,1)S(1)} %gather_fusion.2), kind=kCustom, calls=%fused_computation.6 | custom fusion | bytes 3146240 | tf_op jit(solution)/shard_map/scatter | solution.py:125
  530.0 7.2 %all-to-all-start.1 = ((bf16[32,8,32,128]{3,2,1,0:T(8,128)(2,1)}), bf16[32,8,32,128]{3,2,1,0:T(8,128)(2,1)S(1)}, u32[]{:S(2)}, u32[]{:S(2)}) async-start(bf16[32,8,32,128]{3,2,1,0:T(8,128)(2,1)} %bitcast.24), calls=%async_computation.3 | async-start | bytes 4194304 | tf_op jit(solution)/shard_map/all_to_all | solution.py:133
  537.4 12.0 %gather_fusion.3 = bf16[256,128,128]{2,1,0:T(8,128)(2,1)} fusion(bf16[256,128,128]{2,1,0:T(8,128)(2,1)} %param.24, s32[1024]{0:T(1024)S(1)} %pad_clamp_fusion.2), kind=kCustom, calls=%fused_computation.3 | custom fusion | bytes 16778240 | tf_op jit(solution)/shard_map/gather | solution.py:129
  549.4 1.9 gather_fusion.1
  551.5 36.0 %all-to-all-done.1 = bf16[32,8,32,128]{3,2,1,0:T(8,128)(2,1)S(1)} async-done(((bf16[32,8,32,128]{3,2,1,0:T(8,128)(2,1)}), bf16[32,8,32,128]{3,2,1,0:T(8,128)(2,1)S(1)}, u32[]{:S(2)}, u32[]{:S(2)}) %all-to-all-start.1) | async-done | bytes 2097184 | tf_op jit(solution)/shard_map/all_to_all | solution.py:133
  587.6 8.0 %select_reduce_fusion = bf16[32,8,32]{2,1,0:T(8,128)(2,1)S(1)} fusion(bf16[32,8,32,128]{3,2,1,0:T(8,128)(2,1)S(1)} %all-to-all-done.1, bf16[32,8,128,128]{3,2,1,0:T(8,128)(2,1)} %bitcast.87, pred[32,8,128]{2,1,0:T(8,128)(4,1)S(1)} %iota_compare_fusion.1), kind=kOutput, calls=%fused_computation.8 | convolution fusion | flops 270524416 | bytes 10534912 | tf_op jit(solution)/shard_map/snie,snte->snit/dot_general | solution.py:131
  596.2 6.4 %all-to-all-start.2 = ((bf16[32,2,128]{2,1,0:T(2,128)(2,1)}), bf16[32,2,128]{2,1,0:T(2,128)(2,1)S(1)}, u32[]{:S(2)}, u32[]{:S(2)}) async-start(bf16[32,2,128]{2,1,0:T(2,128)(2,1)} %reshape.374), calls=%async_computation.4 | async-start | bytes 32768 | tf_op jit(solution)/shard_map/all_to_all | solution.py:21
  602.7 9.8 %all-to-all-done.2 = bf16[32,2,128]{2,1,0:T(2,128)(2,1)S(1)} async-done(((bf16[32,2,128]{2,1,0:T(2,128)(2,1)}), bf16[32,2,128]{2,1,0:T(2,128)(2,1)S(1)}, u32[]{:S(2)}, u32[]{:S(2)}) %all-to-all-start.2) | async-done | bytes 16416 | tf_op jit(solution)/shard_map/all_to_all | solution.py:21
  (92 shorter events, 23.5 us)
Async XLA Ops:
  7.2 427.4 %copy-start = (s32[8192]{0:T(1024)S(1)}, s32[8192]{0:T(1024)}, u32[]{:S(2)}) copy-start(s32[8192]{0:T(1024)} %param.26) | copy-start | bytes 98308
  7.2 197.9 %all-gather.7.cloned.1.call-start = ((), (), s32[]{:S(2)}) async-start(), calls=%async_computation.5 | async-start | bytes 1179648 | tf_op jit(solution)/shard_map/all_gather | solution.py:45
  7.9 201.5 %all-gather.9.cloned.1.call-start = ((), (), s32[]{:S(2)}) async-start(), calls=%async_computation.6 | async-start | bytes 1081344 | tf_op jit(solution)/shard_map/all_gather | solution.py:48
  8.7 239.0 %reduce-scatter.3.cloned.1.call-start = ((), (), s32[]{:S(2)}) async-start(), calls=%async_computation.7 | async-start | bytes 1179648 | tf_op jit(solution)/shard_map/reduce_scatter | solution.py:85
  205.0 3.7 copy-start.3
  209.2 2.4 copy-start.7
  211.6 1.7 copy-start.4
  216.7 31.0 %copy-start.5 = (bf16[2,32,1024]{2,1,0:T(8,128)(2,1)S(1)}, bf16[2,32,1024]{2,1,0:T(8,128)(2,1)}, u32[]{:S(2)}) copy-start(bf16[2,32,1024]{2,1,0:T(8,128)(2,1)} %param.14) | copy-start | bytes 393220
  218.5 109.9 %all-gather.13.cloned.1.call-start = ((), (), s32[]{:S(2)}) async-start(), calls=%async_computation.9 | async-start | bytes 1081344 | tf_op jit(solution)/shard_map/all_gather | solution.py:91
  219.1 185.6 %all-gather.15.cloned.1.call-start = ((), (), s32[]{:S(2)}) async-start(), calls=%async_computation.10 | async-start | bytes 1081344 | tf_op jit(solution)/shard_map/all_gather | solution.py:94
  219.7 208.4 %all-gather.11.cloned.1.call-start = ((), (), s32[]{:S(2)}) async-start(), calls=%async_computation.8 | async-start | bytes 1179648 | tf_op jit(solution)/shard_map/all_gather | solution.py:90
  251.5 182.8 %copy-start.8 = (s32[2,16,4]{1,2,0:T(4,128)S(1)}, s32[2,16,4]{1,2,0:T(4,128)}, u32[]{:S(2)}) copy-start(s32[2,16,4]{1,2,0:T(4,128)} %param.27) | copy-start | bytes 1540
  251.5 196.2 %copy-start.9 = (bf16[4,128]{1,0:T(4,128)(2,1)S(1)}, bf16[4,128]{1,0:T(4,128)(2,1)}, u32[]{:S(2)}) copy-start(bf16[4,128]{1,0:T(4,128)(2,1)} %param.23) | copy-start | bytes 3076
  251.5 258.7 %reduce-scatter.5.cloned.1.call-start = ((), (), s32[]{:S(2)}) async-start(), calls=%async_computation.11 | async-start | bytes 1179648 | tf_op jit(solution)/shard_map/reduce_scatter | solution.py:96
  434.3 76.0 %copy-start.6 = (bf16[64,1024]{1,0:T(8,128)(2,1)S(1)}, bf16[64,1024]{1,0:T(8,128)(2,1)}, u32[]{:S(2)}) copy-start(bf16[64,1024]{1,0:T(8,128)(2,1)} %divide_convert_fusion.3) | copy-start | bytes 393220
  437.9 92.1 %all-to-all-start = ((s32[32,1,8]{2,1,0:T(1,128)}), s32[32,1,8]{2,1,0:T(1,128)S(1)}, u32[]{:S(2)}, u32[]{:S(2)}) async-start(s32[32,1,8]{2,1,0:T(1,128)} %bitcast.21), calls=%async_computation.2 | async-start | bytes 32768 | tf_op jit(solution)/shard_map/all_to_all | solution.py:128
  513.8 2.5 copy-start.2
  530.0 57.6 %all-to-all-start.1 = ((bf16[32,8,32,128]{3,2,1,0:T(8,128)(2,1)}), bf16[32,8,32,128]{3,2,1,0:T(8,128)(2,1)S(1)}, u32[]{:S(2)}, u32[]{:S(2)}) async-start(bf16[32,8,32,128]{3,2,1,0:T(8,128)(2,1)} %bitcast.24), calls=%async_computation.3 | async-start | bytes 4194304 | tf_op jit(solution)/shard_map/all_to_all | solution.py:133
  537.3 12.0 %copy-start.1 = (s32[256]{0:T(256)S(1)}, s32[256]{0:T(256)}, u32[]{:S(2)}) copy-start(s32[256]{0:T(256)} %param.25) | copy-start | bytes 3076
  596.2 16.2 %all-to-all-start.2 = ((bf16[32,2,128]{2,1,0:T(2,128)(2,1)}), bf16[32,2,128]{2,1,0:T(2,128)(2,1)S(1)}, u32[]{:S(2)}, u32[]{:S(2)}) async-start(bf16[32,2,128]{2,1,0:T(2,128)(2,1)} %reshape.374), calls=%async_computation.4 | async-start | bytes 32768 | tf_op jit(solution)/shard_map/all_to_all | solution.py:21
Sparse Core Ops, SparseCore 0:
  9.8 27.1 all-gather.6
  39.7 78.0 all-gather.8
  218.7 28.9 reduce-scatter.2
  250.1 78.2 all-gather.12
  330.8 73.8 all-gather.14
  406.4 21.5 all-gather.10
  434.4 33.3 reduce-scatter.4
where the time goes:
time: 622 us; the launch traced here: 621 us
  blocking collectives  259 us (42%)
  waiting for transfers between devices  253 us (41%)
  local copies, waits for them, and re-layouts  35.9 us (6%)
  matrix products  27.4 us (4%)
  starting transfers between devices  24 us (4%)
  between operations  14.6 us (2%)
  other arithmetic  7.57 us (1%)
    all_gather x1, waiting for transfers between devices, body(): up = add_rows(mid_all, lax.all_gather(w_up, 'dp', axis=0, tiled=True))  76.6 us
    all_gather x1, waiting for transfers between devices, body(): lax.all_gather(w_down, 'dp', axis=1, tiled=True)  76.3 us
    all_gather x1, blocking collectives, body(): lax.all_gather(w_proj, ('dp', 'mp'), axis=0, tiled=True)  62.5 us
    all_gather x1, blocking collectives, body(): lax.all_gather(query_weight, 'dp', axis=0, tiled=True)  52.7 us
    all_gather x1, blocking collectives, body(): lax.all_gather(w_key, 'dp', axis=0, tiled=True)  48.4 us
    all_gather x1, blocking collectives, body(): lax.all_gather(w_out, 'dp', axis=1, tiled=True)  48.2 us
    all_gather x1, blocking collectives, body(): lax.all_gather(w_value, 'dp', axis=0, tiled=True)  47 us
    all_to_all x1, waiting for transfers between devices, body(): lax.all_to_all(rows_out, 'dp', split_axis=0, concat_axis=0, tiled=True)  36 us
  transfers between devices with their start and end apart: 10, of which 6 were waited for; matrix products, arithmetic and copies ran while one was open for 7% of the time, Pallas kernels for 0%

commit v1 on v0

--- a/solution.py
+++ b/solution.py
@@ -42,20 +42,59 @@
     qry_dev, qlen, width = hidden.shape
     heads_local = query_weight.shape[1] // HD
     cols = query_weight.shape[1]
+    page_owners = lax.axis_size("dp")
+    n_mp = lax.axis_size("mp")
+
+    pg_dev = pages.shape[0]
+    ptok = pages.shape[1]
+    ncand, ppc = (candidates.shape[1], candidates.shape[2])
+    req = qry_dev * ncand * ppc
+    cap = 2 * req // page_owners
+    slots = slot_per_page[candidates.reshape(req)]
+    dest = slots // pg_dev
+    local = slots % pg_dev
+    query_of = jnp.arange(req, dtype=jnp.int32) // (ncand * ppc)
+    member = (dest[:, None] == jnp.arange(page_owners, dtype=jnp.int32)[None, :]).astype(jnp.int32)
+    place = jnp.sum((jnp.cumsum(member, axis=0) - 1) * member, axis=1)
+    index = dest * cap + place
+    codes = jnp.full((page_owners * cap,), -1, jnp.int32).at[index].set(query_of * pg_dev + local)
+    codes = codes.reshape(page_owners, cap)
+    got = lax.all_to_all(codes, "dp", split_axis=0, concat_axis=0, tiled=True)
+    where_local = got % pg_dev
+    which_query = jnp.clip(got // pg_dev, 0, qry_dev - 1)
+    chosen = pages[where_local]
+    lens = page_len[where_local]
+
+    w_out_t = w_out.T
+    w_down_t = w_down.T
+    pieces = (query_weight, w_key, w_value, w_out_t, w_up, w_down_t, rel_table, w_proj)
+    flat_pieces = jnp.concatenate([p.reshape(-1) for p in pieces])
+    gathered = lax.all_gather(flat_pieces, "dp", axis=0, tiled=False)
+    parts = []
+    start = 0
+    for p in pieces:
+        size = p.size
+        parts.append(gathered[:, start : start + size].reshape((page_owners,) + p.shape))
+        start += size
+    g_q, g_k, g_v, g_out, g_up, g_down, g_rel, g_proj = parts
+    wq = g_q.reshape(page_owners * query_weight.shape[0], cols)
+    wk = g_k.reshape(page_owners * w_key.shape[0], cols)
+    wv = g_v.reshape(page_owners * w_value.shape[0], cols)
+    wo = jnp.transpose(g_out, (2, 0, 1)).reshape(w_out.shape[0], page_owners * w_out.shape[1])
+    wu = g_up.reshape(page_owners * w_up.shape[0], w_up.shape[1])
+    wd = jnp.transpose(g_down, (2, 0, 1)).reshape(w_down.shape[0], page_owners * w_down.shape[1])
+    left_rel = g_rel.reshape(page_owners * rel_table.shape[0], rel_table.shape[1])
+    proj_all = lax.all_gather(g_proj, "mp", axis=0, tiled=False)
+    wp = jnp.transpose(proj_all, (1, 0, 2, 3)).reshape(page_owners * n_mp * w_proj.shape[0], w_proj.shape[1])
+
     tokens = lax.all_gather(hidden, "mp", axis=0, tiled=True)
     group = tokens.shape[0]
     flat = tokens.reshape(group * qlen, width)
-    left_rel = lax.all_gather(rel_table, "dp", axis=0, tiled=True)
-    pieces = (
-        lax.all_gather(query_weight, "dp", axis=0, tiled=True),
-        lax.all_gather(w_key, "dp", axis=0, tiled=True),
-        lax.all_gather(w_value, "dp", axis=0, tiled=True),
-    )
-    qsum = add_rows(flat, pieces[0])
-    ksum = add_rows(flat, pieces[1])
-    vsum = add_rows(flat, pieces[2])
-    qrsum = add_rows(left_rel, pieces[0])
-    krsum = add_rows(left_rel, pieces[1])
+    qsum = add_rows(flat, wq)
+    ksum = add_rows(flat, wk)
+    vsum = add_rows(flat, wv)
+    qrsum = add_rows(left_rel, wq)
+    krsum = add_rows(left_rel, wk)
     rel_q = qrsum.astype(jnp.bfloat16)
     rel_k = krsum.astype(jnp.bfloat16)
     nbuck = rel_q.shape[0]
@@ -77,63 +116,32 @@
     probs = jax.nn.softmax(logits, axis=-1).astype(jnp.bfloat16)
     context_rows = jnp.einsum("qhij,qjhd->qihd", probs, vx, preferred_element_type=jnp.float32)
     context_rows = context_rows.astype(jnp.bfloat16).reshape(group * qlen, cols)
-    attn_terms = jnp.dot(
-        context_rows,
-        lax.all_gather(w_out, "dp", axis=1, tiled=True),
-        preferred_element_type=jnp.float32,
-    )
+    attn_terms = jnp.dot(context_rows, wo, preferred_element_type=jnp.float32)
     attn = lax.psum_scatter(
         attn_terms.astype(jnp.bfloat16), "mp", scatter_dimension=0, tiled=True
     ).astype(jnp.float32)
     own = hidden.reshape(qry_dev * qlen, width).astype(jnp.float32)
     mid = layer_norm(own + attn).astype(jnp.bfloat16)
     mid_all = lax.all_gather(mid, "mp", axis=0, tiled=True)
-    up = add_rows(mid_all, lax.all_gather(w_up, "dp", axis=0, tiled=True))
+    up = add_rows(mid_all, wu)
     inner = jax.nn.gelu(up, approximate=False).astype(jnp.bfloat16)
-    down_terms = jnp.dot(
-        inner, lax.all_gather(w_down, "dp", axis=1, tiled=True), preferred_element_type=jnp.float32
-    )
+    down_terms = jnp.dot(inner, wd, preferred_element_type=jnp.float32)
     mlp = lax.psum_scatter(
         down_terms.astype(jnp.bfloat16), "mp", scatter_dimension=0, tiled=True
     ).astype(jnp.float32)
     state = layer_norm(mid.astype(jnp.float32) + mlp).astype(jnp.bfloat16)
     width_out = w_proj.shape[1]
-    proj = add_rows(state, lax.all_gather(w_proj, ("dp", "mp"), axis=0, tiled=True))
+    proj = add_rows(state, wp)
     vectors = (proj / jnp.sqrt(jnp.sum(proj * proj, axis=-1, keepdims=True) + 1e-06)).astype(
         jnp.bfloat16
     )
     vectors = vectors.reshape(qry_dev, qlen, width_out)
-    page_owners = lax.axis_size("dp")
-    pg_dev = pages.shape[0]
-    ptok = pages.shape[1]
-    ncand, ppc = (candidates.shape[1], candidates.shape[2])
-    req = qry_dev * ncand * ppc
-    cap = 2 * req // page_owners
-    slots = slot_per_page[candidates.reshape(req)]
-    dest = slots // pg_dev
-    local = slots % pg_dev
-    query_of = jnp.arange(req, dtype=jnp.int32) // (ncand * ppc)
-    member = (dest[:, None] == jnp.arange(page_owners, dtype=jnp.int32)[None, :]).astype(jnp.int32)
-    place = jnp.sum((jnp.cumsum(member, axis=0) - 1) * member, axis=1)
-    index = dest * cap + place
-    codes = jnp.full((page_owners * cap,), -1, jnp.int32).at[index].set(query_of * pg_dev + local)
-    codes = codes.reshape(page_owners, cap)
+
+    sent = jnp.broadcast_to(vectors[None], (page_owners, qry_dev, qlen, width_out))
+    recv = lax.all_to_all(sent, "dp", split_axis=0, concat_axis=0, tiled=True)
+    rows_in = jnp.take_along_axis(recv, which_query[:, :, None, None], axis=1)
     token_positions = jnp.arange(ptok, dtype=jnp.int32)
-    rows_out = (
-        jnp.zeros((page_owners * cap, qlen, width_out), jnp.bfloat16)
-        .at[index]
-        .set(vectors[query_of])
-    )
-    rows_out = rows_out.reshape(page_owners, cap, qlen, width_out)
-    where_local = lax.all_to_all(codes, "dp", split_axis=0, concat_axis=0, tiled=True) % pg_dev
-    chosen = pages[where_local]
-    lens = page_len[where_local]
-    sim = jnp.einsum(
-        "snie,snte->snit",
-        lax.all_to_all(rows_out, "dp", split_axis=0, concat_axis=0, tiled=True),
-        chosen,
-        preferred_element_type=jnp.float32,
-    )
+    sim = jnp.einsum("snie,snte->snit", rows_in, chosen, preferred_element_type=jnp.float32)
     valid = token_positions[None, None, None, :] < lens[:, :, None, None]
     returned = return_maxima(jnp.max(jnp.where(valid, sim, -1e30), axis=-1))
     best = returned.reshape(page_owners * cap, qlen)[index]

time: 622 us -> 332 us (0.53)
  blocking collectives: 259 us -> 10.7 us
  waiting for transfers between devices: 253 us -> 190 us
  local copies, waits for them, and re-layouts: 35.9 us -> 45.7 us
    all_gather x5 -> x1, blocking collectives: 259 us -> 10.7 us  [body(): proj_all = lax.all_gather(g_proj, 'mp', axis=0, tiled=False)]
    all_gather x3 -> x1, waiting for transfers between devices: 153 us -> 101 us  [body(): gathered = lax.all_gather(flat_pieces, 'dp', axis=0, tiled=False)]
    all_to_all x2, waiting for transfers between devices: 36 us -> 2.08 us  [the longest x1 2.07 us: body(): recv = lax.all_to_all(sent, 'dp', split_axis=0, concat_axis=0, tiled=True)]
    scatter x1 -> x0, local copies, waits for them, and re-layouts: 13.7 us -> none  [body(): rows_out = jnp.zeros((page_owners * cap, qlen, width_out), jnp.bfloat16)....]
    unnamed x23 -> x46, local copies, waits for them, and re-layouts: 0.94 us -> 13.4 us
    all_gather x1, waiting for transfers between devices: 0.01 us -> 9.38 us  [body(): tokens = lax.all_gather(hidden, 'mp', axis=0, tiled=True)]
    reduce_scatter x1, waiting for transfers between devices: 0.01 us -> 9.05 us  [body(): lax.psum_scatter(down_terms.astype(jnp.bfloat16), 'mp', scatter_dimension...]
  transfers between devices with their start and end apart: 10 -> 8, of which waited for: 6 -> 7; matrix products, arithmetic and copies ran while one was open for 7% -> 11% of each run, Pallas kernels for 0% -> 0%
where the time goes in v1:
time: 332 us; the launch traced here: 329 us
  waiting for transfers between devices  190 us (57%)
  local copies, waits for them, and re-layouts  45.7 us (14%)
  matrix products  32.7 us (10%)
  starting transfers between devices  27.7 us (8%)
  between operations  14.3 us (4%)
  blocking collectives  10.7 us (3%)
  other arithmetic  7.6 us (2%)
    all_gather x1, waiting for transfers between devices, body(): gathered = lax.all_gather(flat_pieces, 'dp', axis=0, tiled=False)  101 us
    reduce_scatter x1, waiting for transfers between devices, body(): lax.psum_scatter(attn_terms.astype(jnp.bfloat16), 'mp', scatter_dimension...  33.3 us
    all_gather x1, waiting for transfers between devices, body(): mid_all = lax.all_gather(mid, 'mp', axis=0, tiled=True)  25.2 us
    unnamed x46, local copies, waits for them, and re-layouts  13.4 us
    gather x1, local copies, waits for them, and re-layouts, body(): chosen = pages[where_local]  11.8 us
    all_gather x1, blocking collectives, body(): proj_all = lax.all_gather(g_proj, 'mp', axis=0, tiled=False)  10.7 us
    all_to_all x1, starting transfers between devices, body(): recv = lax.all_to_all(sent, 'dp', split_axis=0, concat_axis=0, tiled=True)  9.93 us
    all_to_all x1, starting transfers between devices, body(): got = lax.all_to_all(codes, 'dp', split_axis=0, concat_axis=0, tiled=True)  9.85 us
  transfers between devices with their start and end apart: 8, of which 7 were waited for; matrix products, arithmetic and copies ran while one was open for 11% of the time, Pallas kernels for 0%

profile of v1, /device:TPU:2, one launch (start us, length us, event | category | flops | bytes accessed | tf_op | source)
XLA Modules:
  0.0 328.7 jit_solution(3690136183016734294)
XLA Ops:
  14.7 100.6 %all-gather.10.cloned.1.call-done = bf16[32,1,66048]{2,1,0:T(2,128)(2,1)} async-done(((bf16[1,1,66048]{2,1,0:T(2,128)(2,1)}), bf16[32,1,66048]{2,1,0:T(2,128)(2,1)}) %all-gather.10.cloned.1.call-update) | async-done | bytes 4227088 | tf_op jit(solution)/shard_map/all_gather | solution.py:72
  115.3 3.9 %copy.85 = bf16[32,1,66048]{2,0,1:T(8,128)(2,1)S(1)} copy(bf16[32,1,66048]{2,1,0:T(2,128)(2,1)} %all-gather.10.cloned.1.call-done) | data formatting | bytes 8454144
  124.0 1.8 reshape_reshape.17
  127.0 2.1 convolution_convert_fusion.4
  129.0 9.4 %all-gather.6.cloned.1.call-done = bf16[16,32,1024]{2,1,0:T(8,128)(2,1)} async-done(((bf16[2,32,1024]{2,1,0:T(8,128)(2,1)}), bf16[16,32,1024]{2,1,0:T(8,128)(2,1)}) %all-gather.6.cloned.1.call-update) | async-done | bytes 1048592 | tf_op jit(solution)/shard_map/all_gather | solution.py:90
  138.4 1.8 fusion.17
  140.3 1.7 fusion.16
  143.0 2.2 fusion.1
  145.7 2.2 fusion.3
  147.9 2.2 copy.56
  150.1 1.7 fusion.13
  159.6 33.3 %reduce-scatter.3.cloned.1.call-done = bf16[64,1024]{1,0:T(8,128)(2,1)} async-done(((bf16[512,1024]{1,0:T(8,128)(2,1)}), bf16[64,1024]{1,0:T(8,128)(2,1)}) %reduce-scatter.3.cloned.1.call-update) | async-done | bytes 131088 | tf_op jit(solution)/shard_map/reduce_scatter | solution.py:120
  197.9 25.2 %all-gather.8.cloned.1.call-done = bf16[512,1024]{1,0:T(8,128)(2,1)} async-done(((bf16[64,1024]{1,0:T(8,128)(2,1)}), bf16[512,1024]{1,0:T(8,128)(2,1)}) %all-gather.8.cloned.1.call-update) | async-done | bytes 1048592 | tf_op jit(solution)/shard_map/all_gather | solution.py:125
  223.0 5.6 %convolution_convert_fusion.1 = bf16[512,1024]{1,0:T(8,128)(2,1)} fusion(bf16[512,1024]{0,1:T(8,128)(2,1)S(1)} %bitcast.137, bf16[512,1024]{1,0:T(8,128)(2,1)} %all-gather.8.cloned.1.call-done, bf16[1024,512]{1,0:T(8,128)(2,1)S(1)} %reshape_reshape.19), kind=kOutput, calls=%fused_computation.19 | convolution fusion | flops 1091305472 | bytes 4194304 | tf_op jit(solution)/shard_map/dot_general | solution.py:128
  232.2 9.8 %all-to-all-start = ((s32[32,1,8]{2,1,0:T(1,128)}), s32[32,1,8]{2,1,0:T(1,128)S(1)}, u32[]{:S(2)}, u32[]{:S(2)}) async-start(s32[32,1,8]{2,1,0:T(1,128)} %bitcast.36), calls=%async_computation.2 | async-start | bytes 32768 | tf_op jit(solution)/shard_map/all_to_all | solution.py:62
  242.8 10.7 %all_gather.19 = bf16[8,32,4,128]{3,2,0,1:T(4,128)(2,1)S(1)} all-gather(bf16[1,32,4,128]{3,2,0,1:T(4,128)(2,1)S(1)} %bitcast.145), channel_id=1, replica_groups=mesh['dp'=32,'mp'=8] {'mp'}, dimensions={0}, use_global_device_ids=true | all-gather | bytes 294912 | tf_op jit(solution)/shard_map/all_gather | solution.py:87
  253.5 9.1 %reduce-scatter.5.cloned.1.call-done = bf16[64,1024]{1,0:T(8,128)(2,1)} async-done(((bf16[512,1024]{1,0:T(8,128)(2,1)}), bf16[64,1024]{1,0:T(8,128)(2,1)}) %reduce-scatter.5.cloned.1.call-update) | async-done | bytes 131088 | tf_op jit(solution)/shard_map/reduce_scatter | solution.py:129
  267.1 9.9 %all-to-all-start.1 = ((bf16[32,2,32,128]{3,2,1,0:T(8,128)(2,1)}), bf16[32,2,32,128]{3,2,1,0:T(8,128)(2,1)S(1)}, u32[]{:S(2)}, u32[]{:S(2)}) async-start(bf16[32,2,32,128]{3,2,1,0:T(8,128)(2,1)} %broadcast_in_dim.21), calls=%async_computation.3 | async-start | bytes 1048576 | tf_op jit(solution)/shard_map/all_to_all | solution.py:141
  277.3 11.8 %gather_fusion.2 = bf16[256,128,128]{2,1,0:T(8,128)(2,1)} fusion(bf16[256,128,128]{2,1,0:T(8,128)(2,1)} %param.24, s32[1024]{0:T(1024)S(1)} %pad_clamp_fusion.1), kind=kCustom, calls=%fused_computation.2 | custom fusion | bytes 16778240 | tf_op jit(solution)/shard_map/gather | solution.py:65
  289.1 1.9 gather_fusion.1
  291.2 2.1 all-to-all-done.1
  294.7 8.0 %select_reduce_fusion = bf16[32,8,32]{2,1,0:T(8,128)(2,1)S(1)} fusion(bf16[32,8,128,128]{3,2,1,0:T(8,128)(2,1)} %bitcast.134, bf16[32,8,32,128]{3,2,1,0:T(8,128)(2,1)S(1)} %bitcast.136, pred[32,8]{1,0:T(8,128)(4,1)S(1)} %compare_and_fusion, pred[32,8,128]{2,1,0:T(8,128)(4,1)S(1)} %iota_compare_fusion.1), kind=kOutput, calls=%fused_computation.8 | convolution fusion | flops 271572992 | bytes 10535168 | tf_op jit(solution)/shard_map/snie,snte->snit/dot_general | solution.py:144
  303.4 7.5 %all-to-all-start.2 = ((bf16[32,2,128]{2,1,0:T(2,128)(2,1)}), bf16[32,2,128]{2,1,0:T(2,128)(2,1)S(1)}, u32[]{:S(2)}, u32[]{:S(2)}) async-start(bf16[32,2,128]{2,1,0:T(2,128)(2,1)} %reshape.452), calls=%async_computation.4 | async-start | bytes 32768 | tf_op jit(solution)/shard_map/all_to_all | solution.py:21
  310.9 9.8 %all-to-all-done.2 = bf16[32,2,128]{2,1,0:T(2,128)(2,1)S(1)} async-done(((bf16[32,2,128]{2,1,0:T(2,128)(2,1)}), bf16[32,2,128]{2,1,0:T(2,128)(2,1)S(1)}, u32[]{:S(2)}, u32[]{:S(2)}) %all-to-all-start.2) | async-done | bytes 16416 | tf_op jit(solution)/shard_map/all_to_all | solution.py:21
  (116 shorter events, 40.2 us)
Async XLA Ops:
  7.2 221.7 %copy-start = (s32[8192]{0:T(1024)S(1)}, s32[8192]{0:T(1024)}, u32[]{:S(2)}) copy-start(s32[8192]{0:T(1024)} %param.26) | copy-start | bytes 98308
  7.2 108.1 %all-gather.10.cloned.1.call-start = ((), (), s32[]{:S(2)}) async-start(), calls=%async_computation.9 | async-start | bytes 8718336 | tf_op jit(solution)/shard_map/all_gather | solution.py:72
  13.9 124.5 %all-gather.6.cloned.1.call-start = ((), (), s32[]{:S(2)}) async-start(), calls=%async_computation.5 | async-start | bytes 1179648 | tf_op jit(solution)/shard_map/all_gather | solution.py:90
  14.7 178.2 %reduce-scatter.3.cloned.1.call-start = ((), (), s32[]{:S(2)}) async-start(), calls=%async_computation.6 | async-start | bytes 1179648 | tf_op jit(solution)/shard_map/reduce_scatter | solution.py:120
  119.1 2.3 copy-start.2
  138.4 4.1 %copy-start.10 = (bf16[512,128]{0,1:T(8,128)(2,1)S(1)}, bf16[512,128]{0,1:T(8,128)(2,1)}, u32[]{:S(2)}) copy-start(bf16[512,128]{0,1:T(8,128)(2,1)} %convolution_convert_fusion.3) | copy-start | bytes 393220
  142.0 1.1 copy-start.11
  142.5 2.7 copy-start.4
  142.6 2.7 copy-start.9
  147.9 5.8 %copy-start.3 = (bf16[16,32,1024]{2,1,0:T(8,128)(2,1)S(1)}, bf16[16,32,1024]{2,1,0:T(8,128)(2,1)}, u32[]{:S(2)}) copy-start(bf16[16,32,1024]{2,1,0:T(8,128)(2,1)} %all-gather.6.cloned.1.call-done) | copy-start | bytes 3145732
  151.9 0.8 copy-start.8
  154.9 3.2 copy-start.7
  157.7 35.2 %copy-start.5 = (bf16[2,32,1024]{2,1,0:T(8,128)(2,1)S(1)}, bf16[2,32,1024]{2,1,0:T(8,128)(2,1)}, u32[]{:S(2)}) copy-start(bf16[2,32,1024]{2,1,0:T(8,128)(2,1)} %param.14) | copy-start | bytes 393220
  159.6 63.5 %all-gather.8.cloned.1.call-start = ((), (), s32[]{:S(2)}) async-start(), calls=%async_computation.7 | async-start | bytes 1179648 | tf_op jit(solution)/shard_map/all_gather | solution.py:125
  196.8 65.8 %reduce-scatter.5.cloned.1.call-start = ((), (), s32[]{:S(2)}) async-start(), calls=%async_computation.8 | async-start | bytes 1179648 | tf_op jit(solution)/shard_map/reduce_scatter | solution.py:129
  223.0 5.6 %copy-start.13 = (s32[2,16,4]{1,2,0:T(4,128)S(1)}, s32[2,16,4]{1,2,0:T(4,128)}, u32[]{:S(2)}) copy-start(s32[2,16,4]{1,2,0:T(4,128)} %param.27) | copy-start | bytes 1540
  228.6 33.9 %copy-start.6 = (bf16[64,1024]{1,0:T(8,128)(2,1)S(1)}, bf16[64,1024]{1,0:T(8,128)(2,1)}, u32[]{:S(2)}) copy-start(bf16[64,1024]{1,0:T(8,128)(2,1)} %divide_convert_fusion.3) | copy-start | bytes 393220
  232.2 33.9 %all-to-all-start = ((s32[32,1,8]{2,1,0:T(1,128)}), s32[32,1,8]{2,1,0:T(1,128)S(1)}, u32[]{:S(2)}, u32[]{:S(2)}) async-start(s32[32,1,8]{2,1,0:T(1,128)} %bitcast.36), calls=%async_computation.2 | async-start | bytes 32768 | tf_op jit(solution)/shard_map/all_to_all | solution.py:62
  266.1 23.0 %copy-start.12 = (bf16[64,128]{1,0:T(8,128)(2,1)}, bf16[64,128]{1,0:T(8,128)(2,1)S(1)}, u32[]{:S(2)}) copy-start(bf16[64,128]{1,0:T(8,128)(2,1)S(1)} %divide_convert_fusion.5) | copy-start | bytes 49156
  267.1 26.3 %all-to-all-start.1 = ((bf16[32,2,32,128]{3,2,1,0:T(8,128)(2,1)}), bf16[32,2,32,128]{3,2,1,0:T(8,128)(2,1)S(1)}, u32[]{:S(2)}, u32[]{:S(2)}) async-start(bf16[32,2,32,128]{3,2,1,0:T(8,128)(2,1)} %broadcast_in_dim.21), calls=%async_computation.3 | async-start | bytes 1048576 | tf_op jit(solution)/shard_map/all_to_all | solution.py:141
  277.2 11.8 %copy-start.1 = (s32[256]{0:T(256)S(1)}, s32[256]{0:T(256)}, u32[]{:S(2)}) copy-start(s32[256]{0:T(256)} %param.25) | copy-start | bytes 3076
  303.4 17.3 %all-to-all-start.2 = ((bf16[32,2,128]{2,1,0:T(2,128)(2,1)}), bf16[32,2,128]{2,1,0:T(2,128)(2,1)S(1)}, u32[]{:S(2)}, u32[]{:S(2)}) async-start(bf16[32,2,128]{2,1,0:T(2,128)(2,1)} %reshape.452), calls=%async_computation.4 | async-start | bytes 32768 | tf_op jit(solution)/shard_map/all_to_all | solution.py:21
Sparse Core Ops, SparseCore 0:
  14.0 101.2 all-gather.9
  117.1 21.2 all-gather.5
  159.7 33.1 reduce-scatter.2
  196.9 26.0 all-gather.7
  228.8 33.7 reduce-scatter.4

commit v2 on v1

--- a/solution.py
+++ b/solution.py
@@ -15,6 +15,12 @@
 
 def add_rows(left, piece):
     return jnp.dot(left, piece, preferred_element_type=jnp.float32)
+
+
+def sum_to_owner(terms, n_mp):
+    pieces = terms.astype(jnp.bfloat16).reshape((n_mp, terms.shape[0] // n_mp) + terms.shape[1:])
+    got = lax.all_to_all(pieces, "mp", split_axis=0, concat_axis=0, tiled=True)
+    return jnp.sum(got.astype(jnp.float32), axis=0).astype(jnp.bfloat16).astype(jnp.float32)
 
 
 def return_maxima(maxima):
@@ -57,17 +63,13 @@
     member = (dest[:, None] == jnp.arange(page_owners, dtype=jnp.int32)[None, :]).astype(jnp.int32)
     place = jnp.sum((jnp.cumsum(member, axis=0) - 1) * member, axis=1)
     index = dest * cap + place
-    codes = jnp.full((page_owners * cap,), -1, jnp.int32).at[index].set(query_of * pg_dev + local)
-    codes = codes.reshape(page_owners, cap)
-    got = lax.all_to_all(codes, "dp", split_axis=0, concat_axis=0, tiled=True)
-    where_local = got % pg_dev
-    which_query = jnp.clip(got // pg_dev, 0, qry_dev - 1)
-    chosen = pages[where_local]
-    lens = page_len[where_local]
+    table_local = jnp.zeros((page_owners * cap,), jnp.int32).at[index].set(local)
+    table_query = jnp.zeros((page_owners * cap,), jnp.int32).at[index].set(query_of)
+    table = jnp.concatenate([table_local, table_query]).astype(jnp.bfloat16)
 
     w_out_t = w_out.T
     w_down_t = w_down.T
-    pieces = (query_weight, w_key, w_value, w_out_t, w_up, w_down_t, rel_table, w_proj)
+    pieces = (query_weight, w_key, w_value, w_out_t, w_up, w_down_t, rel_table, w_proj, table)
     flat_pieces = jnp.concatenate([p.reshape(-1) for p in pieces])
     gathered = lax.all_gather(flat_pieces, "dp", axis=0, tiled=False)
     parts = []
@@ -76,7 +78,14 @@
         size = p.size
         parts.append(gathered[:, start : start + size].reshape((page_owners,) + p.shape))
         start += size
-    g_q, g_k, g_v, g_out, g_up, g_down, g_rel, g_proj = parts
+    g_q, g_k, g_v, g_out, g_up, g_down, g_rel, g_proj, g_table = parts
+    me = lax.axis_index("dp")
+    g_table = g_table.reshape(page_owners, 2, page_owners, cap)
+    mine = lax.dynamic_index_in_dim(g_table, me, axis=2, keepdims=False).astype(jnp.int32)
+    where_local = mine[:, 0]
+    which_query = mine[:, 1]
+    chosen = pages[where_local]
+    lens = page_len[where_local]
     wq = g_q.reshape(page_owners * query_weight.shape[0], cols)
     wk = g_k.reshape(page_owners * w_key.shape[0], cols)
     wv = g_v.reshape(page_owners * w_value.shape[0], cols)
@@ -84,10 +93,10 @@
     wu = g_up.reshape(page_owners * w_up.shape[0], w_up.shape[1])
     wd = jnp.transpose(g_down, (2, 0, 1)).reshape(w_down.shape[0], page_owners * w_down.shape[1])
     left_rel = g_rel.reshape(page_owners * rel_table.shape[0], rel_table.shape[1])
-    proj_all = lax.all_gather(g_proj, "mp", axis=0, tiled=False)
-    wp = jnp.transpose(proj_all, (1, 0, 2, 3)).reshape(page_owners * n_mp * w_proj.shape[0], w_proj.shape[1])
 
-    tokens = lax.all_gather(hidden, "mp", axis=0, tiled=True)
+    spread = jnp.broadcast_to(hidden[None], (n_mp,) + hidden.shape)
+    tokens = lax.all_to_all(spread, "mp", split_axis=0, concat_axis=0, tiled=True)
+    tokens = tokens.reshape((n_mp * qry_dev,) + hidden.shape[1:])
     group = tokens.shape[0]
     flat = tokens.reshape(group * qlen, width)
     qsum = add_rows(flat, wq)
@@ -117,18 +126,18 @@
     context_rows = jnp.einsum("qhij,qjhd->qihd", probs, vx, preferred_element_type=jnp.float32)
     context_rows = context_rows.astype(jnp.bfloat16).reshape(group * qlen, cols)
     attn_terms = jnp.dot(context_rows, wo, preferred_element_type=jnp.float32)
-    attn = lax.psum_scatter(
-        attn_terms.astype(jnp.bfloat16), "mp", scatter_dimension=0, tiled=True
-    ).astype(jnp.float32)
+    attn = sum_to_owner(attn_terms, n_mp)
     own = hidden.reshape(qry_dev * qlen, width).astype(jnp.float32)
     mid = layer_norm(own + attn).astype(jnp.bfloat16)
-    mid_all = lax.all_gather(mid, "mp", axis=0, tiled=True)
+    both = jnp.concatenate([mid.reshape(-1), g_proj.reshape(-1)])
+    both_all = lax.all_gather(both, "mp", axis=0, tiled=False)
+    mid_all = both_all[:, : mid.size].reshape((n_mp * mid.shape[0], mid.shape[1]))
+    proj_all = both_all[:, mid.size :].reshape((n_mp,) + g_proj.shape)
+    wp = jnp.transpose(proj_all, (1, 0, 2, 3)).reshape(page_owners * n_mp * w_proj.shape[0], w_proj.shape[1])
     up = add_rows(mid_all, wu)
     inner = jax.nn.gelu(up, approximate=False).astype(jnp.bfloat16)
     down_terms = jnp.dot(inner, wd, preferred_element_type=jnp.float32)
-    mlp = lax.psum_scatter(
-        down_terms.astype(jnp.bfloat16), "mp", scatter_dimension=0, tiled=True
-    ).astype(jnp.float32)
+    mlp = sum_to_owner(down_terms, n_mp)
     state = layer_norm(mid.astype(jnp.float32) + mlp).astype(jnp.bfloat16)
     width_out = w_proj.shape[1]
     proj = add_rows(state, wp)

time: 332 us -> 273 us (0.82)
  waiting for transfers between devices: 190 us -> 135 us
  local copies, waits for them, and re-layouts: 45.7 us -> 56.9 us
  blocking collectives: 10.7 us -> 0 us
  starting transfers between devices: 27.7 us -> 34.5 us
  matrix products: 32.7 us -> 27.4 us
  other arithmetic: 7.6 us -> 3.67 us
    reduce_scatter x2 -> x0, waiting for transfers between devices: 42.3 us -> none  [the longest x1 33.3 us: body(): lax.psum_scatter(attn_terms.astype(jnp.bfloat16), 'mp', scatter_dimension...]
    all_to_all x1 -> x3, waiting for transfers between devices: 0.01 us -> 27.7 us  [the longest x2 27.7 us: sum_to_owner(): got = lax.all_to_all(pieces, 'mp', split_axis=0, concat_axis=0, tiled=True)]
    all_gather x1, waiting for transfers between devices: 101 us -> 77.3 us  [body(): gathered = lax.all_gather(flat_pieces, 'dp', axis=0, tiled=False)]
    all_gather x2 -> x1, waiting for transfers between devices: 34.5 us -> 18.1 us  [body(): both_all = lax.all_gather(both, 'mp', axis=0, tiled=False)]
    all_gather x1 -> x0, blocking collectives: 10.7 us -> none  [body(): proj_all = lax.all_gather(g_proj, 'mp', axis=0, tiled=False)]
    all_gather x0 -> x2, local copies, waits for them, and re-layouts: none -> 7.45 us  [the longest x1 5.58 us: body(): gathered = lax.all_gather(flat_pieces, 'dp', axis=0, tiled=False)]
    all_to_all x1 -> x3, starting transfers between devices: 9.85 us -> 16.3 us  [the longest x2 10.6 us: sum_to_owner(): got = lax.all_to_all(pieces, 'mp', split_axis=0, concat_axis=0, tiled=True)]
    unnamed x46 -> x47, local copies, waits for them, and re-layouts: 13.4 us -> 12.3 us
  transfers between devices with their start and end apart: 8 -> 7, of which waited for: 7 -> 6; matrix products, arithmetic and copies ran while one was open for 11% -> 12% of each run, Pallas kernels for 0% -> 0%
where the time goes in v2:
time: 273 us; the launch traced here: 272 us
  waiting for transfers between devices  135 us (49%)
  local copies, waits for them, and re-layouts  56.9 us (21%)
  starting transfers between devices  34.5 us (13%)
  matrix products  27.4 us (10%)
  between operations  14.6 us (5%)
  other arithmetic  3.67 us (1%)
    all_gather x1, waiting for transfers between devices, body(): gathered = lax.all_gather(flat_pieces, 'dp', axis=0, tiled=False)  77.3 us
    all_to_all x2, waiting for transfers between devices, sum_to_owner(): got = lax.all_to_all(pieces, 'mp', split_axis=0, concat_axis=0, tiled=True)  27.7 us
    all_gather x1, waiting for transfers between devices, body(): both_all = lax.all_gather(both, 'mp', axis=0, tiled=False)  18.1 us
    unnamed x47, local copies, waits for them, and re-layouts  12.3 us
    gather x1, local copies, waits for them, and re-layouts, body(): chosen = pages[where_local]  11.8 us
    all_to_all x2, starting transfers between devices, sum_to_owner(): got = lax.all_to_all(pieces, 'mp', split_axis=0, concat_axis=0, tiled=True)  10.6 us
    all_to_all x1, starting transfers between devices, body(): recv = lax.all_to_all(sent, 'dp', split_axis=0, concat_axis=0, tiled=True)  10.1 us
    all_to_all x1, waiting for transfers between devices, return_maxima(): lax.all_to_all(maxima.astype(jnp.bfloat16), 'dp', split_axis=0, concat_ax...  9.79 us
  transfers between devices with their start and end apart: 7, of which 6 were waited for; matrix products, arithmetic and copies ran while one was open for 12% of the time, Pallas kernels for 0%

profile of v2, /device:TPU:2, one launch (start us, length us, event | category | flops | bytes accessed | tf_op | source)
XLA Modules:
  0.0 271.7 jit_solution(1207508934101758872)
XLA Ops:
  18.8 2.1 broadcast_in_dim.18
  20.9 5.7 %all-to-all-start = ((bf16[8,2,32,1024]{3,2,1,0:T(8,128)(2,1)}), bf16[8,2,32,1024]{3,2,1,0:T(8,128)(2,1)S(1)}, u32[]{:S(2)}, u32[]{:S(2)}) async-start(bf16[8,2,32,1024]{3,2,1,0:T(8,128)(2,1)} %broadcast_in_dim.18), calls=%async_computation | async-start | bytes 2097152 | tf_op jit(solution)/shard_map/all_to_all | solution.py:98
  26.6 77.3 %all-gather.5.cloned.1.call-done = bf16[2129920]{0:T(1024)(128)(2,1)} async-done(((bf16[66560]{0:T(1024)(128)(2,1)}), bf16[2129920]{0:T(1024)(128)(2,1)}) %all-gather.5.cloned.1.call-update) | async-done | bytes 4259856 | tf_op jit(solution)/shard_map/all_gather | solution.py:74
  103.9 5.6 %reshape.511 = bf16[32,66560]{1,0:T(8,128)(2,1)} reshape(bf16[2129920]{0:T(1024)(128)(2,1)} %all-gather.5.cloned.1.call-done) | data formatting | bytes 8519680 | tf_op jit(solution)/shard_map/all_gather | solution.py:74
  109.5 3.4 %fusion.116 = (bf16[32,16384]{1,0:T(8,128)(2,1)}, bf16[32,16384]{1,0:T(8,128)(2,1)S(1)}, bf16[32,16384]{1,0:T(8,128)(2,1)}) fusion(bf16[32,66560]{1,0:T(8,128)(2,1)} %reshape.511), kind=kLoop, calls=%fused_computation.198 | loop fusion | bytes 6291456 | tf_op jit(solution)/shard_map/slice | solution.py:79
  112.8 2.1 slice_bitcast_fusion
  117.5 1.6 reshape_reshape.25
  119.1 2.1 convolution_convert_fusion.3
  133.7 1.4 convolution_convert_fusion
  135.2 4.8 %all-to-all-start.1 = ((bf16[8,64,1024]{2,1,0:T(8,128)(2,1)}), bf16[8,64,1024]{2,1,0:T(8,128)(2,1)S(1)}, u32[]{:S(2)}, u32[]{:S(2)}) async-start(bf16[8,64,1024]{2,1,0:T(8,128)(2,1)} %bitcast.29), calls=%async_computation.1 | async-start | bytes 2097152 | tf_op jit(solution)/shard_map/all_to_all | solution.py:22
  140.9 13.6 %all-to-all-done.1 = bf16[8,64,1024]{2,1,0:T(8,128)(2,1)S(1)} async-done(((bf16[8,64,1024]{2,1,0:T(8,128)(2,1)}), bf16[8,64,1024]{2,1,0:T(8,128)(2,1)S(1)}, u32[]{:S(2)}, u32[]{:S(2)}) %all-to-all-start.1) | async-done | bytes 1048608 | tf_op jit(solution)/shard_map/all_to_all | solution.py:22
  159.0 18.1 %all-gather.7.cloned.1.call-done = bf16[655360]{0:T(1024)(128)(2,1)} async-done(((bf16[81920]{0:T(1024)(128)(2,1)}), bf16[655360]{0:T(1024)(128)(2,1)}) %all-gather.7.cloned.1.call-update) | async-done | bytes 1310736 | tf_op jit(solution)/shard_map/all_gather | solution.py:133
  177.1 1.9 reshape.512
  179.0 1.5 reshape.439
  180.5 6.2 %convolution_convert_fusion.1 = bf16[512,1024]{1,0:T(8,128)(2,1)} fusion(bf16[512,1024]{0,1:T(8,128)(2,1)} %bitcast.166, bf16[512,1024]{1,0:T(8,128)(2,1)} %reshape.439, bf16[1024,512]{1,0:T(8,128)(2,1)} %reshape_reshape.27), kind=kOutput, calls=%fused_computation.19 | convolution fusion | flops 1091305472 | bytes 4194304 | tf_op jit(solution)/shard_map/dot_general | solution.py:139
  186.7 5.8 %all-to-all-start.2 = ((bf16[8,64,1024]{2,1,0:T(8,128)(2,1)}), bf16[8,64,1024]{2,1,0:T(8,128)(2,1)S(1)}, u32[]{:S(2)}, u32[]{:S(2)}) async-start(bf16[8,64,1024]{2,1,0:T(8,128)(2,1)} %bitcast.165), calls=%async_computation.2 | async-start | bytes 2097152 | tf_op jit(solution)/shard_map/all_to_all | solution.py:22
  192.9 14.1 %all-to-all-done.2 = bf16[8,64,1024]{2,1,0:T(8,128)(2,1)S(1)} async-done(((bf16[8,64,1024]{2,1,0:T(8,128)(2,1)}), bf16[8,64,1024]{2,1,0:T(8,128)(2,1)S(1)}, u32[]{:S(2)}, u32[]{:S(2)}) %all-to-all-start.2) | async-done | bytes 1048608 | tf_op jit(solution)/shard_map/all_to_all | solution.py:22
  209.1 10.1 %all-to-all-start.3 = ((bf16[32,2,32,128]{3,2,1,0:T(8,128)(2,1)}), bf16[32,2,32,128]{3,2,1,0:T(8,128)(2,1)S(1)}, u32[]{:S(2)}, u32[]{:S(2)}) async-start(bf16[32,2,32,128]{3,2,1,0:T(8,128)(2,1)} %broadcast_in_dim.21), calls=%async_computation.3 | async-start | bytes 1048576 | tf_op jit(solution)/shard_map/all_to_all | solution.py:150
  219.8 1.9 gather_fusion.1
  221.8 11.8 %gather_fusion.2 = bf16[256,128,128]{2,1,0:T(8,128)(2,1)} fusion(bf16[256,128,128]{2,1,0:T(8,128)(2,1)} %param.24, s32[1024]{0:T(1024)S(1)} %pad_clamp_fusion.1), kind=kCustom, calls=%fused_computation.2 | custom fusion | bytes 16778240 | tf_op jit(solution)/shard_map/gather | solution.py:87
  233.7 1.7 all-to-all-done.3
  236.8 8.0 %select_reduce_fusion = bf16[32,8,32]{2,1,0:T(8,128)(2,1)S(1)} fusion(bf16[32,8,128,128]{3,2,1,0:T(8,128)(2,1)} %bitcast.158, bf16[32,8,32,128]{3,2,1,0:T(8,128)(2,1)S(1)} %bitcast.164, pred[32,8]{1,0:T(8,128)(4,1)S(1)} %copy.89, pred[32,8,128]{2,1,0:T(8,128)(4,1)S(1)} %iota_compare_fusion.1), kind=kOutput, calls=%fused_computation.8 | convolution fusion | flops 271572992 | bytes 10535168 | tf_op jit(solution)/shard_map/snie,snte->snit/dot_general | solution.py:153
  245.5 8.1 %all-to-all-start.4 = ((bf16[32,2,128]{2,1,0:T(2,128)(2,1)}), bf16[32,2,128]{2,1,0:T(2,128)(2,1)S(1)}, u32[]{:S(2)}, u32[]{:S(2)}) async-start(bf16[32,2,128]{2,1,0:T(2,128)(2,1)} %reshape.522), calls=%async_computation.4 | async-start | bytes 32768 | tf_op jit(solution)/shard_map/all_to_all | solution.py:27
  253.6 9.8 %all-to-all-done.4 = bf16[32,2,128]{2,1,0:T(2,128)(2,1)S(1)} async-done(((bf16[32,2,128]{2,1,0:T(2,128)(2,1)}), bf16[32,2,128]{2,1,0:T(2,128)(2,1)S(1)}, u32[]{:S(2)}, u32[]{:S(2)}) %all-to-all-start.4) | async-done | bytes 16416 | tf_op jit(solution)/shard_map/all_to_all | solution.py:27
  (135 shorter events, 38.5 us)
Async XLA Ops:
  7.2 1.0 copy-start
  7.2 96.7 %all-gather.5.cloned.1.call-start = ((), (), s32[]{:S(2)}) async-start(), calls=%async_computation.5 | async-start | bytes 4392960 | tf_op jit(solution)/shard_map/all_gather | solution.py:74
  18.2 0.6 copy-start.8
  20.9 94.3 %all-to-all-start = ((bf16[8,2,32,1024]{3,2,1,0:T(8,128)(2,1)}), bf16[8,2,32,1024]{3,2,1,0:T(8,128)(2,1)S(1)}, u32[]{:S(2)}, u32[]{:S(2)}) async-start(bf16[8,2,32,1024]{3,2,1,0:T(8,128)(2,1)} %broadcast_in_dim.18), calls=%async_computation | async-start | bytes 2097152 | tf_op jit(solution)/shard_map/all_to_all | solution.py:98
  115.2 2.3 copy-start.4
  119.1 3.3 %copy-start.5 = (bf16[4,8,32,128]{3,1,2,0:T(8,128)(2,1)S(1)}, bf16[4,8,32,128]{3,1,2,0:T(8,128)(2,1)}, u32[]{:S(2)}) copy-start(bf16[4,8,32,128]{3,1,2,0:T(8,128)(2,1)} %get-tuple-element.7) | copy-start | bytes 786436
  122.4 4.9 %copy-start.7 = (bf16[512,128]{0,1:T(8,128)(2,1)S(1)}, bf16[512,128]{0,1:T(8,128)(2,1)}, u32[]{:S(2)}) copy-start(bf16[512,128]{0,1:T(8,128)(2,1)} %convolution_convert_fusion.3) | copy-start | bytes 393220
  125.8 1.9 copy-start.9
  127.3 1.9 copy-start.6
  133.6 6.4 %copy-start.2 = (bf16[2,32,1024]{2,1,0:T(8,128)(2,1)S(1)}, bf16[2,32,1024]{2,1,0:T(8,128)(2,1)}, u32[]{:S(2)}) copy-start(bf16[2,32,1024]{2,1,0:T(8,128)(2,1)} %param.14) | copy-start | bytes 393220
  135.2 19.3 %all-to-all-start.1 = ((bf16[8,64,1024]{2,1,0:T(8,128)(2,1)}), bf16[8,64,1024]{2,1,0:T(8,128)(2,1)S(1)}, u32[]{:S(2)}, u32[]{:S(2)}) async-start(bf16[8,64,1024]{2,1,0:T(8,128)(2,1)} %bitcast.29), calls=%async_computation.1 | async-start | bytes 2097152 | tf_op jit(solution)/shard_map/all_to_all | solution.py:22
  140.0 37.1 %all-gather.7.cloned.1.call-start = ((), (), s32[]{:S(2)}) async-start(), calls=%async_computation.6 | async-start | bytes 1474560 | tf_op jit(solution)/shard_map/all_gather | solution.py:133
  154.8 1.5 copy-start.3
  186.7 20.3 %all-to-all-start.2 = ((bf16[8,64,1024]{2,1,0:T(8,128)(2,1)}), bf16[8,64,1024]{2,1,0:T(8,128)(2,1)S(1)}, u32[]{:S(2)}, u32[]{:S(2)}) async-start(bf16[8,64,1024]{2,1,0:T(8,128)(2,1)} %bitcast.165), calls=%async_computation.2 | async-start | bytes 2097152 | tf_op jit(solution)/shard_map/all_to_all | solution.py:22
  192.9 26.8 %copy-start.1 = (s32[256]{0:T(256)S(1)}, s32[256]{0:T(256)}, u32[]{:S(2)}) copy-start(s32[256]{0:T(256)} %param.25) | copy-start | bytes 3076
  208.1 13.6 %copy-start.10 = (bf16[64,128]{1,0:T(8,128)(2,1)}, bf16[64,128]{1,0:T(8,128)(2,1)S(1)}, u32[]{:S(2)}) copy-start(bf16[64,128]{1,0:T(8,128)(2,1)S(1)} %divide_convert_fusion.5) | copy-start | bytes 49156
  209.1 26.4 %all-to-all-start.3 = ((bf16[32,2,32,128]{3,2,1,0:T(8,128)(2,1)}), bf16[32,2,32,128]{3,2,1,0:T(8,128)(2,1)S(1)}, u32[]{:S(2)}, u32[]{:S(2)}) async-start(bf16[32,2,32,128]{3,2,1,0:T(8,128)(2,1)} %broadcast_in_dim.21), calls=%async_computation.3 | async-start | bytes 1048576 | tf_op jit(solution)/shard_map/all_to_all | solution.py:150
  245.5 17.9 %all-to-all-start.4 = ((bf16[32,2,128]{2,1,0:T(2,128)(2,1)}), bf16[32,2,128]{2,1,0:T(2,128)(2,1)S(1)}, u32[]{:S(2)}, u32[]{:S(2)}) async-start(bf16[32,2,128]{2,1,0:T(2,128)(2,1)} %reshape.522), calls=%async_computation.4 | async-start | bytes 32768 | tf_op jit(solution)/shard_map/all_to_all | solution.py:27
Sparse Core Ops, SparseCore 0:
  18.9 84.8 all-gather.4
  156.4 20.6 all-gather.6

commit v3 on v2

--- a/solution.py
+++ b/solution.py
@@ -1,9 +1,11 @@
 import jax
 import jax.numpy as jnp
 from jax import lax
-from jax.sharding import PartitionSpec as P
+from jax.sharding import Mesh, PartitionSpec as P
 
 HD = 64
+DP = ("y", "z")
+MP = ("x", "c")
 
 
 def layer_norm(value):
@@ -19,13 +21,13 @@
 
 def sum_to_owner(terms, n_mp):
     pieces = terms.astype(jnp.bfloat16).reshape((n_mp, terms.shape[0] // n_mp) + terms.shape[1:])
-    got = lax.all_to_all(pieces, "mp", split_axis=0, concat_axis=0, tiled=True)
+    got = lax.all_to_all(pieces, MP, split_axis=0, concat_axis=0, tiled=True)
     return jnp.sum(got.astype(jnp.float32), axis=0).astype(jnp.bfloat16).astype(jnp.float32)
 
 
 def return_maxima(maxima):
     return lax.all_to_all(
-        maxima.astype(jnp.bfloat16), "dp", split_axis=0, concat_axis=0, tiled=True
+        maxima.astype(jnp.bfloat16), DP, split_axis=0, concat_axis=0, tiled=True
     ).astype(maxima.dtype)
 
 
@@ -48,8 +50,8 @@
     qry_dev, qlen, width = hidden.shape
     heads_local = query_weight.shape[1] // HD
     cols = query_weight.shape[1]
-    page_owners = lax.axis_size("dp")
-    n_mp = lax.axis_size("mp")
+    page_owners = lax.axis_size(DP)
+    n_mp = lax.axis_size(MP)
 
     pg_dev = pages.shape[0]
     ptok = pages.shape[1]
@@ -67,19 +69,20 @@
     table_query = jnp.zeros((page_owners * cap,), jnp.int32).at[index].set(query_of)
     table = jnp.concatenate([table_local, table_query]).astype(jnp.bfloat16)
 
-    w_out_t = w_out.T
-    w_down_t = w_down.T
-    pieces = (query_weight, w_key, w_value, w_out_t, w_up, w_down_t, rel_table, w_proj, table)
-    flat_pieces = jnp.concatenate([p.reshape(-1) for p in pieces])
-    gathered = lax.all_gather(flat_pieces, "dp", axis=0, tiled=False)
+    lanes = query_weight.shape[1]
+    pieces = (query_weight, w_key, w_value, w_out.T, w_up, w_down.T, rel_table, w_proj, table)
+    rows = [p.size // lanes for p in pieces]
+    flat_pieces = jnp.concatenate([p.reshape(-1, lanes) for p in pieces], axis=0)
+    by_y = lax.all_gather(flat_pieces, DP[0], axis=0, tiled=False)
+    by_zy = lax.all_gather(by_y, DP[1], axis=0, tiled=False)
+    gathered = jnp.swapaxes(by_zy, 0, 1).reshape((page_owners,) + flat_pieces.shape)
     parts = []
     start = 0
-    for p in pieces:
-        size = p.size
-        parts.append(gathered[:, start : start + size].reshape((page_owners,) + p.shape))
-        start += size
+    for p, n in zip(pieces, rows):
+        parts.append(gathered[:, start : start + n])
+        start += n
     g_q, g_k, g_v, g_out, g_up, g_down, g_rel, g_proj, g_table = parts
-    me = lax.axis_index("dp")
+    me = lax.axis_index(DP)
     g_table = g_table.reshape(page_owners, 2, page_owners, cap)
     mine = lax.dynamic_index_in_dim(g_table, me, axis=2, keepdims=False).astype(jnp.int32)
     where_local = mine[:, 0]
@@ -89,13 +92,14 @@
     wq = g_q.reshape(page_owners * query_weight.shape[0], cols)
     wk = g_k.reshape(page_owners * w_key.shape[0], cols)
     wv = g_v.reshape(page_owners * w_value.shape[0], cols)
-    wo = jnp.transpose(g_out, (2, 0, 1)).reshape(w_out.shape[0], page_owners * w_out.shape[1])
+    wo = g_out.reshape(page_owners * w_out.shape[1], w_out.shape[0]).T
     wu = g_up.reshape(page_owners * w_up.shape[0], w_up.shape[1])
-    wd = jnp.transpose(g_down, (2, 0, 1)).reshape(w_down.shape[0], page_owners * w_down.shape[1])
+    wd = g_down.reshape(page_owners * w_down.shape[1], w_down.shape[0]).T
     left_rel = g_rel.reshape(page_owners * rel_table.shape[0], rel_table.shape[1])
+    g_proj = g_proj.reshape((page_owners,) + w_proj.shape)
 
     spread = jnp.broadcast_to(hidden[None], (n_mp,) + hidden.shape)
-    tokens = lax.all_to_all(spread, "mp", split_axis=0, concat_axis=0, tiled=True)
+    tokens = lax.all_to_all(spread, MP, split_axis=0, concat_axis=0, tiled=True)
     tokens = tokens.reshape((n_mp * qry_dev,) + hidden.shape[1:])
     group = tokens.shape[0]
     flat = tokens.reshape(group * qlen, width)
@@ -129,8 +133,9 @@
     attn = sum_to_owner(attn_terms, n_mp)
     own = hidden.reshape(qry_dev * qlen, width).astype(jnp.float32)
     mid = layer_norm(own + attn).astype(jnp.bfloat16)
+    chosen, lens, mid = lax.optimization_barrier((chosen, lens, mid))
     both = jnp.concatenate([mid.reshape(-1), g_proj.reshape(-1)])
-    both_all = lax.all_gather(both, "mp", axis=0, tiled=False)
+    both_all = lax.all_gather(both, MP, axis=0, tiled=False)
     mid_all = both_all[:, : mid.size].reshape((n_mp * mid.shape[0], mid.shape[1]))
     proj_all = both_all[:, mid.size :].reshape((n_mp,) + g_proj.shape)
     wp = jnp.transpose(proj_all, (1, 0, 2, 3)).reshape(page_owners * n_mp * w_proj.shape[0], w_proj.shape[1])
@@ -147,7 +152,7 @@
     vectors = vectors.reshape(qry_dev, qlen, width_out)
 
     sent = jnp.broadcast_to(vectors[None], (page_owners, qry_dev, qlen, width_out))
-    recv = lax.all_to_all(sent, "dp", split_axis=0, concat_axis=0, tiled=True)
+    recv = lax.all_to_all(sent, DP, split_axis=0, concat_axis=0, tiled=True)
     rows_in = jnp.take_along_axis(recv, which_query[:, :, None, None], axis=1)
     token_positions = jnp.arange(ptok, dtype=jnp.int32)
     sim = jnp.einsum("snie,snte->snit", rows_in, chosen, preferred_element_type=jnp.float32)
@@ -161,20 +166,21 @@
 
 def solution(mesh):
     in_specs = (
-        P(("dp", "mp"), None, None),
-        P("dp", "mp"),
-        P("dp", "mp"),
-        P("dp", "mp"),
-        P("dp", None),
+        P(DP + MP, None, None),
+        P(DP, MP),
+        P(DP, MP),
+        P(DP, MP),
+        P(DP, None),
         P(),
-        P("mp", "dp"),
-        P("dp", "mp"),
-        P("mp", "dp"),
-        P(("dp", "mp"), None),
-        P("dp", None, None),
-        P("dp"),
+        P(MP, DP),
+        P(DP, MP),
+        P(MP, DP),
+        P(DP + MP, None),
+        P(DP, None, None),
+        P(DP),
         P(),
-        P(("dp", "mp"), None, None),
+        P(DP + MP, None, None),
     )
-    out_specs = (P(("dp", "mp"), None, None), P(("dp", "mp"), None))
-    return jax.shard_map(body, mesh=mesh, in_specs=in_specs, out_specs=out_specs, check_vma=False)
+    out_specs = (P(DP + MP, None, None), P(DP + MP, None))
+    fine = Mesh(mesh.devices.reshape(mesh.devices.shape[0] // 8, 8, mesh.devices.shape[1] // 2, 2), DP + MP)
+    return jax.shard_map(body, mesh=fine, in_specs=in_specs, out_specs=out_specs, check_vma=False)

time: 273 us -> 255 us (0.934)
  waiting for transfers between devices: 135 us -> 112 us
  blocking collectives: 0 us -> 14.1 us
  local copies, waits for them, and re-layouts: 56.9 us -> 49.4 us
    all_gather x2, waiting for transfers between devices: 95.4 us -> 72.4 us  [the longest x1 51.9 us: body(): by_zy = lax.all_gather(by_y, DP[1], axis=0, tiled=False)]
    all_gather x0 -> x1, blocking collectives: none -> 14.1 us  [body(): by_y = lax.all_gather(flat_pieces, DP[0], axis=0, tiled=False)]
    unnamed x47 -> x34, local copies, waits for them, and re-layouts: 12.3 us -> 3.92 us
    reshape x0 -> x6, local copies, waits for them, and re-layouts: none -> 6.77 us  [the longest x3 2.36 us: body(): p.reshape(-1, lanes)]
    all_gather x2 -> x1, local copies, waits for them, and re-layouts: 7.45 us -> 1.87 us  [body(): both_all = lax.all_gather(both, MP, axis=0, tiled=False)]
    another operation x5 -> x0, local copies, waits for them, and re-layouts: 4.21 us -> none  [the longest x1 1.55 us: body(): g_rel.reshape(page_owners * rel_table.shape[0], rel_table.shape[1])]
    concatenate x1, local copies, waits for them, and re-layouts: 0.19 us -> 3.56 us  [body(): jnp.concatenate([p.reshape(-1, lanes) for p in pieces], axis=0)]
  transfers between devices with their start and end apart: 7 -> 7, of which waited for: 6 -> 5; matrix products, arithmetic and copies ran while one was open for 12% -> 10% of each run, Pallas kernels for 0% -> 0%
where the time goes in v3:
time: 255 us; the launch traced here: 254 us
  waiting for transfers between devices  112 us (44%)
  local copies, waits for them, and re-layouts  49.4 us (19%)
  starting transfers between devices  31.8 us (12%)
  matrix products  27.7 us (11%)
  between operations  14.6 us (6%)
  blocking collectives  14.1 us (6%)
  other arithmetic  4.3 us (2%)
    all_gather x1, waiting for transfers between devices, body(): by_zy = lax.all_gather(by_y, DP[1], axis=0, tiled=False)  51.9 us
    all_gather x1, waiting for transfers between devices, body(): both_all = lax.all_gather(both, MP, axis=0, tiled=False)  20.5 us
    all_to_all x1, waiting for transfers between devices, body(): recv = lax.all_to_all(sent, DP, split_axis=0, concat_axis=0, tiled=True)  15.9 us
    all_to_all x2, waiting for transfers between devices, sum_to_owner(): got = lax.all_to_all(pieces, MP, split_axis=0, concat_axis=0, tiled=True)  14.2 us
    all_gather x1, blocking collectives, body(): by_y = lax.all_gather(flat_pieces, DP[0], axis=0, tiled=False)  14.1 us
    gather x1, local copies, waits for them, and re-layouts, body(): chosen = pages[where_local]  12 us
    all_to_all x2, starting transfers between devices, sum_to_owner(): got = lax.all_to_all(pieces, MP, split_axis=0, concat_axis=0, tiled=True)  10.6 us
    all_to_all x1, starting transfers between devices, body(): recv = lax.all_to_all(sent, DP, split_axis=0, concat_axis=0, tiled=True)  10.1 us
  transfers between devices with their start and end apart: 7, of which 5 were waited for; matrix products, arithmetic and copies ran while one was open for 10% of the time, Pallas kernels for 0%

profile of v3, /device:TPU:2, one launch (start us, length us, event | category | flops | bytes accessed | tf_op | source)
XLA Modules:
  0.0 254.2 jit_solution(555020727891699922)
XLA Ops:
  14.1 3.6 %concatenate.16 = bf16[520,128]{1,0:T(8,128)(2,1)S(1)} concatenate(bf16[32,128]{1,0:T(8,128)(2,1)} %param.15, bf16[32,128]{1,0:T(8,128)(2,1)} %param.16, bf16[32,128]{1,0:T(8,128)(2,1)} %param.17, bf16[32,128]{1,0:T(8,128)(2,1)} %bitcast.159, bf16[128,128]{1,0:T(8,128)(2,1)S(1)} %reshape.362, bf16[128,128]{1,0:T(8,128)(2,1)S(1)} %reshape.363, bf16[128,128]{1,0:T(8,128)(2,1)S(1)} %reshape.364, ...), dimensions={0} | concatenate | bytes 266240 | tf_op jit(solution)/shard_map/concatenate | solution.py:75
  17.7 14.1 %all-gather = bf16[2080,128]{1,0:T(8,128)(2,1)} all-gather(bf16[520,128]{1,0:T(8,128)(2,1)S(1)} %concatenate.16), channel_id=2, replica_groups=mesh['y'=4,'z'=8,'x'=4,'c'=2] {'y'}, dimensions={0}, use_global_device_ids=true | all-gather | bytes 665600 | tf_op jit(solution)/shard_map/all_gather | solution.py:76
  32.9 5.4 %all-to-all-start = ((bf16[8,2,32,1024]{3,2,1,0:T(8,128)(2,1)}), bf16[8,2,32,1024]{3,2,1,0:T(8,128)(2,1)S(1)}, u32[]{:S(2)}, u32[]{:S(2)}) async-start(bf16[8,2,32,1024]{3,2,1,0:T(8,128)(2,1)} %broadcast_in_dim.18), calls=%async_computation | async-start | bytes 2097152 | tf_op jit(solution)/shard_map/all_to_all | solution.py:102
  38.4 51.9 %all-gather.6.cloned.1.call-done = bf16[32,520,128]{2,1,0:T(8,128)(2,1)} async-done(((bf16[4,520,128]{2,1,0:T(8,128)(2,1)}), bf16[32,520,128]{2,1,0:T(8,128)(2,1)}) %all-gather.6.cloned.1.call-update) | async-done | bytes 4259856 | tf_op jit(solution)/shard_map/all_gather | solution.py:77
  90.2 2.6 %copy.77 = bf16[4,8,520,128]{3,2,1,0:T(8,128)(2,1)S(1)} copy(bf16[4,8,520,128]{3,2,0,1:T(8,128)(2,1)} %bitcast.136) | data formatting | bytes 8519680 | tf_op jit(solution)/shard_map/transpose | solution.py:78
  95.0 1.8 fusion.119
  99.1 1.5 reshape.374
  100.7 2.1 convolution_convert_fusion.3
  112.6 1.5 fusion.14
  116.0 4.8 %all-to-all-start.1 = ((bf16[8,64,1024]{2,1,0:T(8,128)(2,1)}), bf16[8,64,1024]{2,1,0:T(8,128)(2,1)S(1)}, u32[]{:S(2)}, u32[]{:S(2)}) async-start(bf16[8,64,1024]{2,1,0:T(8,128)(2,1)} %bitcast.37), calls=%async_computation.1 | async-start | bytes 2097152 | tf_op jit(solution)/shard_map/all_to_all | solution.py:24
  122.1 1.9 gather_fusion.2
  124.2 12.0 %gather_fusion.1 = bf16[256,128,128]{2,1,0:T(8,128)(2,1)} fusion(bf16[256,128,128]{2,1,0:T(8,128)(2,1)} %param.24, s32[1024]{0:T(1024)S(1)} %pad_clamp_fusion.1), kind=kCustom, calls=%fused_computation.1 | custom fusion | bytes 16778240 | tf_op jit(solution)/shard_map/gather | solution.py:90
  140.2 1.4 reshape.384
  141.7 20.5 %all-gather.8.cloned.1.call-done = bf16[655360]{0:T(1024)(128)(2,1)} async-done(((bf16[81920]{0:T(1024)(128)(2,1)}), bf16[655360]{0:T(1024)(128)(2,1)}) %all-gather.8.cloned.1.call-update) | async-done | bytes 1310736 | tf_op jit(solution)/shard_map/all_gather | solution.py:138
  162.2 1.9 reshape.453
  164.1 1.5 reshape.382
  165.6 6.2 %convolution_convert_fusion.1 = bf16[512,1024]{1,0:T(8,128)(2,1)} fusion(bf16[1024,512]{1,0:T(8,128)(2,1)} %reshape.384, bf16[512,1024]{1,0:T(8,128)(2,1)} %reshape.382, bf16[1024,512]{1,0:T(8,128)(2,1)} %reshape.383), kind=kOutput, calls=%fused_computation.19 | convolution fusion | flops 1091305472 | bytes 4194304 | tf_op jit(solution)/shard_map/dot_general | solution.py:144
  171.8 5.8 %all-to-all-start.2 = ((bf16[8,64,1024]{2,1,0:T(8,128)(2,1)}), bf16[8,64,1024]{2,1,0:T(8,128)(2,1)S(1)}, u32[]{:S(2)}, u32[]{:S(2)}) async-start(bf16[8,64,1024]{2,1,0:T(8,128)(2,1)} %bitcast.145), calls=%async_computation.2 | async-start | bytes 2097152 | tf_op jit(solution)/shard_map/all_to_all | solution.py:24
  177.9 14.2 %all-to-all-done.2 = bf16[8,64,1024]{2,1,0:T(8,128)(2,1)S(1)} async-done(((bf16[8,64,1024]{2,1,0:T(8,128)(2,1)}), bf16[8,64,1024]{2,1,0:T(8,128)(2,1)S(1)}, u32[]{:S(2)}, u32[]{:S(2)}) %all-to-all-start.2) | async-done | bytes 1048608 | tf_op jit(solution)/shard_map/all_to_all | solution.py:24
  194.0 10.1 %all-to-all-start.3 = ((bf16[32,2,32,128]{3,2,1,0:T(8,128)(2,1)}), bf16[32,2,32,128]{3,2,1,0:T(8,128)(2,1)S(1)}, u32[]{:S(2)}, u32[]{:S(2)}) async-start(bf16[32,2,32,128]{3,2,1,0:T(8,128)(2,1)} %broadcast_in_dim.21), calls=%async_computation.3 | async-start | bytes 1048576 | tf_op jit(solution)/shard_map/all_to_all | solution.py:155
  204.5 15.9 %all-to-all-done.3 = bf16[32,2,32,128]{3,2,1,0:T(8,128)(2,1)S(1)} async-done(((bf16[32,2,32,128]{3,2,1,0:T(8,128)(2,1)}), bf16[32,2,32,128]{3,2,1,0:T(8,128)(2,1)S(1)}, u32[]{:S(2)}, u32[]{:S(2)}) %all-to-all-start.3) | async-done | bytes 524320 | tf_op jit(solution)/shard_map/all_to_all | solution.py:155
  221.7 8.0 %select_reduce_fusion = bf16[32,8,32]{2,1,0:T(8,128)(2,1)S(1)} fusion(bf16[32,8,128,128]{3,2,1,0:T(8,128)(2,1)} %bitcast.135, bf16[32,8,32,128]{3,2,1,0:T(8,128)(2,1)S(1)} %bitcast.143, pred[32,8]{1,0:T(8,128)(4,1)S(1)} %copy.93, pred[32,8,128]{2,1,0:T(8,128)(4,1)S(1)} %iota_compare_fusion.1), kind=kOutput, calls=%fused_computation.8 | convolution fusion | flops 271572992 | bytes 10535168 | tf_op jit(solution)/shard_map/snie,snte->snit/dot_general | solution.py:158
  230.4 5.7 %all-to-all-start.4 = ((bf16[32,2,128]{2,1,0:T(2,128)(2,1)}), bf16[32,2,128]{2,1,0:T(2,128)(2,1)S(1)}, u32[]{:S(2)}, u32[]{:S(2)}) async-start(bf16[32,2,128]{2,1,0:T(2,128)(2,1)} %reshape.463), calls=%async_computation.4 | async-start | bytes 32768 | tf_op jit(solution)/shard_map/all_to_all | solution.py:29
  236.1 9.8 %all-to-all-done.4 = bf16[32,2,128]{2,1,0:T(2,128)(2,1)S(1)} async-done(((bf16[32,2,128]{2,1,0:T(2,128)(2,1)}), bf16[32,2,128]{2,1,0:T(2,128)(2,1)S(1)}, u32[]{:S(2)}, u32[]{:S(2)}) %all-to-all-start.4) | async-done | bytes 16416 | tf_op jit(solution)/shard_map/all_to_all | solution.py:29
  (120 shorter events, 35.5 us)
Async XLA Ops:
  7.2 1.0 copy-start
  7.2 24.6 %copy-start.5 = (bf16[2,32,1024]{2,1,0:T(8,128)(2,1)S(1)}, bf16[2,32,1024]{2,1,0:T(8,128)(2,1)}, u32[]{:S(2)}) copy-start(bf16[2,32,1024]{2,1,0:T(8,128)(2,1)} %param.14) | copy-start | bytes 393220
  7.2 83.0 %all-gather.6.cloned.1.call-start = ((), (), s32[]{:S(2)}) async-start(), calls=%async_computation.5 | async-start | bytes 4792320 | tf_op jit(solution)/shard_map/all_gather | solution.py:77
  32.9 63.9 %all-to-all-start = ((bf16[8,2,32,1024]{3,2,1,0:T(8,128)(2,1)}), bf16[8,2,32,1024]{3,2,1,0:T(8,128)(2,1)S(1)}, u32[]{:S(2)}, u32[]{:S(2)}) async-start(bf16[8,2,32,1024]{3,2,1,0:T(8,128)(2,1)} %broadcast_in_dim.18), calls=%async_computation | async-start | bytes 2097152 | tf_op jit(solution)/shard_map/all_to_all | solution.py:102
  92.8 2.2 copy-start.2
  95.0 2.9 %copy-start.4 = (bf16[32,32,128]{2,1,0:T(8,128)(2,1)}, bf16[32,32,128]{2,1,0:T(8,128)(2,1)S(1)}, u32[]{:S(2)}) copy-start(bf16[32,32,128]{2,1,0:T(8,128)(2,1)S(1)} %get-tuple-element.15) | copy-start | bytes 786436
  100.6 3.3 %copy-start.9 = (bf16[32,32,128]{2,1,0:T(8,128)(2,1)S(1)}, bf16[32,32,128]{2,1,0:T(8,128)(2,1)}, u32[]{:S(2)}) copy-start(bf16[32,32,128]{2,1,0:T(8,128)(2,1)} %get-tuple-element.16) | copy-start | bytes 786436
  103.9 3.1 %copy-start.12 = (bf16[512,128]{0,1:T(8,128)(2,1)S(1)}, bf16[512,128]{0,1:T(8,128)(2,1)}, u32[]{:S(2)}) copy-start(bf16[512,128]{0,1:T(8,128)(2,1)} %convolution_convert_fusion.3) | copy-start | bytes 393220
  105.4 2.1 copy-start.13
  107.1 1.9 copy-start.11
  111.6 0.8 copy-start.10
  112.4 2.1 copy-start.8
  114.4 7.7 %copy-start.1 = (s32[256]{0:T(256)S(1)}, s32[256]{0:T(256)}, u32[]{:S(2)}) copy-start(s32[256]{0:T(256)} %param.25) | copy-start | bytes 3076
  116.0 20.1 %all-to-all-start.1 = ((bf16[8,64,1024]{2,1,0:T(8,128)(2,1)}), bf16[8,64,1024]{2,1,0:T(8,128)(2,1)S(1)}, u32[]{:S(2)}, u32[]{:S(2)}) async-start(bf16[8,64,1024]{2,1,0:T(8,128)(2,1)} %bitcast.37), calls=%async_computation.1 | async-start | bytes 2097152 | tf_op jit(solution)/shard_map/all_to_all | solution.py:24
  120.8 41.4 %all-gather.8.cloned.1.call-start = ((), (), s32[]{:S(2)}) async-start(), calls=%async_computation.6 | async-start | bytes 1474560 | tf_op jit(solution)/shard_map/all_gather | solution.py:138
  124.1 12.2 %copy-start.6 = (bf16[2,32,1024]{2,1,0:T(8,128)(2,1)S(1)}, bf16[2,32,1024]{2,1,0:T(8,128)(2,1)}, u32[]{:S(2)}) copy-start(bf16[2,32,1024]{2,1,0:T(8,128)(2,1)} %param.14) | copy-start | bytes 393220
  136.1 2.7 %copy-start.3 = (bf16[32,128,128]{2,1,0:T(8,128)(2,1)S(1)}, bf16[32,128,128]{2,1,0:T(8,128)(2,1)}, u32[]{:S(2)}) copy-start(bf16[32,128,128]{2,1,0:T(8,128)(2,1)} %get-tuple-element.10) | copy-start | bytes 3145732
  136.3 0.7 copy-start.7
  171.8 20.3 %all-to-all-start.2 = ((bf16[8,64,1024]{2,1,0:T(8,128)(2,1)}), bf16[8,64,1024]{2,1,0:T(8,128)(2,1)S(1)}, u32[]{:S(2)}, u32[]{:S(2)}) async-start(bf16[8,64,1024]{2,1,0:T(8,128)(2,1)} %bitcast.145), calls=%async_computation.2 | async-start | bytes 2097152 | tf_op jit(solution)/shard_map/all_to_all | solution.py:24
  193.1 28.6 %copy-start.14 = (bf16[64,128]{1,0:T(8,128)(2,1)}, bf16[64,128]{1,0:T(8,128)(2,1)S(1)}, u32[]{:S(2)}) copy-start(bf16[64,128]{1,0:T(8,128)(2,1)S(1)} %divide_convert_fusion.4) | copy-start | bytes 49156
  194.0 26.4 %all-to-all-start.3 = ((bf16[32,2,32,128]{3,2,1,0:T(8,128)(2,1)}), bf16[32,2,32,128]{3,2,1,0:T(8,128)(2,1)S(1)}, u32[]{:S(2)}, u32[]{:S(2)}) async-start(bf16[32,2,32,128]{3,2,1,0:T(8,128)(2,1)} %broadcast_in_dim.21), calls=%async_computation.3 | async-start | bytes 1048576 | tf_op jit(solution)/shard_map/all_to_all | solution.py:155
  230.4 15.5 %all-to-all-start.4 = ((bf16[32,2,128]{2,1,0:T(2,128)(2,1)}), bf16[32,2,128]{2,1,0:T(2,128)(2,1)S(1)}, u32[]{:S(2)}, u32[]{:S(2)}) async-start(bf16[32,2,128]{2,1,0:T(2,128)(2,1)} %reshape.463), calls=%async_computation.4 | async-start | bytes 32768 | tf_op jit(solution)/shard_map/all_to_all | solution.py:29
Sparse Core Ops, SparseCore 0:
  31.9 58.2 all-gather.5
  138.9 23.2 all-gather.7

commit v4 on v3

--- a/solution.py
+++ b/solution.py
@@ -23,6 +23,20 @@
     pieces = terms.astype(jnp.bfloat16).reshape((n_mp, terms.shape[0] // n_mp) + terms.shape[1:])
     got = lax.all_to_all(pieces, MP, split_axis=0, concat_axis=0, tiled=True)
     return jnp.sum(got.astype(jnp.float32), axis=0).astype(jnp.bfloat16).astype(jnp.float32)
+
+
+def gather_rows(pieces, lanes, page_owners):
+    rows = [p.size // lanes for p in pieces]
+    flat_pieces = jnp.concatenate([p.reshape(-1, lanes) for p in pieces], axis=0)
+    by_y = lax.all_gather(flat_pieces, DP[0], axis=0, tiled=False)
+    by_zy = lax.all_gather(by_y, DP[1], axis=0, tiled=False)
+    gathered = jnp.swapaxes(by_zy, 0, 1).reshape((page_owners,) + flat_pieces.shape)
+    parts = []
+    start = 0
+    for n in rows:
+        parts.append(gathered[:, start : start + n])
+        start += n
+    return parts
 
 
 def return_maxima(maxima):
@@ -70,18 +84,10 @@
     table = jnp.concatenate([table_local, table_query]).astype(jnp.bfloat16)
 
     lanes = query_weight.shape[1]
-    pieces = (query_weight, w_key, w_value, w_out.T, w_up, w_down.T, rel_table, w_proj, table)
-    rows = [p.size // lanes for p in pieces]
-    flat_pieces = jnp.concatenate([p.reshape(-1, lanes) for p in pieces], axis=0)
-    by_y = lax.all_gather(flat_pieces, DP[0], axis=0, tiled=False)
-    by_zy = lax.all_gather(by_y, DP[1], axis=0, tiled=False)
-    gathered = jnp.swapaxes(by_zy, 0, 1).reshape((page_owners,) + flat_pieces.shape)
-    parts = []
-    start = 0
-    for p, n in zip(pieces, rows):
-        parts.append(gathered[:, start : start + n])
-        start += n
-    g_q, g_k, g_v, g_out, g_up, g_down, g_rel, g_proj, g_table = parts
+    first = (query_weight, w_key, w_value, w_out.T, rel_table, w_proj, table)
+    second = (w_up, w_down.T)
+    g_q, g_k, g_v, g_out, g_rel, g_proj, g_table = gather_rows(first, lanes, page_owners)
+    g_up, g_down = gather_rows(second, lanes, page_owners)
     me = lax.axis_index(DP)
     g_table = g_table.reshape(page_owners, 2, page_owners, cap)
     mine = lax.dynamic_index_in_dim(g_table, me, axis=2, keepdims=False).astype(jnp.int32)

time: 255 us -> 232 us (0.910)
  waiting for transfers between devices: 112 us -> 87.9 us
  blocking collectives: 14.1 us -> 26.5 us
  matrix products: 27.7 us -> 22.9 us
  local copies, waits for them, and re-layouts: 49.4 us -> 44.8 us
    all_gather x1 -> x2, waiting for transfers between devices: 51.9 us -> 27.8 us  [gather_rows(): by_zy = lax.all_gather(by_y, DP[1], axis=0, tiled=False)]
    all_gather x1 -> x2, blocking collectives: 14.1 us -> 26.5 us  [gather_rows(): by_y = lax.all_gather(flat_pieces, DP[0], axis=0, tiled=False)]
    dot_general x6, matrix products: 6.38 us -> 2.76 us  [add_rows(): return jnp.dot(left, piece, preferred_element_type=jnp.float32)]
  transfers between devices with their start and end apart: 7 -> 8, of which waited for: 5 -> 6; matrix products, arithmetic and copies ran while one was open for 10% -> 16% of each run, Pallas kernels for 0% -> 0%
where the time goes in v4:
time: 232 us; the launch traced here: 231 us
  waiting for transfers between devices  87.9 us (38%)
  local copies, waits for them, and re-layouts  44.8 us (19%)
  starting transfers between devices  31.5 us (14%)
  blocking collectives  26.5 us (11%)
  matrix products  22.9 us (10%)
  between operations  14.3 us (6%)
  other arithmetic  3.41 us (1%)
    all_gather x2, waiting for transfers between devices, gather_rows(): by_zy = lax.all_gather(by_y, DP[1], axis=0, tiled=False)  27.8 us
    all_gather x2, blocking collectives, gather_rows(): by_y = lax.all_gather(flat_pieces, DP[0], axis=0, tiled=False)  26.5 us
    all_gather x1, waiting for transfers between devices, body(): both_all = lax.all_gather(both, MP, axis=0, tiled=False)  20.2 us
    all_to_all x1, waiting for transfers between devices, body(): recv = lax.all_to_all(sent, DP, split_axis=0, concat_axis=0, tiled=True)  15.9 us
    all_to_all x2, waiting for transfers between devices, sum_to_owner(): got = lax.all_to_all(pieces, MP, split_axis=0, concat_axis=0, tiled=True)  14.2 us
    gather x1, local copies, waits for them, and re-layouts, body(): chosen = pages[where_local]  11.9 us
    all_to_all x2, starting transfers between devices, sum_to_owner(): got = lax.all_to_all(pieces, MP, split_axis=0, concat_axis=0, tiled=True)  10.6 us
    all_to_all x1, starting transfers between devices, body(): recv = lax.all_to_all(sent, DP, split_axis=0, concat_axis=0, tiled=True)  10.1 us
  transfers between devices with their start and end apart: 8, of which 6 were waited for; matrix products, arithmetic and copies ran while one was open for 16% of the time, Pallas kernels for 0%

profile of v4, /device:TPU:2, one launch (start us, length us, event | category | flops | bytes accessed | tf_op | source)
XLA Modules:
  0.0 231.4 jit_solution(8359369429507678212)
XLA Ops:
  12.6 3.5 %concatenate.19 = bf16[264,128]{1,0:T(8,128)(2,1)S(1)} concatenate(bf16[32,128]{1,0:T(8,128)(2,1)} %param.15, bf16[32,128]{1,0:T(8,128)(2,1)} %param.16, bf16[32,128]{1,0:T(8,128)(2,1)} %param.17, bf16[32,128]{1,0:T(8,128)(2,1)} %bitcast.167, bf16[128,128]{1,0:T(8,128)(2,1)S(1)} %reshape.365, bf16[4,128]{1,0:T(4,128)(2,1)} %param.23, bf16[2,128]{1,0:T(2,128)(2,1)S(1)} %get-tuple-element.25, ...), dimensions={0} | concatenate | bytes 135168 | tf_op jit(solution)/shard_map/concatenate | solution.py:30
  16.1 13.5 %all-gather = bf16[1056,128]{1,0:T(8,128)(2,1)} all-gather(bf16[264,128]{1,0:T(8,128)(2,1)S(1)} %concatenate.19), channel_id=2, replica_groups=mesh['y'=4,'z'=8,'x'=4,'c'=2] {'y'}, dimensions={0}, use_global_device_ids=true | all-gather | bytes 337920 | tf_op jit(solution)/shard_map/all_gather | solution.py:31
  29.7 2.0 broadcast_in_dim.18
  31.7 5.2 %all-to-all-start = ((bf16[8,2,32,1024]{3,2,1,0:T(8,128)(2,1)}), bf16[8,2,32,1024]{3,2,1,0:T(8,128)(2,1)S(1)}, u32[]{:S(2)}, u32[]{:S(2)}) async-start(bf16[8,2,32,1024]{3,2,1,0:T(8,128)(2,1)} %broadcast_in_dim.18), calls=%async_computation | async-start | bytes 2097152 | tf_op jit(solution)/shard_map/all_to_all | solution.py:108
  37.0 13.0 %all-gather.3 = bf16[1024,128]{1,0:T(8,128)(2,1)} all-gather(bf16[256,128]{1,0:T(8,128)(2,1)S(1)} %pad_maximum_fusion.1), channel_id=5, replica_groups=mesh['y'=4,'z'=8,'x'=4,'c'=2] {'y'}, dimensions={0}, use_global_device_ids=true | all-gather | bytes 327680 | tf_op jit(solution)/shard_map/all_gather | solution.py:31
  50.0 23.3 %all-gather.9.cloned.1.call-done = bf16[32,264,128]{2,1,0:T(8,128)(2,1)} async-done(((bf16[4,264,128]{2,1,0:T(8,128)(2,1)}), bf16[32,264,128]{2,1,0:T(8,128)(2,1)}) %all-gather.9.cloned.1.call-update) | async-done | bytes 2162704 | tf_op jit(solution)/shard_map/all_gather | solution.py:32
  73.3 1.8 copy.79
  88.6 4.8 %all-to-all-start.1 = ((bf16[8,64,1024]{2,1,0:T(8,128)(2,1)}), bf16[8,64,1024]{2,1,0:T(8,128)(2,1)S(1)}, u32[]{:S(2)}, u32[]{:S(2)}) async-start(bf16[8,64,1024]{2,1,0:T(8,128)(2,1)} %bitcast.36), calls=%async_computation.1 | async-start | bytes 2097152 | tf_op jit(solution)/shard_map/all_to_all | solution.py:24
  94.7 1.9 gather_fusion.2
  96.8 11.9 %gather_fusion.1 = bf16[256,128,128]{2,1,0:T(8,128)(2,1)} fusion(bf16[256,128,128]{2,1,0:T(8,128)(2,1)} %param.24, s32[1024]{0:T(1024)S(1)} %pad_clamp_fusion.1), kind=kCustom, calls=%fused_computation.1 | custom fusion | bytes 16778240 | tf_op jit(solution)/shard_map/gather | solution.py:96
  110.2 4.4 %all-gather.13.cloned.1.call-done = bf16[32,256,128]{2,1,0:T(8,128)(2,1)} async-done(((bf16[4,256,128]{2,1,0:T(8,128)(2,1)}), bf16[32,256,128]{2,1,0:T(8,128)(2,1)}) %all-gather.13.cloned.1.call-update) | async-done | bytes 2097168 | tf_op jit(solution)/shard_map/all_gather | solution.py:32
  114.7 1.7 copy.94
  118.0 1.5 reshape.388
  119.5 20.2 %all-gather.11.cloned.1.call-done = bf16[655360]{0:T(1024)(128)(2,1)} async-done(((bf16[81920]{0:T(1024)(128)(2,1)}), bf16[655360]{0:T(1024)(128)(2,1)}) %all-gather.11.cloned.1.call-update) | async-done | bytes 1310736 | tf_op jit(solution)/shard_map/all_gather | solution.py:144
  139.7 1.9 reshape.457
  141.6 1.5 reshape.383
  143.1 6.2 %convolution_convert_fusion.1 = bf16[512,1024]{1,0:T(8,128)(2,1)} fusion(bf16[1024,512]{1,0:T(8,128)(2,1)} %reshape.388, bf16[512,1024]{1,0:T(8,128)(2,1)} %reshape.383, bf16[1024,512]{1,0:T(8,128)(2,1)} %reshape.387), kind=kOutput, calls=%fused_computation.19 | convolution fusion | flops 1091305472 | bytes 4194304 | tf_op jit(solution)/shard_map/dot_general | solution.py:150
  149.3 5.8 %all-to-all-start.2 = ((bf16[8,64,1024]{2,1,0:T(8,128)(2,1)}), bf16[8,64,1024]{2,1,0:T(8,128)(2,1)S(1)}, u32[]{:S(2)}, u32[]{:S(2)}) async-start(bf16[8,64,1024]{2,1,0:T(8,128)(2,1)} %bitcast.153), calls=%async_computation.2 | async-start | bytes 2097152 | tf_op jit(solution)/shard_map/all_to_all | solution.py:24
  155.4 14.2 %all-to-all-done.2 = bf16[8,64,1024]{2,1,0:T(8,128)(2,1)S(1)} async-done(((bf16[8,64,1024]{2,1,0:T(8,128)(2,1)}), bf16[8,64,1024]{2,1,0:T(8,128)(2,1)S(1)}, u32[]{:S(2)}, u32[]{:S(2)}) %all-to-all-start.2) | async-done | bytes 1048608 | tf_op jit(solution)/shard_map/all_to_all | solution.py:24
  171.5 10.1 %all-to-all-start.3 = ((bf16[32,2,32,128]{3,2,1,0:T(8,128)(2,1)}), bf16[32,2,32,128]{3,2,1,0:T(8,128)(2,1)S(1)}, u32[]{:S(2)}, u32[]{:S(2)}) async-start(bf16[32,2,32,128]{3,2,1,0:T(8,128)(2,1)} %broadcast_in_dim.21), calls=%async_computation.3 | async-start | bytes 1048576 | tf_op jit(solution)/shard_map/all_to_all | solution.py:161
  182.0 15.9 %all-to-all-done.3 = bf16[32,2,32,128]{3,2,1,0:T(8,128)(2,1)S(1)} async-done(((bf16[32,2,32,128]{3,2,1,0:T(8,128)(2,1)}), bf16[32,2,32,128]{3,2,1,0:T(8,128)(2,1)S(1)}, u32[]{:S(2)}, u32[]{:S(2)}) %all-to-all-start.3) | async-done | bytes 524320 | tf_op jit(solution)/shard_map/all_to_all | solution.py:161
  199.3 8.0 %select_reduce_fusion = bf16[32,8,32]{2,1,0:T(8,128)(2,1)S(1)} fusion(bf16[32,8,128,128]{3,2,1,0:T(8,128)(2,1)} %bitcast.140, bf16[32,8,32,128]{3,2,1,0:T(8,128)(2,1)S(1)} %bitcast.149, pred[32,8]{1,0:T(8,128)(4,1)S(1)} %copy.96, pred[32,8,128]{2,1,0:T(8,128)(4,1)S(1)} %iota_compare_fusion.1), kind=kOutput, calls=%fused_computation.8 | convolution fusion | flops 271572992 | bytes 10535168 | tf_op jit(solution)/shard_map/snie,snte->snit/dot_general | solution.py:164
  208.0 5.7 %all-to-all-start.4 = ((bf16[32,2,128]{2,1,0:T(2,128)(2,1)}), bf16[32,2,128]{2,1,0:T(2,128)(2,1)S(1)}, u32[]{:S(2)}, u32[]{:S(2)}) async-start(bf16[32,2,128]{2,1,0:T(2,128)(2,1)} %reshape.469), calls=%async_computation.4 | async-start | bytes 32768 | tf_op jit(solution)/shard_map/all_to_all | solution.py:43
  213.7 9.8 %all-to-all-done.4 = bf16[32,2,128]{2,1,0:T(2,128)(2,1)S(1)} async-done(((bf16[32,2,128]{2,1,0:T(2,128)(2,1)}), bf16[32,2,128]{2,1,0:T(2,128)(2,1)S(1)}, u32[]{:S(2)}, u32[]{:S(2)}) %all-to-all-start.4) | async-done | bytes 16416 | tf_op jit(solution)/shard_map/all_to_all | solution.py:43
  (113 shorter events, 29.2 us)
Async XLA Ops:
  7.2 1.0 copy-start
  7.2 66.2 %all-gather.9.cloned.1.call-start = ((), (), s32[]{:S(2)}) async-start(), calls=%async_computation.5 | async-start | bytes 2433024 | tf_op jit(solution)/shard_map/all_gather | solution.py:32
  10.2 26.7 %copy-start.6 = (bf16[32,512]{1,0:T(8,128)(2,1)S(1)}, bf16[32,512]{1,0:T(8,128)(2,1)}, u32[]{:S(2)}) copy-start(bf16[32,512]{1,0:T(8,128)(2,1)} %param.21) | copy-start | bytes 98308
  10.4 26.5 %copy-start.7 = (bf16[512,32]{0,1:T(8,128)(2,1)S(1)}, bf16[512,32]{0,1:T(8,128)(2,1)}, u32[]{:S(2)}) copy-start(bf16[512,32]{0,1:T(8,128)(2,1)} %param.22) | copy-start | bytes 98308
  31.7 47.7 %all-to-all-start = ((bf16[8,2,32,1024]{3,2,1,0:T(8,128)(2,1)}), bf16[8,2,32,1024]{3,2,1,0:T(8,128)(2,1)S(1)}, u32[]{:S(2)}, u32[]{:S(2)}) async-start(bf16[8,2,32,1024]{3,2,1,0:T(8,128)(2,1)} %broadcast_in_dim.18), calls=%async_computation | async-start | bytes 2097152 | tf_op jit(solution)/shard_map/all_to_all | solution.py:108
  36.9 77.8 %all-gather.13.cloned.1.call-start = ((), (), s32[]{:S(2)}) async-start(), calls=%async_computation.7 | async-start | bytes 2359296 | tf_op jit(solution)/shard_map/all_gather | solution.py:32
  75.2 1.4 copy-start.2
  81.0 1.2 copy-start.4
  87.0 7.7 %copy-start.1 = (s32[256]{0:T(256)S(1)}, s32[256]{0:T(256)}, u32[]{:S(2)}) copy-start(s32[256]{0:T(256)} %param.25) | copy-start | bytes 3076
  88.6 20.1 %all-to-all-start.1 = ((bf16[8,64,1024]{2,1,0:T(8,128)(2,1)}), bf16[8,64,1024]{2,1,0:T(8,128)(2,1)S(1)}, u32[]{:S(2)}, u32[]{:S(2)}) async-start(bf16[8,64,1024]{2,1,0:T(8,128)(2,1)} %bitcast.36), calls=%async_computation.1 | async-start | bytes 2097152 | tf_op jit(solution)/shard_map/all_to_all | solution.py:24
  93.4 46.3 %all-gather.11.cloned.1.call-start = ((), (), s32[]{:S(2)}) async-start(), calls=%async_computation.6 | async-start | bytes 1474560 | tf_op jit(solution)/shard_map/all_gather | solution.py:144
  96.8 12.1 %copy-start.3 = (bf16[2,32,1024]{2,1,0:T(8,128)(2,1)S(1)}, bf16[2,32,1024]{2,1,0:T(8,128)(2,1)}, u32[]{:S(2)}) copy-start(bf16[2,32,1024]{2,1,0:T(8,128)(2,1)} %param.14) | copy-start | bytes 393220
  149.3 20.3 %all-to-all-start.2 = ((bf16[8,64,1024]{2,1,0:T(8,128)(2,1)}), bf16[8,64,1024]{2,1,0:T(8,128)(2,1)S(1)}, u32[]{:S(2)}, u32[]{:S(2)}) async-start(bf16[8,64,1024]{2,1,0:T(8,128)(2,1)} %bitcast.153), calls=%async_computation.2 | async-start | bytes 2097152 | tf_op jit(solution)/shard_map/all_to_all | solution.py:24
  170.6 28.7 %copy-start.5 = (bf16[64,128]{1,0:T(8,128)(2,1)}, bf16[64,128]{1,0:T(8,128)(2,1)S(1)}, u32[]{:S(2)}) copy-start(bf16[64,128]{1,0:T(8,128)(2,1)S(1)} %divide_convert_fusion.4) | copy-start | bytes 49156
  171.5 26.4 %all-to-all-start.3 = ((bf16[32,2,32,128]{3,2,1,0:T(8,128)(2,1)}), bf16[32,2,32,128]{3,2,1,0:T(8,128)(2,1)S(1)}, u32[]{:S(2)}, u32[]{:S(2)}) async-start(bf16[32,2,32,128]{3,2,1,0:T(8,128)(2,1)} %broadcast_in_dim.21), calls=%async_computation.3 | async-start | bytes 1048576 | tf_op jit(solution)/shard_map/all_to_all | solution.py:161
  208.0 15.5 %all-to-all-start.4 = ((bf16[32,2,128]{2,1,0:T(2,128)(2,1)}), bf16[32,2,128]{2,1,0:T(2,128)(2,1)S(1)}, u32[]{:S(2)}, u32[]{:S(2)}) async-start(bf16[32,2,128]{2,1,0:T(2,128)(2,1)} %reshape.469), calls=%async_computation.4 | async-start | bytes 32768 | tf_op jit(solution)/shard_map/all_to_all | solution.py:43
Sparse Core Ops, SparseCore 0:
  29.8 43.5 all-gather.8
  75.1 39.5 all-gather.12
  116.5 23.1 all-gather.10

commit v5 on v4

--- a/solution.py
+++ b/solution.py
@@ -25,15 +25,18 @@
     return jnp.sum(got.astype(jnp.float32), axis=0).astype(jnp.bfloat16).astype(jnp.float32)
 
 
-def gather_rows(pieces, lanes, page_owners):
-    rows = [p.size // lanes for p in pieces]
+def gather_over_y(pieces, lanes):
     flat_pieces = jnp.concatenate([p.reshape(-1, lanes) for p in pieces], axis=0)
-    by_y = lax.all_gather(flat_pieces, DP[0], axis=0, tiled=False)
+    return lax.all_gather(flat_pieces, DP[0], axis=0, tiled=False)
+
+
+def gather_over_z(pieces, lanes, by_y, page_owners):
     by_zy = lax.all_gather(by_y, DP[1], axis=0, tiled=False)
-    gathered = jnp.swapaxes(by_zy, 0, 1).reshape((page_owners,) + flat_pieces.shape)
+    gathered = jnp.swapaxes(by_zy, 0, 1).reshape((page_owners,) + by_y.shape[1:])
     parts = []
     start = 0
-    for n in rows:
+    for p in pieces:
+        n = p.size // lanes
         parts.append(gathered[:, start : start + n])
         start += n
     return parts
@@ -86,8 +89,12 @@
     lanes = query_weight.shape[1]
     first = (query_weight, w_key, w_value, w_out.T, rel_table, w_proj, table)
     second = (w_up, w_down.T)
-    g_q, g_k, g_v, g_out, g_rel, g_proj, g_table = gather_rows(first, lanes, page_owners)
-    g_up, g_down = gather_rows(second, lanes, page_owners)
+    first_y = gather_over_y(first, lanes)
+    first_parts = gather_over_z(first, lanes, first_y, page_owners)
+    second_y = gather_over_y(second, lanes)
+    first_parts, second_y = lax.optimization_barrier((first_parts, second_y))
+    g_q, g_k, g_v, g_out, g_rel, g_proj, g_table = first_parts
+    g_up, g_down = gather_over_z(second, lanes, second_y, page_owners)
     me = lax.axis_index(DP)
     g_table = g_table.reshape(page_owners, 2, page_owners, cap)
     mine = lax.dynamic_index_in_dim(g_table, me, axis=2, keepdims=False).astype(jnp.int32)
@@ -139,12 +146,14 @@
     attn = sum_to_owner(attn_terms, n_mp)
     own = hidden.reshape(qry_dev * qlen, width).astype(jnp.float32)
     mid = layer_norm(own + attn).astype(jnp.bfloat16)
-    chosen, lens, mid = lax.optimization_barrier((chosen, lens, mid))
-    both = jnp.concatenate([mid.reshape(-1), g_proj.reshape(-1)])
-    both_all = lax.all_gather(both, MP, axis=0, tiled=False)
-    mid_all = both_all[:, : mid.size].reshape((n_mp * mid.shape[0], mid.shape[1]))
-    proj_all = both_all[:, mid.size :].reshape((n_mp,) + g_proj.shape)
+    both = jnp.concatenate([mid, g_proj.reshape(-1, mid.shape[1])], axis=0)
+    both_all = lax.all_to_all(
+        jnp.broadcast_to(both[None], (n_mp,) + both.shape), MP, split_axis=0, concat_axis=0, tiled=True
+    )
+    mid_all = both_all[:, : mid.shape[0]].reshape((n_mp * mid.shape[0], mid.shape[1]))
+    proj_all = both_all[:, mid.shape[0] :].reshape((n_mp,) + g_proj.shape)
     wp = jnp.transpose(proj_all, (1, 0, 2, 3)).reshape(page_owners * n_mp * w_proj.shape[0], w_proj.shape[1])
+    chosen, lens, mid_all = lax.optimization_barrier((chosen, lens, mid_all))
     up = add_rows(mid_all, wu)
     inner = jax.nn.gelu(up, approximate=False).astype(jnp.bfloat16)
     down_terms = jnp.dot(inner, wd, preferred_element_type=jnp.float32)

time: 232 us -> 225 us (0.970)
  waiting for transfers between devices: 87.9 us -> 80.6 us
    all_gather x3 -> x2, waiting for transfers between devices: 47.9 us -> 23.4 us  [gather_over_z(): by_zy = lax.all_gather(by_y, DP[1], axis=0, tiled=False)]
    all_to_all x2, waiting for transfers between devices: 14.2 us -> 28.6 us  [sum_to_owner(): got = lax.all_to_all(pieces, MP, split_axis=0, concat_axis=0, tiled=True)]
    all_to_all x0 -> x1, starting transfers between devices: none -> 4.94 us  [body(): lax.all_to_all(jnp.broadcast_to(both[None], (n_mp,) + both.shape), MP, sp...]
    all_to_all x0 -> x1, waiting for transfers between devices: none -> 2.91 us  [body(): lax.all_to_all(jnp.broadcast_to(both[None], (n_mp,) + both.shape), MP, sp...]
    all_to_all x1, starting transfers between devices: 10.1 us -> 7.34 us  [body(): recv = lax.all_to_all(sent, DP, split_axis=0, concat_axis=0, tiled=True)]
  transfers between devices with their start and end apart: 8 -> 8, of which waited for: 6 -> 6; matrix products, arithmetic and copies ran while one was open for 16% -> 15% of each run, Pallas kernels for 0% -> 0%
where the time goes in v5:
time: 225 us; the launch traced here: 224 us
  waiting for transfers between devices  80.6 us (36%)
  local copies, waits for them, and re-layouts  42.7 us (19%)
  starting transfers between devices  33.1 us (15%)
  blocking collectives  26.5 us (12%)
  matrix products  23.5 us (10%)
  between operations  14.6 us (6%)
  other arithmetic  3 us (1%)
    all_to_all x2, waiting for transfers between devices, sum_to_owner(): got = lax.all_to_all(pieces, MP, split_axis=0, concat_axis=0, tiled=True)  28.6 us
    all_gather x2, blocking collectives, gather_over_y(): return lax.all_gather(flat_pieces, DP[0], axis=0, tiled=False)  26.5 us
    all_gather x2, waiting for transfers between devices, gather_over_z(): by_zy = lax.all_gather(by_y, DP[1], axis=0, tiled=False)  23.4 us
    all_to_all x1, waiting for transfers between devices, body(): recv = lax.all_to_all(sent, DP, split_axis=0, concat_axis=0, tiled=True)  15.9 us
    gather x1, local copies, waits for them, and re-layouts, body(): chosen = pages[where_local]  12 us
    all_to_all x2, starting transfers between devices, sum_to_owner(): got = lax.all_to_all(pieces, MP, split_axis=0, concat_axis=0, tiled=True)  9.96 us
    all_to_all x1, waiting for transfers between devices, return_maxima(): lax.all_to_all(maxima.astype(jnp.bfloat16), DP, split_axis=0, concat_axis...  9.79 us
    dot_general x1, matrix products, body(): jnp.einsum('snie,snte->snit', rows_in, chosen, preferred_element_type=jnp...  8.01 us
  transfers between devices with their start and end apart: 8, of which 6 were waited for; matrix products, arithmetic and copies ran while one was open for 15% of the time, Pallas kernels for 0%

profile of v5, /device:TPU:2, one launch (start us, length us, event | category | flops | bytes accessed | tf_op | source)
XLA Modules:
  0.0 224.1 jit_solution(10921766931980851669)
XLA Ops:
  12.6 3.5 %concatenate.19 = bf16[264,128]{1,0:T(8,128)(2,1)S(1)} concatenate(bf16[32,128]{1,0:T(8,128)(2,1)} %param.15, bf16[32,128]{1,0:T(8,128)(2,1)} %param.16, bf16[32,128]{1,0:T(8,128)(2,1)} %param.17, bf16[32,128]{1,0:T(8,128)(2,1)} %bitcast.173, bf16[128,128]{1,0:T(8,128)(2,1)S(1)} %reshape.423, bf16[4,128]{1,0:T(4,128)(2,1)} %param.23, bf16[2,128]{1,0:T(2,128)(2,1)S(1)} %get-tuple-element.39, ...), dimensions={0} | concatenate | bytes 135168 | tf_op jit(solution)/shard_map/concatenate | solution.py:29
  16.1 13.5 %all-gather = bf16[1056,128]{1,0:T(8,128)(2,1)} all-gather(bf16[264,128]{1,0:T(8,128)(2,1)S(1)} %concatenate.19), channel_id=2, replica_groups=mesh['y'=4,'z'=8,'x'=4,'c'=2] {'y'}, dimensions={0}, use_global_device_ids=true | all-gather | bytes 337920 | tf_op jit(solution)/shard_map/all_gather | solution.py:30
  29.7 2.0 broadcast_in_dim.20
  31.7 5.2 %all-to-all-start = ((bf16[8,2,32,1024]{3,2,1,0:T(8,128)(2,1)}), bf16[8,2,32,1024]{3,2,1,0:T(8,128)(2,1)S(1)}, u32[]{:S(2)}, u32[]{:S(2)}) async-start(bf16[8,2,32,1024]{3,2,1,0:T(8,128)(2,1)} %broadcast_in_dim.20), calls=%async_computation | async-start | bytes 2097152 | tf_op jit(solution)/shard_map/all_to_all | solution.py:115
  37.0 13.0 %all-gather.2 = bf16[1024,128]{1,0:T(8,128)(2,1)} all-gather(bf16[256,128]{1,0:T(8,128)(2,1)S(1)} %pad_maximum_fusion.1), channel_id=4, replica_groups=mesh['y'=4,'z'=8,'x'=4,'c'=2] {'y'}, dimensions={0}, use_global_device_ids=true | all-gather | bytes 327680 | tf_op jit(solution)/shard_map/all_gather | solution.py:30
  50.0 23.4 %all-gather.7.cloned.1.call-done = bf16[32,264,128]{2,1,0:T(8,128)(2,1)} async-done(((bf16[4,264,128]{2,1,0:T(8,128)(2,1)}), bf16[32,264,128]{2,1,0:T(8,128)(2,1)}) %all-gather.7.cloned.1.call-update) | async-done | bytes 2162704 | tf_op jit(solution)/shard_map/all_gather | solution.py:34
  73.3 1.8 copy.79
  77.2 1.5 convolution_convert_fusion.4
  88.0 4.9 %all-to-all-start.1 = ((bf16[8,64,1024]{2,1,0:T(8,128)(2,1)}), bf16[8,64,1024]{2,1,0:T(8,128)(2,1)S(1)}, u32[]{:S(2)}, u32[]{:S(2)}) async-start(bf16[8,64,1024]{2,1,0:T(8,128)(2,1)} %bitcast.33), calls=%async_computation.1 | async-start | bytes 2097152 | tf_op jit(solution)/shard_map/all_to_all | solution.py:24
  92.9 14.5 %all-to-all-done.1 = bf16[8,64,1024]{2,1,0:T(8,128)(2,1)S(1)} async-done(((bf16[8,64,1024]{2,1,0:T(8,128)(2,1)}), bf16[8,64,1024]{2,1,0:T(8,128)(2,1)S(1)}, u32[]{:S(2)}, u32[]{:S(2)}) %all-to-all-start.1) | async-done | bytes 1048608 | tf_op jit(solution)/shard_map/all_to_all | solution.py:24
  109.5 4.9 %all-to-all-start.2 = ((bf16[8,80,1024]{2,1,0:T(8,128)(2,1)}), bf16[8,80,1024]{2,1,0:T(8,128)(2,1)S(1)}, u32[]{:S(2)}, u32[]{:S(2)}) async-start(bf16[8,80,1024]{2,1,0:T(8,128)(2,1)} %broadcast_in_dim.21), calls=%async_computation.2 | async-start | bytes 2621440 | tf_op jit(solution)/shard_map/all_to_all | solution.py:150
  114.8 1.9 gather_fusion.2
  116.8 12.0 %gather_fusion.1 = bf16[256,128,128]{2,1,0:T(8,128)(2,1)} fusion(bf16[256,128,128]{2,1,0:T(8,128)(2,1)} %param.24, s32[1024]{0:T(1024)S(1)} %pad_clamp_fusion.1), kind=kCustom, calls=%fused_computation.1 | custom fusion | bytes 16778240 | tf_op jit(solution)/shard_map/gather | solution.py:103
  128.8 2.9 %all-to-all-done.2 = bf16[8,80,1024]{2,1,0:T(8,128)(2,1)S(1)} async-done(((bf16[8,80,1024]{2,1,0:T(8,128)(2,1)}), bf16[8,80,1024]{2,1,0:T(8,128)(2,1)S(1)}, u32[]{:S(2)}, u32[]{:S(2)}) %all-to-all-start.2) | async-done | bytes 1310752 | tf_op jit(solution)/shard_map/all_to_all | solution.py:150
  131.7 2.2 copy.94
  135.1 2.6 %reshape.444 = bf16[1024,512]{1,0:T(8,128)(2,1)} reshape(bf16[32,128,128]{2,1,0:T(8,128)(2,1)} %get-tuple-element.30) | data formatting | bytes 2097152 | tf_op jit(solution)/shard_map/reshape | solution.py:109
  139.1 5.9 %convolution_convert_fusion.1 = bf16[512,1024]{1,0:T(8,128)(2,1)} fusion(bf16[1024,512]{1,0:T(8,128)(2,1)} %reshape.445, bf16[512,1024]{1,0:T(8,128)(2,1)S(1)} %bitcast.147, bf16[1024,512]{1,0:T(8,128)(2,1)} %reshape.444), kind=kOutput, calls=%fused_computation.19 | convolution fusion | flops 1091305472 | bytes 4194304 | tf_op jit(solution)/shard_map/dot_general | solution.py:159
  145.0 5.1 %all-to-all-start.3 = ((bf16[8,64,1024]{2,1,0:T(8,128)(2,1)}), bf16[8,64,1024]{2,1,0:T(8,128)(2,1)S(1)}, u32[]{:S(2)}, u32[]{:S(2)}) async-start(bf16[8,64,1024]{2,1,0:T(8,128)(2,1)} %bitcast.44), calls=%async_computation.3 | async-start | bytes 2097152 | tf_op jit(solution)/shard_map/all_to_all | solution.py:24
  150.5 14.1 %all-to-all-done.3 = bf16[8,64,1024]{2,1,0:T(8,128)(2,1)S(1)} async-done(((bf16[8,64,1024]{2,1,0:T(8,128)(2,1)}), bf16[8,64,1024]{2,1,0:T(8,128)(2,1)S(1)}, u32[]{:S(2)}, u32[]{:S(2)}) %all-to-all-start.3) | async-done | bytes 1048608 | tf_op jit(solution)/shard_map/all_to_all | solution.py:24
  166.6 7.3 %all-to-all-start.4 = ((bf16[32,2,32,128]{3,2,1,0:T(8,128)(2,1)}), bf16[32,2,32,128]{3,2,1,0:T(8,128)(2,1)S(1)}, u32[]{:S(2)}, u32[]{:S(2)}) async-start(bf16[32,2,32,128]{3,2,1,0:T(8,128)(2,1)} %broadcast_in_dim.24), calls=%async_computation.4 | async-start | bytes 1048576 | tf_op jit(solution)/shard_map/all_to_all | solution.py:170
  174.4 15.9 %all-to-all-done.4 = bf16[32,2,32,128]{3,2,1,0:T(8,128)(2,1)S(1)} async-done(((bf16[32,2,32,128]{3,2,1,0:T(8,128)(2,1)}), bf16[32,2,32,128]{3,2,1,0:T(8,128)(2,1)S(1)}, u32[]{:S(2)}, u32[]{:S(2)}) %all-to-all-start.4) | async-done | bytes 524320 | tf_op jit(solution)/shard_map/all_to_all | solution.py:170
  191.6 8.0 %select_reduce_fusion = bf16[32,8,32]{2,1,0:T(8,128)(2,1)S(1)} fusion(bf16[32,8,128,128]{3,2,1,0:T(8,128)(2,1)} %bitcast.145, bf16[32,8,32,128]{3,2,1,0:T(8,128)(2,1)S(1)} %bitcast.156, pred[32,8]{1,0:T(8,128)(4,1)S(1)} %copy.96, pred[32,8,128]{2,1,0:T(8,128)(4,1)S(1)} %iota_compare_fusion.1), kind=kOutput, calls=%fused_computation.8 | convolution fusion | flops 271572992 | bytes 10535168 | tf_op jit(solution)/shard_map/snie,snte->snit/dot_general | solution.py:173
  200.3 5.7 %all-to-all-start.5 = ((bf16[32,2,128]{2,1,0:T(2,128)(2,1)}), bf16[32,2,128]{2,1,0:T(2,128)(2,1)S(1)}, u32[]{:S(2)}, u32[]{:S(2)}) async-start(bf16[32,2,128]{2,1,0:T(2,128)(2,1)} %reshape.526), calls=%async_computation.5 | async-start | bytes 32768 | tf_op jit(solution)/shard_map/all_to_all | solution.py:46
  206.0 9.8 %all-to-all-done.5 = bf16[32,2,128]{2,1,0:T(2,128)(2,1)S(1)} async-done(((bf16[32,2,128]{2,1,0:T(2,128)(2,1)}), bf16[32,2,128]{2,1,0:T(2,128)(2,1)S(1)}, u32[]{:S(2)}, u32[]{:S(2)}) %all-to-all-start.5) | async-done | bytes 16416 | tf_op jit(solution)/shard_map/all_to_all | solution.py:46
  (122 shorter events, 27.7 us)
Async XLA Ops:
  7.2 1.0 copy-start
  7.2 66.2 %all-gather.7.cloned.1.call-start = ((), (), s32[]{:S(2)}) async-start(), calls=%async_computation.6 | async-start | bytes 2433024 | tf_op jit(solution)/shard_map/all_gather | solution.py:34
  10.2 26.7 %copy-start.9 = (bf16[32,512]{1,0:T(8,128)(2,1)S(1)}, bf16[32,512]{1,0:T(8,128)(2,1)}, u32[]{:S(2)}) copy-start(bf16[32,512]{1,0:T(8,128)(2,1)} %param.21) | copy-start | bytes 98308
  10.4 26.5 %copy-start.10 = (bf16[512,32]{0,1:T(8,128)(2,1)S(1)}, bf16[512,32]{0,1:T(8,128)(2,1)}, u32[]{:S(2)}) copy-start(bf16[512,32]{0,1:T(8,128)(2,1)} %param.22) | copy-start | bytes 98308
  31.7 47.0 %all-to-all-start = ((bf16[8,2,32,1024]{3,2,1,0:T(8,128)(2,1)}), bf16[8,2,32,1024]{3,2,1,0:T(8,128)(2,1)S(1)}, u32[]{:S(2)}, u32[]{:S(2)}) async-start(bf16[8,2,32,1024]{3,2,1,0:T(8,128)(2,1)} %broadcast_in_dim.20), calls=%async_computation | async-start | bytes 2097152 | tf_op jit(solution)/shard_map/all_to_all | solution.py:115
  36.9 94.9 %all-gather.9.cloned.1.call-start = ((), (), s32[]{:S(2)}) async-start(), calls=%async_computation.7 | async-start | bytes 2359296 | tf_op jit(solution)/shard_map/all_gather | solution.py:34
  76.7 2.0 copy-start.4
  77.2 2.5 %copy-start.6 = (bf16[32,32,128]{2,1,0:T(8,128)(2,1)S(1)}, bf16[32,32,128]{2,1,0:T(8,128)(2,1)}, u32[]{:S(2)}) copy-start(bf16[32,32,128]{2,1,0:T(8,128)(2,1)} %get-tuple-element.13) | copy-start | bytes 786436
  80.2 1.0 copy-start.7
  85.5 1.0 copy-start.5
  88.0 19.6 %copy-start.3 = (bf16[2,32,1024]{2,1,0:T(8,128)(2,1)S(1)}, bf16[2,32,1024]{2,1,0:T(8,128)(2,1)}, u32[]{:S(2)}) copy-start(bf16[2,32,1024]{2,1,0:T(8,128)(2,1)} %param.14) | copy-start | bytes 393220
  88.0 19.4 %all-to-all-start.1 = ((bf16[8,64,1024]{2,1,0:T(8,128)(2,1)}), bf16[8,64,1024]{2,1,0:T(8,128)(2,1)S(1)}, u32[]{:S(2)}, u32[]{:S(2)}) async-start(bf16[8,64,1024]{2,1,0:T(8,128)(2,1)} %bitcast.33), calls=%async_computation.1 | async-start | bytes 2097152 | tf_op jit(solution)/shard_map/all_to_all | solution.py:24
  108.2 6.6 %copy-start.1 = (s32[256]{0:T(256)S(1)}, s32[256]{0:T(256)}, u32[]{:S(2)}) copy-start(s32[256]{0:T(256)} %param.25) | copy-start | bytes 3076
  109.5 22.3 %all-to-all-start.2 = ((bf16[8,80,1024]{2,1,0:T(8,128)(2,1)}), bf16[8,80,1024]{2,1,0:T(8,128)(2,1)S(1)}, u32[]{:S(2)}, u32[]{:S(2)}) async-start(bf16[8,80,1024]{2,1,0:T(8,128)(2,1)} %broadcast_in_dim.21), calls=%async_computation.2 | async-start | bytes 2621440 | tf_op jit(solution)/shard_map/all_to_all | solution.py:150
  131.7 2.2 copy-start.2
  135.1 4.1 %slice-start = ((bf16[8,80,1024]{2,1,0:T(8,128)(2,1)}), bf16[8,64,1024]{2,1,0:T(8,128)(2,1)S(1)}, s32[]{:S(2)}) async-start(bf16[8,80,1024]{2,1,0:T(8,128)(2,1)} %copy-done.2), calls=%async_computation.8 | async-start | bytes 2097152 | tf_op jit(solution)/shard_map/slice | solution.py:153
  145.0 5.2 %slice-start.1 = ((bf16[8,80,1024]{2,1,0:T(8,128)(2,1)}), bf16[8,16,1024]{2,1,0:T(8,128)(2,1)S(1)}, s32[]{:S(2)}) async-start(bf16[8,80,1024]{2,1,0:T(8,128)(2,1)} %copy-done.2), calls=%async_computation.9 | async-start | bytes 524288 | tf_op jit(solution)/shard_map/slice | solution.py:154
  145.0 19.6 %all-to-all-start.3 = ((bf16[8,64,1024]{2,1,0:T(8,128)(2,1)}), bf16[8,64,1024]{2,1,0:T(8,128)(2,1)S(1)}, u32[]{:S(2)}, u32[]{:S(2)}) async-start(bf16[8,64,1024]{2,1,0:T(8,128)(2,1)} %bitcast.44), calls=%async_computation.3 | async-start | bytes 2097152 | tf_op jit(solution)/shard_map/all_to_all | solution.py:24
  165.6 26.0 %copy-start.8 = (bf16[64,128]{1,0:T(8,128)(2,1)}, bf16[64,128]{1,0:T(8,128)(2,1)S(1)}, u32[]{:S(2)}) copy-start(bf16[64,128]{1,0:T(8,128)(2,1)S(1)} %divide_convert_fusion.4) | copy-start | bytes 49156
  166.6 23.7 %all-to-all-start.4 = ((bf16[32,2,32,128]{3,2,1,0:T(8,128)(2,1)}), bf16[32,2,32,128]{3,2,1,0:T(8,128)(2,1)S(1)}, u32[]{:S(2)}, u32[]{:S(2)}) async-start(bf16[32,2,32,128]{3,2,1,0:T(8,128)(2,1)} %broadcast_in_dim.24), calls=%async_computation.4 | async-start | bytes 1048576 | tf_op jit(solution)/shard_map/all_to_all | solution.py:170
  200.3 15.5 %all-to-all-start.5 = ((bf16[32,2,128]{2,1,0:T(2,128)(2,1)}), bf16[32,2,128]{2,1,0:T(2,128)(2,1)S(1)}, u32[]{:S(2)}, u32[]{:S(2)}) async-start(bf16[32,2,128]{2,1,0:T(2,128)(2,1)} %reshape.526), calls=%async_computation.5 | async-start | bytes 32768 | tf_op jit(solution)/shard_map/all_to_all | solution.py:46
Sparse Core Ops, SparseCore 0:
  29.8 43.5 all-gather.6
  79.9 39.4 all-gather.8

commit v6 on v5

--- a/solution.py
+++ b/solution.py
@@ -31,8 +31,8 @@
 
 
 def gather_over_z(pieces, lanes, by_y, page_owners):
-    by_zy = lax.all_gather(by_y, DP[1], axis=0, tiled=False)
-    gathered = jnp.swapaxes(by_zy, 0, 1).reshape((page_owners,) + by_y.shape[1:])
+    by_yz = lax.all_gather(by_y, DP[1], axis=1, tiled=False)
+    gathered = by_yz.reshape((page_owners,) + by_y.shape[1:])
     parts = []
     start = 0
     for p in pieces:
@@ -70,11 +70,17 @@
     page_owners = lax.axis_size(DP)
     n_mp = lax.axis_size(MP)
 
+    lanes = query_weight.shape[1]
+    first = (query_weight, w_key, w_value, w_out.T, rel_table, w_proj)
+    second = (w_up, w_down.T)
+    first_y = gather_over_y(first, lanes)
+    first_parts = gather_over_z(first, lanes, first_y, page_owners)
     pg_dev = pages.shape[0]
     ptok = pages.shape[1]
     ncand, ppc = (candidates.shape[1], candidates.shape[2])
     req = qry_dev * ncand * ppc
     cap = 2 * req // page_owners
+    first_y, candidates = lax.optimization_barrier((first_y, candidates))
     slots = slot_per_page[candidates.reshape(req)]
     dest = slots // pg_dev
     local = slots % pg_dev
@@ -82,24 +88,15 @@
     member = (dest[:, None] == jnp.arange(page_owners, dtype=jnp.int32)[None, :]).astype(jnp.int32)
     place = jnp.sum((jnp.cumsum(member, axis=0) - 1) * member, axis=1)
     index = dest * cap + place
-    table_local = jnp.zeros((page_owners * cap,), jnp.int32).at[index].set(local)
-    table_query = jnp.zeros((page_owners * cap,), jnp.int32).at[index].set(query_of)
-    table = jnp.concatenate([table_local, table_query]).astype(jnp.bfloat16)
+    codes = jnp.zeros((page_owners * cap,), jnp.int32).at[index].set(query_of * pg_dev + local)
+    got = lax.all_to_all(codes.reshape(page_owners, cap), DP, split_axis=0, concat_axis=0, tiled=True)
+    second_y = gather_over_y(second, lanes)
+    first_parts, second_y, got = lax.optimization_barrier((first_parts, second_y, got))
+    where_local = got % pg_dev
+    which_query = got // pg_dev
 
-    lanes = query_weight.shape[1]
-    first = (query_weight, w_key, w_value, w_out.T, rel_table, w_proj, table)
-    second = (w_up, w_down.T)
-    first_y = gather_over_y(first, lanes)
-    first_parts = gather_over_z(first, lanes, first_y, page_owners)
-    second_y = gather_over_y(second, lanes)
-    first_parts, second_y = lax.optimization_barrier((first_parts, second_y))
-    g_q, g_k, g_v, g_out, g_rel, g_proj, g_table = first_parts
+    g_q, g_k, g_v, g_out, g_rel, g_proj = first_parts
     g_up, g_down = gather_over_z(second, lanes, second_y, page_owners)
-    me = lax.axis_index(DP)
-    g_table = g_table.reshape(page_owners, 2, page_owners, cap)
-    mine = lax.dynamic_index_in_dim(g_table, me, axis=2, keepdims=False).astype(jnp.int32)
-    where_local = mine[:, 0]
-    which_query = mine[:, 1]
     chosen = pages[where_local]
     lens = page_len[where_local]
     wq = g_q.reshape(page_owners * query_weight.shape[0], cols)

time: 225 us -> 225 us (level)
  waiting for transfers between devices: 80.6 us -> 67.5 us
  starting transfers between devices: 33.1 us -> 43 us
  local copies, waits for them, and re-layouts: 42.7 us -> 47.9 us
    all_gather x2, waiting for transfers between devices: 23.4 us -> 0.01 us  [gather_over_z(): by_yz = lax.all_gather(by_y, DP[1], axis=1, tiled=False)]
    all_to_all x0 -> x1, starting transfers between devices: none -> 10.8 us  [body(): lax.all_to_all(codes.reshape(page_owners, cap), DP, split_axis=0, concat_...]
    all_to_all x0 -> x1, waiting for transfers between devices: none -> 9.87 us  [body(): lax.all_to_all(codes.reshape(page_owners, cap), DP, split_axis=0, concat_...]
    all_gather x0 -> x2, local copies, waits for them, and re-layouts: none -> 4.03 us  [the longest x1 3.2 us: gather_over_z(): by_yz = lax.all_gather(by_y, DP[1], axis=1, tiled=False)]
    transpose x2 -> x0, local copies, waits for them, and re-layouts: 4.01 us -> none  [gather_over_z(): jnp.swapaxes(by_zy, 0, 1).reshape((page_owners,) + by_y.shape[1:])]
    slice x4, local copies, waits for them, and re-layouts: 2.18 us -> 5.37 us  [gather_over_z(): parts.append(gathered[:, start:start + n])]
    concatenate x1, local copies, waits for them, and re-layouts: 3.53 us -> 0.69 us  [gather_over_y(): jnp.concatenate([p.reshape(-1, lanes) for p in pieces], axis=0)]
    reshape x0 -> x1, local copies, waits for them, and re-layouts: none -> 2.48 us  [gather_over_z(): gathered = by_yz.reshape((page_owners,) + by_y.shape[1:])]
  transfers between devices with their start and end apart: 8 -> 9, of which waited for: 6 -> 6; matrix products, arithmetic and copies ran while one was open for 15% -> 18% of each run, Pallas kernels for 0% -> 0%
where the time goes in v6:
time: 225 us; the launch traced here: 224 us
  waiting for transfers between devices  67.5 us (30%)
  local copies, waits for them, and re-layouts  47.9 us (21%)
  starting transfers between devices  43 us (19%)
  blocking collectives  25.8 us (11%)
  matrix products  22.5 us (10%)
  between operations  14.6 us (6%)
  other arithmetic  3.02 us (1%)
    all_to_all x2, waiting for transfers between devices, sum_to_owner(): got = lax.all_to_all(pieces, MP, split_axis=0, concat_axis=0, tiled=True)  28.6 us
    all_gather x2, blocking collectives, gather_over_y(): return lax.all_gather(flat_pieces, DP[0], axis=0, tiled=False)  25.8 us
    all_to_all x1, waiting for transfers between devices, body(): recv = lax.all_to_all(sent, DP, split_axis=0, concat_axis=0, tiled=True)  16.1 us
    gather x1, local copies, waits for them, and re-layouts, body(): chosen = pages[where_local]  12 us
    all_to_all x1, starting transfers between devices, body(): lax.all_to_all(codes.reshape(page_owners, cap), DP, split_axis=0, concat_...  10.8 us
    all_to_all x1, waiting for transfers between devices, body(): lax.all_to_all(codes.reshape(page_owners, cap), DP, split_axis=0, concat_...  9.87 us
    all_to_all x2, starting transfers between devices, sum_to_owner(): got = lax.all_to_all(pieces, MP, split_axis=0, concat_axis=0, tiled=True)  9.85 us
    all_to_all x1, waiting for transfers between devices, return_maxima(): lax.all_to_all(maxima.astype(jnp.bfloat16), DP, split_axis=0, concat_axis...  9.79 us
  transfers between devices with their start and end apart: 9, of which 6 were waited for; matrix products, arithmetic and copies ran while one was open for 18% of the time, Pallas kernels for 0%

profile of v6, /device:TPU:2, one launch (start us, length us, event | category | flops | bytes accessed | tf_op | source)
XLA Modules:
  0.0 224.3 jit_solution(6387781415400610785)
XLA Ops:
  11.6 12.8 %all-gather.4 = bf16[4,260,128]{2,1,0:T(8,128)(2,1)S(1)} all-gather(bf16[1,260,128]{2,1,0:T(8,128)(2,1)S(1)} %bitcast.143), channel_id=2, replica_groups=mesh['y'=4,'z'=8,'x'=4,'c'=2] {'y'}, dimensions={0}, use_global_device_ids=true | all-gather | bytes 332800 | tf_op jit(solution)/shard_map/all_gather | solution.py:30
  29.5 10.8 %all-to-all-start = ((s32[32,1,8]{2,1,0:T(1,128)}), s32[32,1,8]{2,1,0:T(1,128)S(1)}, u32[]{:S(2)}, u32[]{:S(2)}) async-start(s32[32,1,8]{2,1,0:T(1,128)} %bitcast.8), calls=%async_computation | async-start | bytes 32768 | tf_op jit(solution)/shard_map/all_to_all | solution.py:92
  40.4 9.9 %all-to-all-done = s32[32,1,8]{2,1,0:T(1,128)S(1)} async-done(((s32[32,1,8]{2,1,0:T(1,128)}), s32[32,1,8]{2,1,0:T(1,128)S(1)}, u32[]{:S(2)}, u32[]{:S(2)}) %all-to-all-start) | async-done | bytes 1056 | tf_op jit(solution)/shard_map/all_to_all | solution.py:92
  51.4 4.8 %all-to-all-start.1 = ((bf16[8,2,32,1024]{3,2,1,0:T(8,128)(2,1)}), bf16[8,2,32,1024]{3,2,1,0:T(8,128)(2,1)S(1)}, u32[]{:S(2)}, u32[]{:S(2)}) async-start(bf16[8,2,32,1024]{3,2,1,0:T(8,128)(2,1)} %broadcast_in_dim.25), calls=%async_computation.1 | async-start | bytes 2097152 | tf_op jit(solution)/shard_map/all_to_all | solution.py:112
  56.2 13.0 %all-gather.2 = bf16[1024,128]{1,0:T(8,128)(2,1)} all-gather(bf16[256,128]{1,0:T(8,128)(2,1)S(1)} %pad_maximum_fusion.1), channel_id=4, replica_groups=mesh['y'=4,'z'=8,'x'=4,'c'=2] {'y'}, dimensions={0}, use_global_device_ids=true | all-gather | bytes 327680 | tf_op jit(solution)/shard_map/all_gather | solution.py:30
  69.2 3.2 %copy.66 = bf16[4,2080,128]{2,1,0:T(8,128)(2,1)} copy(bf16[4,2080,128]{2,0,1:T(4,128)(2,1)} %all-gather.8.cloned.1.call-done) | data formatting | bytes 4259840 | tf_op jit(solution)/shard_map/all_gather | solution.py:34
  72.4 2.5 %reshape.345 = bf16[32,260,128]{2,1,0:T(8,128)(2,1)S(1)} reshape(bf16[4,2080,128]{2,1,0:T(8,128)(2,1)} %copy.66) | data formatting | bytes 4259840 | tf_op jit(solution)/shard_map/reshape | solution.py:35
  77.1 1.6 reshape.355
  88.9 4.8 %all-to-all-start.2 = ((bf16[8,64,1024]{2,1,0:T(8,128)(2,1)}), bf16[8,64,1024]{2,1,0:T(8,128)(2,1)S(1)}, u32[]{:S(2)}, u32[]{:S(2)}) async-start(bf16[8,64,1024]{2,1,0:T(8,128)(2,1)} %bitcast.30), calls=%async_computation.2 | async-start | bytes 2097152 | tf_op jit(solution)/shard_map/all_to_all | solution.py:24
  93.7 14.5 %all-to-all-done.2 = bf16[8,64,1024]{2,1,0:T(8,128)(2,1)S(1)} async-done(((bf16[8,64,1024]{2,1,0:T(8,128)(2,1)}), bf16[8,64,1024]{2,1,0:T(8,128)(2,1)S(1)}, u32[]{:S(2)}, u32[]{:S(2)}) %all-to-all-start.2) | async-done | bytes 1048608 | tf_op jit(solution)/shard_map/all_to_all | solution.py:24
  110.3 4.9 %all-to-all-start.3 = ((bf16[8,80,1024]{2,1,0:T(8,128)(2,1)}), bf16[8,80,1024]{2,1,0:T(8,128)(2,1)S(1)}, u32[]{:S(2)}, u32[]{:S(2)}) async-start(bf16[8,80,1024]{2,1,0:T(8,128)(2,1)} %broadcast_in_dim.27), calls=%async_computation.3 | async-start | bytes 2621440 | tf_op jit(solution)/shard_map/all_to_all | solution.py:147
  115.3 1.9 gather_fusion.2
  117.4 12.0 %gather_fusion.1 = bf16[256,128,128]{2,1,0:T(8,128)(2,1)} fusion(bf16[256,128,128]{2,1,0:T(8,128)(2,1)} %param.24, s32[1024]{0:T(1024)S(1)} %pad_clamp_fusion.1), kind=kCustom, calls=%fused_computation.1 | custom fusion | bytes 16778240 | tf_op jit(solution)/shard_map/gather | solution.py:100
  129.4 3.1 %all-to-all-done.3 = bf16[8,80,1024]{2,1,0:T(8,128)(2,1)S(1)} async-done(((bf16[8,80,1024]{2,1,0:T(8,128)(2,1)}), bf16[8,80,1024]{2,1,0:T(8,128)(2,1)S(1)}, u32[]{:S(2)}, u32[]{:S(2)}) %all-to-all-start.3) | async-done | bytes 1310752 | tf_op jit(solution)/shard_map/all_to_all | solution.py:147
  132.5 3.2 %fusion.118 = (bf16[32,128,128]{2,1,0:T(8,128)(2,1)}, bf16[32,128,128]{2,1,0:T(8,128)(2,1)S(1)}) fusion(bf16[32,256,128]{2,1,0:T(8,128)(2,1)} %bitcast.127), kind=kLoop, calls=%fused_computation.198 | loop fusion | bytes 4194304 | tf_op jit(solution)/shard_map/slice | solution.py:40
  135.8 2.6 %reshape.364 = bf16[1024,512]{1,0:T(8,128)(2,1)} reshape(bf16[32,128,128]{2,1,0:T(8,128)(2,1)} %get-tuple-element.30) | data formatting | bytes 2097152 | tf_op jit(solution)/shard_map/reshape | solution.py:106
  139.8 5.9 %convolution_convert_fusion.1 = bf16[512,1024]{1,0:T(8,128)(2,1)} fusion(bf16[1024,512]{1,0:T(8,128)(2,1)} %reshape.365, bf16[512,1024]{1,0:T(8,128)(2,1)S(1)} %bitcast.120, bf16[1024,512]{1,0:T(8,128)(2,1)} %reshape.364), kind=kOutput, calls=%fused_computation.18 | convolution fusion | flops 1091305472 | bytes 4194304 | tf_op jit(solution)/shard_map/dot_general | solution.py:156
  145.7 5.0 %all-to-all-start.4 = ((bf16[8,64,1024]{2,1,0:T(8,128)(2,1)}), bf16[8,64,1024]{2,1,0:T(8,128)(2,1)S(1)}, u32[]{:S(2)}, u32[]{:S(2)}) async-start(bf16[8,64,1024]{2,1,0:T(8,128)(2,1)} %bitcast.36), calls=%async_computation.4 | async-start | bytes 2097152 | tf_op jit(solution)/shard_map/all_to_all | solution.py:24
  151.2 14.1 %all-to-all-done.4 = bf16[8,64,1024]{2,1,0:T(8,128)(2,1)S(1)} async-done(((bf16[8,64,1024]{2,1,0:T(8,128)(2,1)}), bf16[8,64,1024]{2,1,0:T(8,128)(2,1)S(1)}, u32[]{:S(2)}, u32[]{:S(2)}) %all-to-all-start.4) | async-done | bytes 1048608 | tf_op jit(solution)/shard_map/all_to_all | solution.py:24
  167.3 6.9 %all-to-all-start.5 = ((bf16[32,2,32,128]{3,2,1,0:T(8,128)(2,1)}), bf16[32,2,32,128]{3,2,1,0:T(8,128)(2,1)S(1)}, u32[]{:S(2)}, u32[]{:S(2)}) async-start(bf16[32,2,32,128]{3,2,1,0:T(8,128)(2,1)} %broadcast_in_dim.32), calls=%async_computation.5 | async-start | bytes 1048576 | tf_op jit(solution)/shard_map/all_to_all | solution.py:167
  174.4 16.1 %all-to-all-done.5 = bf16[32,2,32,128]{3,2,1,0:T(8,128)(2,1)S(1)} async-done(((bf16[32,2,32,128]{3,2,1,0:T(8,128)(2,1)}), bf16[32,2,32,128]{3,2,1,0:T(8,128)(2,1)S(1)}, u32[]{:S(2)}, u32[]{:S(2)}) %all-to-all-start.5) | async-done | bytes 524320 | tf_op jit(solution)/shard_map/all_to_all | solution.py:167
  191.8 8.0 %select_reduce_fusion = bf16[32,8,32]{2,1,0:T(8,128)(2,1)S(1)} fusion(bf16[32,8,128,128]{3,2,1,0:T(8,128)(2,1)} %bitcast.119, bf16[32,8,32,128]{3,2,1,0:T(8,128)(2,1)S(1)} %bitcast.128, pred[32,8]{1,0:T(8,128)(4,1)S(1)} %compare_and_fusion, pred[32,8,128]{2,1,0:T(8,128)(4,1)S(1)} %iota_compare_fusion.1), kind=kOutput, calls=%fused_computation.7 | convolution fusion | flops 271572992 | bytes 10535168 | tf_op jit(solution)/shard_map/snie,snte->snit/dot_general | solution.py:170
  200.6 5.7 %all-to-all-start.6 = ((bf16[32,2,128]{2,1,0:T(2,128)(2,1)}), bf16[32,2,128]{2,1,0:T(2,128)(2,1)S(1)}, u32[]{:S(2)}, u32[]{:S(2)}) async-start(bf16[32,2,128]{2,1,0:T(2,128)(2,1)} %reshape.448), calls=%async_computation.6 | async-start | bytes 32768 | tf_op jit(solution)/shard_map/all_to_all | solution.py:46
  206.2 9.8 %all-to-all-done.6 = bf16[32,2,128]{2,1,0:T(2,128)(2,1)S(1)} async-done(((bf16[32,2,128]{2,1,0:T(2,128)(2,1)}), bf16[32,2,128]{2,1,0:T(2,128)(2,1)S(1)}, u32[]{:S(2)}, u32[]{:S(2)}) %all-to-all-start.6) | async-done | bytes 16416 | tf_op jit(solution)/shard_map/all_to_all | solution.py:46
  (126 shorter events, 32.5 us)
Async XLA Ops:
  7.2 19.0 %copy-start = (s32[8192]{0:T(1024)S(1)}, s32[8192]{0:T(1024)}, u32[]{:S(2)}) copy-start(s32[8192]{0:T(1024)} %param.26) | copy-start | bytes 98308
  7.2 33.1 %copy-start.10 = (bf16[32,512]{1,0:T(8,128)(2,1)S(1)}, bf16[32,512]{1,0:T(8,128)(2,1)}, u32[]{:S(2)}) copy-start(bf16[32,512]{1,0:T(8,128)(2,1)} %param.21) | copy-start | bytes 98308
  7.2 33.2 %copy-start.11 = (bf16[512,32]{0,1:T(8,128)(2,1)S(1)}, bf16[512,32]{0,1:T(8,128)(2,1)}, u32[]{:S(2)}) copy-start(bf16[512,32]{0,1:T(8,128)(2,1)} %param.22) | copy-start | bytes 98308
  7.2 43.1 %copy-start.3 = (bf16[2,32,1024]{2,1,0:T(8,128)(2,1)S(1)}, bf16[2,32,1024]{2,1,0:T(8,128)(2,1)}, u32[]{:S(2)}) copy-start(bf16[2,32,1024]{2,1,0:T(8,128)(2,1)} %param.14) | copy-start | bytes 393220
  7.2 62.0 %all-gather.8.cloned.1.call-start = ((), (), s32[]{:S(2)}) async-start(), calls=%async_computation.7 | async-start | bytes 2396160 | tf_op jit(solution)/shard_map/all_gather | solution.py:34
  29.5 20.8 %all-to-all-start = ((s32[32,1,8]{2,1,0:T(1,128)}), s32[32,1,8]{2,1,0:T(1,128)S(1)}, u32[]{:S(2)}, u32[]{:S(2)}) async-start(s32[32,1,8]{2,1,0:T(1,128)} %bitcast.8), calls=%async_computation | async-start | bytes 32768 | tf_op jit(solution)/shard_map/all_to_all | solution.py:92
  51.4 28.3 %all-to-all-start.1 = ((bf16[8,2,32,1024]{3,2,1,0:T(8,128)(2,1)}), bf16[8,2,32,1024]{3,2,1,0:T(8,128)(2,1)S(1)}, u32[]{:S(2)}, u32[]{:S(2)}) async-start(bf16[8,2,32,1024]{3,2,1,0:T(8,128)(2,1)} %broadcast_in_dim.25), calls=%async_computation.1 | async-start | bytes 2097152 | tf_op jit(solution)/shard_map/all_to_all | solution.py:112
  56.2 76.3 %all-gather.10.cloned.1.call-start = ((), (), s32[]{:S(2)}) async-start(), calls=%async_computation.8 | async-start | bytes 2359296 | tf_op jit(solution)/shard_map/all_gather | solution.py:34
  77.1 1.6 copy-start.4
  77.1 2.1 copy-start.5
  79.2 1.5 copy-start.7
  81.2 1.0 copy-start.8
  86.5 1.0 copy-start.6
  88.9 19.3 %all-to-all-start.2 = ((bf16[8,64,1024]{2,1,0:T(8,128)(2,1)}), bf16[8,64,1024]{2,1,0:T(8,128)(2,1)S(1)}, u32[]{:S(2)}, u32[]{:S(2)}) async-start(bf16[8,64,1024]{2,1,0:T(8,128)(2,1)} %bitcast.30), calls=%async_computation.2 | async-start | bytes 2097152 | tf_op jit(solution)/shard_map/all_to_all | solution.py:24
  109.0 6.3 %copy-start.1 = (s32[256]{0:T(256)S(1)}, s32[256]{0:T(256)}, u32[]{:S(2)}) copy-start(s32[256]{0:T(256)} %param.25) | copy-start | bytes 3076
  110.3 22.3 %all-to-all-start.3 = ((bf16[8,80,1024]{2,1,0:T(8,128)(2,1)}), bf16[8,80,1024]{2,1,0:T(8,128)(2,1)S(1)}, u32[]{:S(2)}, u32[]{:S(2)}) async-start(bf16[8,80,1024]{2,1,0:T(8,128)(2,1)} %broadcast_in_dim.27), calls=%async_computation.3 | async-start | bytes 2621440 | tf_op jit(solution)/shard_map/all_to_all | solution.py:147
  132.5 3.2 %copy-start.2 = (bf16[8,80,1024]{2,1,0:T(8,128)(2,1)}, bf16[8,80,1024]{2,1,0:T(8,128)(2,1)S(1)}, u32[]{:S(2)}) copy-start(bf16[8,80,1024]{2,1,0:T(8,128)(2,1)S(1)} %all-to-all-done.3) | copy-start | bytes 3932164
  135.8 4.1 %slice-start = ((bf16[8,80,1024]{2,1,0:T(8,128)(2,1)}), bf16[8,64,1024]{2,1,0:T(8,128)(2,1)S(1)}, s32[]{:S(2)}) async-start(bf16[8,80,1024]{2,1,0:T(8,128)(2,1)} %copy-done.2), calls=%async_computation.9 | async-start | bytes 2097152 | tf_op jit(solution)/shard_map/slice | solution.py:150
  145.7 5.2 %slice-start.1 = ((bf16[8,80,1024]{2,1,0:T(8,128)(2,1)}), bf16[8,16,1024]{2,1,0:T(8,128)(2,1)S(1)}, s32[]{:S(2)}) async-start(bf16[8,80,1024]{2,1,0:T(8,128)(2,1)} %copy-done.2), calls=%async_computation.10 | async-start | bytes 524288 | tf_op jit(solution)/shard_map/slice | solution.py:151
  145.7 19.6 %all-to-all-start.4 = ((bf16[8,64,1024]{2,1,0:T(8,128)(2,1)}), bf16[8,64,1024]{2,1,0:T(8,128)(2,1)S(1)}, u32[]{:S(2)}, u32[]{:S(2)}) async-start(bf16[8,64,1024]{2,1,0:T(8,128)(2,1)} %bitcast.36), calls=%async_computation.4 | async-start | bytes 2097152 | tf_op jit(solution)/shard_map/all_to_all | solution.py:24
  166.3 25.5 %copy-start.9 = (bf16[64,128]{1,0:T(8,128)(2,1)}, bf16[64,128]{1,0:T(8,128)(2,1)S(1)}, u32[]{:S(2)}) copy-start(bf16[64,128]{1,0:T(8,128)(2,1)S(1)} %divide_convert_fusion.4) | copy-start | bytes 49156
  167.3 23.2 %all-to-all-start.5 = ((bf16[32,2,32,128]{3,2,1,0:T(8,128)(2,1)}), bf16[32,2,32,128]{3,2,1,0:T(8,128)(2,1)S(1)}, u32[]{:S(2)}, u32[]{:S(2)}) async-start(bf16[32,2,32,128]{3,2,1,0:T(8,128)(2,1)} %broadcast_in_dim.32), calls=%async_computation.5 | async-start | bytes 1048576 | tf_op jit(solution)/shard_map/all_to_all | solution.py:167
  200.6 15.5 %all-to-all-start.6 = ((bf16[32,2,128]{2,1,0:T(2,128)(2,1)}), bf16[32,2,128]{2,1,0:T(2,128)(2,1)S(1)}, u32[]{:S(2)}, u32[]{:S(2)}) async-start(bf16[32,2,128]{2,1,0:T(2,128)(2,1)} %reshape.448), calls=%async_computation.6 | async-start | bytes 32768 | tf_op jit(solution)/shard_map/all_to_all | solution.py:46
Sparse Core Ops, SparseCore 0:
  25.3 43.5 all-gather.7
  80.8 39.0 all-gather.9

commit v7 on v6

--- a/solution.py
+++ b/solution.py
@@ -26,7 +26,9 @@
 
 
 def gather_over_y(pieces, lanes):
-    flat_pieces = jnp.concatenate([p.reshape(-1, lanes) for p in pieces], axis=0)
+    rows = sum(p.size // lanes for p in pieces)
+    pad = jnp.zeros((-rows % 16, lanes), pieces[0].dtype)
+    flat_pieces = jnp.concatenate([p.reshape(-1, lanes) for p in pieces] + [pad], axis=0)
     return lax.all_gather(flat_pieces, DP[0], axis=0, tiled=False)
 
 
@@ -143,6 +145,7 @@
     attn = sum_to_owner(attn_terms, n_mp)
     own = hidden.reshape(qry_dev * qlen, width).astype(jnp.float32)
     mid = layer_norm(own + attn).astype(jnp.bfloat16)
+    chosen, lens, mid = lax.optimization_barrier((chosen, lens, mid))
     both = jnp.concatenate([mid, g_proj.reshape(-1, mid.shape[1])], axis=0)
     both_all = lax.all_to_all(
         jnp.broadcast_to(both[None], (n_mp,) + both.shape), MP, split_axis=0, concat_axis=0, tiled=True
@@ -150,7 +153,6 @@
     mid_all = both_all[:, : mid.shape[0]].reshape((n_mp * mid.shape[0], mid.shape[1]))
     proj_all = both_all[:, mid.shape[0] :].reshape((n_mp,) + g_proj.shape)
     wp = jnp.transpose(proj_all, (1, 0, 2, 3)).reshape(page_owners * n_mp * w_proj.shape[0], w_proj.shape[1])
-    chosen, lens, mid_all = lax.optimization_barrier((chosen, lens, mid_all))
     up = add_rows(mid_all, wu)
     inner = jax.nn.gelu(up, approximate=False).astype(jnp.bfloat16)
     down_terms = jnp.dot(inner, wd, preferred_element_type=jnp.float32)

time: 225 us -> 219 us (0.973)
  blocking collectives: 25.8 us -> 48.3 us
  waiting for transfers between devices: 67.5 us -> 48.8 us
  local copies, waits for them, and re-layouts: 47.9 us -> 42.2 us
  starting transfers between devices: 43 us -> 37.5 us
    all_to_all x0 -> x1, blocking collectives: none -> 21.7 us  [body(): lax.all_to_all(jnp.broadcast_to(both[None], (n_mp,) + both.shape), MP, sp...]
    all_to_all x2, waiting for transfers between devices: 28.6 us -> 14.5 us  [sum_to_owner(): got = lax.all_to_all(pieces, MP, split_axis=0, concat_axis=0, tiled=True)]
    all_to_all x1 -> x0, starting transfers between devices: 4.94 us -> none  [body(): lax.all_to_all(jnp.broadcast_to(both[None], (n_mp,) + both.shape), MP, sp...]
    all_gather x2 -> x0, local copies, waits for them, and re-layouts: 4.03 us -> none  [the longest x1 3.2 us: gather_over_z(): by_yz = lax.all_gather(by_y, DP[1], axis=1, tiled=False)]
    all_to_all x1 -> x0, waiting for transfers between devices: 3.15 us -> none  [body(): lax.all_to_all(jnp.broadcast_to(both[None], (n_mp,) + both.shape), MP, sp...]
    concatenate x1, local copies, waits for them, and re-layouts: 0.69 us -> 3.6 us  [gather_over_y(): jnp.concatenate([p.reshape(-1, lanes) for p in pieces] + [pad], axis=0)]
    reshape x1 -> x0, local copies, waits for them, and re-layouts: 2.48 us -> none  [gather_over_z(): gathered = by_yz.reshape((page_owners,) + by_y.shape[1:])]
  transfers between devices with their start and end apart: 9 -> 8, of which waited for: 6 -> 5; matrix products, arithmetic and copies ran while one was open for 18% -> 17% of each run, Pallas kernels for 0% -> 0%
where the time goes in v7:
time: 219 us; the launch traced here: 217 us
  waiting for transfers between devices  48.8 us (22%)
  blocking collectives  48.3 us (22%)
  local copies, waits for them, and re-layouts  42.2 us (19%)
  starting transfers between devices  37.5 us (17%)
  matrix products  23.3 us (11%)
  between operations  14.6 us (7%)
  other arithmetic  2.77 us (1%)
    all_gather x2, blocking collectives, gather_over_y(): return lax.all_gather(flat_pieces, DP[0], axis=0, tiled=False)  26.5 us
    all_to_all x1, blocking collectives, body(): lax.all_to_all(jnp.broadcast_to(both[None], (n_mp,) + both.shape), MP, sp...  21.7 us
    all_to_all x1, waiting for transfers between devices, body(): recv = lax.all_to_all(sent, DP, split_axis=0, concat_axis=0, tiled=True)  16.1 us
    all_to_all x2, waiting for transfers between devices, sum_to_owner(): got = lax.all_to_all(pieces, MP, split_axis=0, concat_axis=0, tiled=True)  14.5 us
    gather x1, local copies, waits for them, and re-layouts, body(): chosen = pages[where_local]  12 us
    all_to_all x1, starting transfers between devices, body(): lax.all_to_all(codes.reshape(page_owners, cap), DP, split_axis=0, concat_...  11 us
    all_to_all x1, waiting for transfers between devices, return_maxima(): lax.all_to_all(maxima.astype(jnp.bfloat16), DP, split_axis=0, concat_axis...  9.79 us
    all_to_all x2, starting transfers between devices, sum_to_owner(): got = lax.all_to_all(pieces, MP, split_axis=0, concat_axis=0, tiled=True)  9.74 us
  transfers between devices with their start and end apart: 8, of which 5 were waited for; matrix products, arithmetic and copies ran while one was open for 17% of the time, Pallas kernels for 0%

profile of v7, /device:TPU:2, one launch (start us, length us, event | category | flops | bytes accessed | tf_op | source)
XLA Modules:
  0.0 217.4 jit_solution(8789179787094052166)
XLA Ops:
  8.0 3.6 %concatenate.9 = bf16[272,128]{1,0:T(8,128)(2,1)S(1)} concatenate(bf16[32,128]{1,0:T(8,128)(2,1)} %param.15, bf16[32,128]{1,0:T(8,128)(2,1)} %param.16, bf16[32,128]{1,0:T(8,128)(2,1)} %param.17, bf16[32,128]{1,0:T(8,128)(2,1)} %bitcast.139, bf16[128,128]{1,0:T(8,128)(2,1)S(1)} %reshape.284, bf16[4,128]{1,0:T(4,128)(2,1)} %param.23, bf16[12,128]{1,0:T(8,128)(2,1)S(1)} %broadcast_in_dim.26), dimensions={0} | concatenate | bytes 139264 | tf_op jit(solution)/shard_map/concatenate | solution.py:31
  11.6 13.5 %all-gather = bf16[1088,128]{1,0:T(8,128)(2,1)} all-gather(bf16[272,128]{1,0:T(8,128)(2,1)S(1)} %concatenate.9), channel_id=2, replica_groups=mesh['y'=4,'z'=8,'x'=4,'c'=2] {'y'}, dimensions={0}, use_global_device_ids=true | all-gather | bytes 348160 | tf_op jit(solution)/shard_map/all_gather | solution.py:32
  29.4 11.0 %all-to-all-start = ((s32[32,1,8]{2,1,0:T(1,128)}), s32[32,1,8]{2,1,0:T(1,128)S(1)}, u32[]{:S(2)}, u32[]{:S(2)}) async-start(s32[32,1,8]{2,1,0:T(1,128)} %bitcast.9), calls=%async_computation | async-start | bytes 32768 | tf_op jit(solution)/shard_map/all_to_all | solution.py:94
  42.0 8.4 %all-to-all-done = s32[32,1,8]{2,1,0:T(1,128)S(1)} async-done(((s32[32,1,8]{2,1,0:T(1,128)}), s32[32,1,8]{2,1,0:T(1,128)S(1)}, u32[]{:S(2)}, u32[]{:S(2)}) %all-to-all-start) | async-done | bytes 1056 | tf_op jit(solution)/shard_map/all_to_all | solution.py:94
  50.4 2.0 broadcast_in_dim.29
  52.4 4.8 %all-to-all-start.1 = ((bf16[8,2,32,1024]{3,2,1,0:T(8,128)(2,1)}), bf16[8,2,32,1024]{3,2,1,0:T(8,128)(2,1)S(1)}, u32[]{:S(2)}, u32[]{:S(2)}) async-start(bf16[8,2,32,1024]{3,2,1,0:T(8,128)(2,1)} %broadcast_in_dim.29), calls=%async_computation.1 | async-start | bytes 2097152 | tf_op jit(solution)/shard_map/all_to_all | solution.py:114
  57.2 13.0 %all-gather.2 = bf16[1024,128]{1,0:T(8,128)(2,1)} all-gather(bf16[256,128]{1,0:T(8,128)(2,1)S(1)} %pad_maximum_fusion.1), channel_id=4, replica_groups=mesh['y'=4,'z'=8,'x'=4,'c'=2] {'y'}, dimensions={0}, use_global_device_ids=true | all-gather | bytes 327680 | tf_op jit(solution)/shard_map/all_gather | solution.py:32
  72.4 2.1 fusion.118
  75.5 1.5 convolution_convert_fusion.4
  86.3 4.8 %all-to-all-start.2 = ((bf16[8,64,1024]{2,1,0:T(8,128)(2,1)}), bf16[8,64,1024]{2,1,0:T(8,128)(2,1)S(1)}, u32[]{:S(2)}, u32[]{:S(2)}) async-start(bf16[8,64,1024]{2,1,0:T(8,128)(2,1)} %bitcast.33), calls=%async_computation.2 | async-start | bytes 2097152 | tf_op jit(solution)/shard_map/all_to_all | solution.py:24
  91.2 1.9 gather_fusion.2
  93.3 12.0 %gather_fusion.1 = bf16[256,128,128]{2,1,0:T(8,128)(2,1)} fusion(bf16[256,128,128]{2,1,0:T(8,128)(2,1)} %param.24, s32[1024]{0:T(1024)S(1)} %pad_clamp_fusion.1), kind=kCustom, calls=%fused_computation.1 | custom fusion | bytes 16778240 | tf_op jit(solution)/shard_map/gather | solution.py:102
  107.1 21.7 %all_to_all.42 = bf16[8,80,1024]{2,1,0:T(8,128)(2,1)S(1)} all-to-all(bf16[8,80,1024]{2,1,0:T(8,128)(2,1)S(1)} %broadcast_in_dim.30), channel_id=1, replica_groups=mesh['y'=4,'z'=8,'x'=4,'c'=2] {'x','c'}, dimensions={0} | all-to-all | bytes 2621440 | tf_op jit(solution)/shard_map/all_to_all | solution.py:150
  128.9 2.2 fusion.119
  131.0 1.4 reshape.304
  132.5 1.5 reshape.305
  134.0 5.6 %convolution_convert_fusion.1 = bf16[512,1024]{1,0:T(8,128)(2,1)} fusion(bf16[1024,512]{1,0:T(8,128)(2,1)} %reshape.305, bf16[512,1024]{1,0:T(8,128)(2,1)S(1)} %bitcast.113, bf16[1024,512]{1,0:T(8,128)(2,1)S(1)} %copy-done.7), kind=kOutput, calls=%fused_computation.18 | convolution fusion | flops 1091305472 | bytes 4194304 | tf_op jit(solution)/shard_map/dot_general | solution.py:158
  139.6 4.9 %all-to-all-start.4 = ((bf16[8,64,1024]{2,1,0:T(8,128)(2,1)}), bf16[8,64,1024]{2,1,0:T(8,128)(2,1)S(1)}, u32[]{:S(2)}, u32[]{:S(2)}) async-start(bf16[8,64,1024]{2,1,0:T(8,128)(2,1)} %bitcast.37), calls=%async_computation.4 | async-start | bytes 2097152 | tf_op jit(solution)/shard_map/all_to_all | solution.py:24
  144.8 14.2 %all-to-all-done.4 = bf16[8,64,1024]{2,1,0:T(8,128)(2,1)S(1)} async-done(((bf16[8,64,1024]{2,1,0:T(8,128)(2,1)}), bf16[8,64,1024]{2,1,0:T(8,128)(2,1)S(1)}, u32[]{:S(2)}, u32[]{:S(2)}) %all-to-all-start.4) | async-done | bytes 1048608 | tf_op jit(solution)/shard_map/all_to_all | solution.py:24
  161.0 6.3 %all-to-all-start.5 = ((bf16[32,2,32,128]{3,2,1,0:T(8,128)(2,1)}), bf16[32,2,32,128]{3,2,1,0:T(8,128)(2,1)S(1)}, u32[]{:S(2)}, u32[]{:S(2)}) async-start(bf16[32,2,32,128]{3,2,1,0:T(8,128)(2,1)} %broadcast_in_dim.35), calls=%async_computation.5 | async-start | bytes 1048576 | tf_op jit(solution)/shard_map/all_to_all | solution.py:169
  167.5 16.1 %all-to-all-done.5 = bf16[32,2,32,128]{3,2,1,0:T(8,128)(2,1)S(1)} async-done(((bf16[32,2,32,128]{3,2,1,0:T(8,128)(2,1)}), bf16[32,2,32,128]{3,2,1,0:T(8,128)(2,1)S(1)}, u32[]{:S(2)}, u32[]{:S(2)}) %all-to-all-start.5) | async-done | bytes 524320 | tf_op jit(solution)/shard_map/all_to_all | solution.py:169
  184.9 8.0 %select_reduce_fusion = bf16[32,8,32]{2,1,0:T(8,128)(2,1)S(1)} fusion(bf16[32,8,128,128]{3,2,1,0:T(8,128)(2,1)} %bitcast.112, bf16[32,8,32,128]{3,2,1,0:T(8,128)(2,1)S(1)} %bitcast.119, pred[32,8]{1,0:T(8,128)(4,1)S(1)} %compare_and_fusion, pred[32,8,128]{2,1,0:T(8,128)(4,1)S(1)} %iota_compare_fusion.1), kind=kOutput, calls=%fused_computation.7 | convolution fusion | flops 271572992 | bytes 10535168 | tf_op jit(solution)/shard_map/snie,snte->snit/dot_general | solution.py:172
  193.6 5.7 %all-to-all-start.6 = ((bf16[32,2,128]{2,1,0:T(2,128)(2,1)}), bf16[32,2,128]{2,1,0:T(2,128)(2,1)S(1)}, u32[]{:S(2)}, u32[]{:S(2)}) async-start(bf16[32,2,128]{2,1,0:T(2,128)(2,1)} %reshape.384), calls=%async_computation.6 | async-start | bytes 32768 | tf_op jit(solution)/shard_map/all_to_all | solution.py:48
  199.3 9.8 %all-to-all-done.6 = bf16[32,2,128]{2,1,0:T(2,128)(2,1)S(1)} async-done(((bf16[32,2,128]{2,1,0:T(2,128)(2,1)}), bf16[32,2,128]{2,1,0:T(2,128)(2,1)S(1)}, u32[]{:S(2)}, u32[]{:S(2)}) %all-to-all-start.6) | async-done | bytes 16416 | tf_op jit(solution)/shard_map/all_to_all | solution.py:48
  (115 shorter events, 26.8 us)
Async XLA Ops:
  7.2 18.9 %copy-start = (s32[8192]{0:T(1024)S(1)}, s32[8192]{0:T(1024)}, u32[]{:S(2)}) copy-start(s32[8192]{0:T(1024)} %param.26) | copy-start | bytes 98308
  7.2 63.0 %all-gather.7.cloned.1.call-start = ((), (), s32[]{:S(2)}) async-start(), calls=%async_computation.7 | async-start | bytes 2506752 | tf_op jit(solution)/shard_map/all_gather | solution.py:36
  29.4 20.9 %all-to-all-start = ((s32[32,1,8]{2,1,0:T(1,128)}), s32[32,1,8]{2,1,0:T(1,128)S(1)}, u32[]{:S(2)}, u32[]{:S(2)}) async-start(s32[32,1,8]{2,1,0:T(1,128)} %bitcast.9), calls=%async_computation | async-start | bytes 32768 | tf_op jit(solution)/shard_map/all_to_all | solution.py:94
  52.4 24.6 %all-to-all-start.1 = ((bf16[8,2,32,1024]{3,2,1,0:T(8,128)(2,1)}), bf16[8,2,32,1024]{3,2,1,0:T(8,128)(2,1)S(1)}, u32[]{:S(2)}, u32[]{:S(2)}) async-start(bf16[8,2,32,1024]{3,2,1,0:T(8,128)(2,1)} %broadcast_in_dim.29), calls=%async_computation.1 | async-start | bytes 2097152 | tf_op jit(solution)/shard_map/all_to_all | solution.py:114
  57.2 71.7 %all-gather.9.cloned.1.call-start = ((), (), s32[]{:S(2)}) async-start(), calls=%async_computation.8 | async-start | bytes 2359296 | tf_op jit(solution)/shard_map/all_gather | solution.py:36
  75.0 2.0 copy-start.3
  75.5 2.5 %copy-start.9 = (bf16[32,32,128]{2,1,0:T(8,128)(2,1)S(1)}, bf16[32,32,128]{2,1,0:T(8,128)(2,1)}, u32[]{:S(2)}) copy-start(bf16[32,32,128]{2,1,0:T(8,128)(2,1)} %get-tuple-element.16) | copy-start | bytes 786436
  78.6 1.2 copy-start.10
  83.9 1.0 copy-start.8
  84.7 6.5 %copy-start.1 = (s32[256]{0:T(256)S(1)}, s32[256]{0:T(256)}, u32[]{:S(2)}) copy-start(s32[256]{0:T(256)} %param.25) | copy-start | bytes 3076
  86.3 19.3 %all-to-all-start.2 = ((bf16[8,64,1024]{2,1,0:T(8,128)(2,1)}), bf16[8,64,1024]{2,1,0:T(8,128)(2,1)S(1)}, u32[]{:S(2)}, u32[]{:S(2)}) async-start(bf16[8,64,1024]{2,1,0:T(8,128)(2,1)} %bitcast.33), calls=%async_computation.2 | async-start | bytes 2097152 | tf_op jit(solution)/shard_map/all_to_all | solution.py:24
  93.2 12.5 %copy-start.4 = (bf16[2,32,1024]{2,1,0:T(8,128)(2,1)S(1)}, bf16[2,32,1024]{2,1,0:T(8,128)(2,1)}, u32[]{:S(2)}) copy-start(bf16[2,32,1024]{2,1,0:T(8,128)(2,1)} %param.14) | copy-start | bytes 393220
  106.3 0.6 copy-start.5
  128.9 2.2 copy-start.2
  131.0 3.0 %slice-start = ((bf16[8,80,1024]{2,1,0:T(8,128)(2,1)}), bf16[8,64,1024]{2,1,0:T(8,128)(2,1)S(1)}, s32[]{:S(2)}) async-start(bf16[8,80,1024]{2,1,0:T(8,128)(2,1)} %copy-done.2), calls=%async_computation.9 | async-start | bytes 2097152 | tf_op jit(solution)/shard_map/slice | solution.py:153
  132.5 1.5 copy-start.7
  139.6 4.9 %slice-start.1 = ((bf16[8,80,1024]{2,1,0:T(8,128)(2,1)}), bf16[8,16,1024]{2,1,0:T(8,128)(2,1)S(1)}, s32[]{:S(2)}) async-start(bf16[8,80,1024]{2,1,0:T(8,128)(2,1)} %copy-done.2), calls=%async_computation.10 | async-start | bytes 524288 | tf_op jit(solution)/shard_map/slice | solution.py:154
  139.6 19.6 %copy-start.6 = (bf16[64,1024]{1,0:T(8,128)(2,1)S(1)}, bf16[64,1024]{1,0:T(8,128)(2,1)}, u32[]{:S(2)}) copy-start(bf16[64,1024]{1,0:T(8,128)(2,1)} %copy-done.5) | copy-start | bytes 393220
  139.6 19.4 %all-to-all-start.4 = ((bf16[8,64,1024]{2,1,0:T(8,128)(2,1)}), bf16[8,64,1024]{2,1,0:T(8,128)(2,1)S(1)}, u32[]{:S(2)}, u32[]{:S(2)}) async-start(bf16[8,64,1024]{2,1,0:T(8,128)(2,1)} %bitcast.37), calls=%async_computation.4 | async-start | bytes 2097152 | tf_op jit(solution)/shard_map/all_to_all | solution.py:24
  160.0 24.9 %copy-start.11 = (bf16[64,128]{1,0:T(8,128)(2,1)}, bf16[64,128]{1,0:T(8,128)(2,1)S(1)}, u32[]{:S(2)}) copy-start(bf16[64,128]{1,0:T(8,128)(2,1)S(1)} %divide_convert_fusion.4) | copy-start | bytes 49156
  161.0 22.6 %all-to-all-start.5 = ((bf16[32,2,32,128]{3,2,1,0:T(8,128)(2,1)}), bf16[32,2,32,128]{3,2,1,0:T(8,128)(2,1)S(1)}, u32[]{:S(2)}, u32[]{:S(2)}) async-start(bf16[32,2,32,128]{3,2,1,0:T(8,128)(2,1)} %broadcast_in_dim.35), calls=%async_computation.5 | async-start | bytes 1048576 | tf_op jit(solution)/shard_map/all_to_all | solution.py:169
  193.6 15.5 %all-to-all-start.6 = ((bf16[32,2,128]{2,1,0:T(2,128)(2,1)}), bf16[32,2,128]{2,1,0:T(2,128)(2,1)S(1)}, u32[]{:S(2)}, u32[]{:S(2)}) async-start(bf16[32,2,128]{2,1,0:T(2,128)(2,1)} %reshape.384), calls=%async_computation.6 | async-start | bytes 32768 | tf_op jit(solution)/shard_map/all_to_all | solution.py:48
Sparse Core Ops, SparseCore 0:
  25.3 43.5 all-gather.6
  78.1 38.5 all-gather.8

commit v8 on v7

--- a/solution.py
+++ b/solution.py
@@ -167,11 +167,12 @@
 
     sent = jnp.broadcast_to(vectors[None], (page_owners, qry_dev, qlen, width_out))
     recv = lax.all_to_all(sent, DP, split_axis=0, concat_axis=0, tiled=True)
-    rows_in = jnp.take_along_axis(recv, which_query[:, :, None, None], axis=1)
     token_positions = jnp.arange(ptok, dtype=jnp.int32)
-    sim = jnp.einsum("snie,snte->snit", rows_in, chosen, preferred_element_type=jnp.float32)
-    valid = token_positions[None, None, None, :] < lens[:, :, None, None]
-    returned = return_maxima(jnp.max(jnp.where(valid, sim, -1e30), axis=-1))
+    sim = jnp.einsum("sqie,snte->snqit", recv, chosen, preferred_element_type=jnp.float32)
+    valid = token_positions[None, None, None, None, :] < lens[:, :, None, None, None]
+    both_best = jnp.max(jnp.where(valid, sim, -1e30), axis=-1)
+    picked = jnp.take_along_axis(both_best, which_query[:, :, None, None], axis=2)[:, :, 0]
+    returned = return_maxima(picked)
     best = returned.reshape(page_owners * cap, qlen)[index]
     best = best.reshape(qry_dev, ncand, ppc, qlen)
     scores = jnp.sum(jnp.max(best, axis=2), axis=-1)

time: 219 us -> 218 us (level)
  no operation moved by 1% of the time
where the time goes in v8:
time: 218 us; the launch traced here: 217 us
  waiting for transfers between devices  48.7 us (22%)
  blocking collectives  48.3 us (22%)
  local copies, waits for them, and re-layouts  42.7 us (20%)
  starting transfers between devices  37.5 us (17%)
  matrix products  21.9 us (10%)
  between operations  14.6 us (7%)
  other arithmetic  2.87 us (1%)
    all_gather x2, blocking collectives, gather_over_y(): return lax.all_gather(flat_pieces, DP[0], axis=0, tiled=False)  26.5 us
    all_to_all x1, blocking collectives, body(): lax.all_to_all(jnp.broadcast_to(both[None], (n_mp,) + both.shape), MP, sp...  21.7 us
    all_to_all x1, waiting for transfers between devices, body(): recv = lax.all_to_all(sent, DP, split_axis=0, concat_axis=0, tiled=True)  15.9 us
    all_to_all x2, waiting for transfers between devices, sum_to_owner(): got = lax.all_to_all(pieces, MP, split_axis=0, concat_axis=0, tiled=True)  14.6 us
    gather x1, local copies, waits for them, and re-layouts, body(): chosen = pages[where_local]  11.9 us
    all_to_all x1, starting transfers between devices, body(): lax.all_to_all(codes.reshape(page_owners, cap), DP, split_axis=0, concat_...  11 us
    all_to_all x1, waiting for transfers between devices, return_maxima(): lax.all_to_all(maxima.astype(jnp.bfloat16), DP, split_axis=0, concat_axis...  9.79 us
    all_to_all x2, starting transfers between devices, sum_to_owner(): got = lax.all_to_all(pieces, MP, split_axis=0, concat_axis=0, tiled=True)  9.75 us
  transfers between devices with their start and end apart: 8, of which 5 were waited for; matrix products, arithmetic and copies ran while one was open for 17% of the time, Pallas kernels for 0%

profile of v8, /device:TPU:2, one launch (start us, length us, event | category | flops | bytes accessed | tf_op | source)
XLA Modules:
  0.0 216.6 jit_solution(13876795563195261909)
XLA Ops:
  8.0 3.6 %concatenate.9 = bf16[272,128]{1,0:T(8,128)(2,1)S(1)} concatenate(bf16[32,128]{1,0:T(8,128)(2,1)} %param.15, bf16[32,128]{1,0:T(8,128)(2,1)} %param.16, bf16[32,128]{1,0:T(8,128)(2,1)} %param.17, bf16[32,128]{1,0:T(8,128)(2,1)} %bitcast.153, bf16[128,128]{1,0:T(8,128)(2,1)S(1)} %reshape.277, bf16[4,128]{1,0:T(4,128)(2,1)} %param.23, bf16[12,128]{1,0:T(8,128)(2,1)S(1)} %broadcast_in_dim.26), dimensions={0} | concatenate | bytes 139264 | tf_op jit(solution)/shard_map/concatenate | solution.py:31
  11.6 13.5 %all-gather = bf16[1088,128]{1,0:T(8,128)(2,1)} all-gather(bf16[272,128]{1,0:T(8,128)(2,1)S(1)} %concatenate.9), channel_id=2, replica_groups=mesh['y'=4,'z'=8,'x'=4,'c'=2] {'y'}, dimensions={0}, use_global_device_ids=true | all-gather | bytes 348160 | tf_op jit(solution)/shard_map/all_gather | solution.py:32
  29.4 11.0 %all-to-all-start = ((s32[32,1,8]{2,1,0:T(1,128)}), s32[32,1,8]{2,1,0:T(1,128)S(1)}, u32[]{:S(2)}, u32[]{:S(2)}) async-start(s32[32,1,8]{2,1,0:T(1,128)} %bitcast.9), calls=%async_computation | async-start | bytes 32768 | tf_op jit(solution)/shard_map/all_to_all | solution.py:94
  42.0 8.4 %all-to-all-done = s32[32,1,8]{2,1,0:T(1,128)S(1)} async-done(((s32[32,1,8]{2,1,0:T(1,128)}), s32[32,1,8]{2,1,0:T(1,128)S(1)}, u32[]{:S(2)}, u32[]{:S(2)}) %all-to-all-start) | async-done | bytes 1056 | tf_op jit(solution)/shard_map/all_to_all | solution.py:94
  50.4 2.0 broadcast_in_dim.29
  52.4 4.8 %all-to-all-start.1 = ((bf16[8,2,32,1024]{3,2,1,0:T(8,128)(2,1)}), bf16[8,2,32,1024]{3,2,1,0:T(8,128)(2,1)S(1)}, u32[]{:S(2)}, u32[]{:S(2)}) async-start(bf16[8,2,32,1024]{3,2,1,0:T(8,128)(2,1)} %broadcast_in_dim.29), calls=%async_computation.1 | async-start | bytes 2097152 | tf_op jit(solution)/shard_map/all_to_all | solution.py:114
  57.2 13.0 %all-gather.2 = bf16[1024,128]{1,0:T(8,128)(2,1)} all-gather(bf16[256,128]{1,0:T(8,128)(2,1)S(1)} %pad_maximum_fusion.1), channel_id=4, replica_groups=mesh['y'=4,'z'=8,'x'=4,'c'=2] {'y'}, dimensions={0}, use_global_device_ids=true | all-gather | bytes 327680 | tf_op jit(solution)/shard_map/all_gather | solution.py:32
  72.4 2.1 fusion.126
  75.5 1.5 convolution_convert_fusion.4
  86.3 4.8 %all-to-all-start.2 = ((bf16[8,64,1024]{2,1,0:T(8,128)(2,1)}), bf16[8,64,1024]{2,1,0:T(8,128)(2,1)S(1)}, u32[]{:S(2)}, u32[]{:S(2)}) async-start(bf16[8,64,1024]{2,1,0:T(8,128)(2,1)} %bitcast.33), calls=%async_computation.2 | async-start | bytes 2097152 | tf_op jit(solution)/shard_map/all_to_all | solution.py:24
  91.2 1.9 gather_fusion.2
  93.3 11.9 %gather_fusion.1 = bf16[256,128,128]{2,1,0:T(8,128)(2,1)} fusion(bf16[256,128,128]{2,1,0:T(8,128)(2,1)} %param.24, s32[1024]{0:T(1024)S(1)} %pad_clamp_fusion.1), kind=kCustom, calls=%fused_computation.1 | custom fusion | bytes 16778240 | tf_op jit(solution)/shard_map/gather | solution.py:102
  107.1 21.7 %all_to_all.42 = bf16[8,80,1024]{2,1,0:T(8,128)(2,1)S(1)} all-to-all(bf16[8,80,1024]{2,1,0:T(8,128)(2,1)S(1)} %broadcast_in_dim.30), channel_id=1, replica_groups=mesh['y'=4,'z'=8,'x'=4,'c'=2] {'x','c'}, dimensions={0} | all-to-all | bytes 2621440 | tf_op jit(solution)/shard_map/all_to_all | solution.py:150
  128.9 2.2 fusion.127
  132.5 1.5 reshape.298
  134.0 5.6 %convolution_convert_fusion.1 = bf16[512,1024]{1,0:T(8,128)(2,1)} fusion(bf16[1024,512]{1,0:T(8,128)(2,1)} %reshape.298, bf16[512,1024]{1,0:T(8,128)(2,1)S(1)} %bitcast.129, bf16[1024,512]{1,0:T(8,128)(2,1)S(1)} %copy-done.7), kind=kOutput, calls=%fused_computation.18 | convolution fusion | flops 1091305472 | bytes 4194304 | tf_op jit(solution)/shard_map/dot_general | solution.py:158
  139.6 4.9 %all-to-all-start.4 = ((bf16[8,64,1024]{2,1,0:T(8,128)(2,1)}), bf16[8,64,1024]{2,1,0:T(8,128)(2,1)S(1)}, u32[]{:S(2)}, u32[]{:S(2)}) async-start(bf16[8,64,1024]{2,1,0:T(8,128)(2,1)} %bitcast.37), calls=%async_computation.4 | async-start | bytes 2097152 | tf_op jit(solution)/shard_map/all_to_all | solution.py:24
  144.8 14.2 %all-to-all-done.4 = bf16[8,64,1024]{2,1,0:T(8,128)(2,1)S(1)} async-done(((bf16[8,64,1024]{2,1,0:T(8,128)(2,1)}), bf16[8,64,1024]{2,1,0:T(8,128)(2,1)S(1)}, u32[]{:S(2)}, u32[]{:S(2)}) %all-to-all-start.4) | async-done | bytes 1048608 | tf_op jit(solution)/shard_map/all_to_all | solution.py:24
  161.0 6.2 %all-to-all-start.5 = ((bf16[32,2,32,128]{3,2,1,0:T(8,128)(2,1)}), bf16[32,2,32,128]{3,2,1,0:T(8,128)(2,1)S(1)}, u32[]{:S(2)}, u32[]{:S(2)}) async-start(bf16[32,2,32,128]{3,2,1,0:T(8,128)(2,1)} %broadcast_in_dim.33), calls=%async_computation.5 | async-start | bytes 1048576 | tf_op jit(solution)/shard_map/all_to_all | solution.py:169
  167.7 15.9 %all-to-all-done.5 = bf16[32,2,32,128]{3,2,1,0:T(8,128)(2,1)S(1)} async-done(((bf16[32,2,32,128]{3,2,1,0:T(8,128)(2,1)}), bf16[32,2,32,128]{3,2,1,0:T(8,128)(2,1)S(1)}, u32[]{:S(2)}, u32[]{:S(2)}) %all-to-all-start.5) | async-done | bytes 524320 | tf_op jit(solution)/shard_map/all_to_all | solution.py:169
  183.6 6.7 %select_reduce_fusion = bf16[32,8,2,32]{3,2,1,0:T(2,128)(2,1)S(1)} fusion(pred[32,8,128]{2,1,0:T(8,128)(4,1)S(1)} %iota_compare_fusion.1, bf16[32,8,128,128]{3,2,1,0:T(8,128)(2,1)} %bitcast.128, bf16[32,2,32,128]{3,2,1,0:T(8,128)(2,1)S(1)} %all-to-all-done.5), kind=kOutput, calls=%fused_computation.9 | convolution fusion | flops 541048832 | bytes 8978432 | tf_op jit(solution)/shard_map/sqie,snte->snqit/dot_general | solution.py:171
  190.3 1.7 gather_fusion.4
  192.8 5.7 %all-to-all-start.6 = ((bf16[32,2,128]{2,1,0:T(2,128)(2,1)}), bf16[32,2,128]{2,1,0:T(2,128)(2,1)S(1)}, u32[]{:S(2)}, u32[]{:S(2)}) async-start(bf16[32,2,128]{2,1,0:T(2,128)(2,1)} %reshape.377), calls=%async_computation.6 | async-start | bytes 32768 | tf_op jit(solution)/shard_map/all_to_all | solution.py:48
  198.5 9.8 %all-to-all-done.6 = bf16[32,2,128]{2,1,0:T(2,128)(2,1)S(1)} async-done(((bf16[32,2,128]{2,1,0:T(2,128)(2,1)}), bf16[32,2,128]{2,1,0:T(2,128)(2,1)S(1)}, u32[]{:S(2)}, u32[]{:S(2)}) %all-to-all-start.6) | async-done | bytes 16416 | tf_op jit(solution)/shard_map/all_to_all | solution.py:48
  (121 shorter events, 27.3 us)
Async XLA Ops:
  7.2 18.9 %copy-start = (s32[8192]{0:T(1024)S(1)}, s32[8192]{0:T(1024)}, u32[]{:S(2)}) copy-start(s32[8192]{0:T(1024)} %param.26) | copy-start | bytes 98308
  7.2 63.0 %all-gather.7.cloned.1.call-start = ((), (), s32[]{:S(2)}) async-start(), calls=%async_computation.7 | async-start | bytes 2506752 | tf_op jit(solution)/shard_map/all_gather | solution.py:36
  29.4 20.9 %all-to-all-start = ((s32[32,1,8]{2,1,0:T(1,128)}), s32[32,1,8]{2,1,0:T(1,128)S(1)}, u32[]{:S(2)}, u32[]{:S(2)}) async-start(s32[32,1,8]{2,1,0:T(1,128)} %bitcast.9), calls=%async_computation | async-start | bytes 32768 | tf_op jit(solution)/shard_map/all_to_all | solution.py:94
  52.4 24.6 %all-to-all-start.1 = ((bf16[8,2,32,1024]{3,2,1,0:T(8,128)(2,1)}), bf16[8,2,32,1024]{3,2,1,0:T(8,128)(2,1)S(1)}, u32[]{:S(2)}, u32[]{:S(2)}) async-start(bf16[8,2,32,1024]{3,2,1,0:T(8,128)(2,1)} %broadcast_in_dim.29), calls=%async_computation.1 | async-start | bytes 2097152 | tf_op jit(solution)/shard_map/all_to_all | solution.py:114
  57.2 71.7 %all-gather.9.cloned.1.call-start = ((), (), s32[]{:S(2)}) async-start(), calls=%async_computation.8 | async-start | bytes 2359296 | tf_op jit(solution)/shard_map/all_gather | solution.py:36
  75.0 2.0 copy-start.3
  75.5 2.5 %copy-start.9 = (bf16[32,32,128]{2,1,0:T(8,128)(2,1)S(1)}, bf16[32,32,128]{2,1,0:T(8,128)(2,1)}, u32[]{:S(2)}) copy-start(bf16[32,32,128]{2,1,0:T(8,128)(2,1)} %get-tuple-element.16) | copy-start | bytes 786436
  78.6 1.2 copy-start.10
  83.9 1.0 copy-start.8
  84.7 6.5 %copy-start.1 = (s32[256]{0:T(256)S(1)}, s32[256]{0:T(256)}, u32[]{:S(2)}) copy-start(s32[256]{0:T(256)} %param.25) | copy-start | bytes 3076
  86.3 19.3 %all-to-all-start.2 = ((bf16[8,64,1024]{2,1,0:T(8,128)(2,1)}), bf16[8,64,1024]{2,1,0:T(8,128)(2,1)S(1)}, u32[]{:S(2)}, u32[]{:S(2)}) async-start(bf16[8,64,1024]{2,1,0:T(8,128)(2,1)} %bitcast.33), calls=%async_computation.2 | async-start | bytes 2097152 | tf_op jit(solution)/shard_map/all_to_all | solution.py:24
  93.3 12.5 %copy-start.4 = (bf16[2,32,1024]{2,1,0:T(8,128)(2,1)S(1)}, bf16[2,32,1024]{2,1,0:T(8,128)(2,1)}, u32[]{:S(2)}) copy-start(bf16[2,32,1024]{2,1,0:T(8,128)(2,1)} %param.14) | copy-start | bytes 393220
  106.3 0.6 copy-start.5
  128.9 2.2 %copy-start.2 = (bf16[8,80,1024]{2,1,0:T(8,128)(2,1)}, bf16[8,80,1024]{2,1,0:T(8,128)(2,1)S(1)}, u32[]{:S(2)}) copy-start(bf16[8,80,1024]{2,1,0:T(8,128)(2,1)S(1)} %all_to_all.42) | copy-start | bytes 3932164
  131.0 3.0 %slice-start = ((bf16[8,80,1024]{2,1,0:T(8,128)(2,1)}), bf16[8,64,1024]{2,1,0:T(8,128)(2,1)S(1)}, s32[]{:S(2)}) async-start(bf16[8,80,1024]{2,1,0:T(8,128)(2,1)} %copy-done.2), calls=%async_computation.9 | async-start | bytes 2097152 | tf_op jit(solution)/shard_map/slice | solution.py:153
  132.5 1.5 copy-start.7
  139.6 4.9 %slice-start.1 = ((bf16[8,80,1024]{2,1,0:T(8,128)(2,1)}), bf16[8,16,1024]{2,1,0:T(8,128)(2,1)S(1)}, s32[]{:S(2)}) async-start(bf16[8,80,1024]{2,1,0:T(8,128)(2,1)} %copy-done.2), calls=%async_computation.10 | async-start | bytes 524288 | tf_op jit(solution)/shard_map/slice | solution.py:154
  139.6 19.6 %copy-start.6 = (bf16[64,1024]{1,0:T(8,128)(2,1)S(1)}, bf16[64,1024]{1,0:T(8,128)(2,1)}, u32[]{:S(2)}) copy-start(bf16[64,1024]{1,0:T(8,128)(2,1)} %copy-done.5) | copy-start | bytes 393220
  139.6 19.5 %all-to-all-start.4 = ((bf16[8,64,1024]{2,1,0:T(8,128)(2,1)}), bf16[8,64,1024]{2,1,0:T(8,128)(2,1)S(1)}, u32[]{:S(2)}, u32[]{:S(2)}) async-start(bf16[8,64,1024]{2,1,0:T(8,128)(2,1)} %bitcast.37), calls=%async_computation.4 | async-start | bytes 2097152 | tf_op jit(solution)/shard_map/all_to_all | solution.py:24
  160.0 30.2 %copy-start.11 = (bf16[64,128]{1,0:T(8,128)(2,1)}, bf16[64,128]{1,0:T(8,128)(2,1)S(1)}, u32[]{:S(2)}) copy-start(bf16[64,128]{1,0:T(8,128)(2,1)S(1)} %divide_convert_fusion.4) | copy-start | bytes 49156
  161.0 22.5 %all-to-all-start.5 = ((bf16[32,2,32,128]{3,2,1,0:T(8,128)(2,1)}), bf16[32,2,32,128]{3,2,1,0:T(8,128)(2,1)S(1)}, u32[]{:S(2)}, u32[]{:S(2)}) async-start(bf16[32,2,32,128]{3,2,1,0:T(8,128)(2,1)} %broadcast_in_dim.33), calls=%async_computation.5 | async-start | bytes 1048576 | tf_op jit(solution)/shard_map/all_to_all | solution.py:169
  192.8 15.5 %all-to-all-start.6 = ((bf16[32,2,128]{2,1,0:T(2,128)(2,1)}), bf16[32,2,128]{2,1,0:T(2,128)(2,1)S(1)}, u32[]{:S(2)}, u32[]{:S(2)}) async-start(bf16[32,2,128]{2,1,0:T(2,128)(2,1)} %reshape.377), calls=%async_computation.6 | async-start | bytes 32768 | tf_op jit(solution)/shard_map/all_to_all | solution.py:48
Sparse Core Ops, SparseCore 0:
  25.3 43.5 all-gather.6
  78.1 38.4 all-gather.8

commit v9 on v8

--- a/solution.py
+++ b/solution.py
@@ -42,6 +42,19 @@
         parts.append(gathered[:, start : start + n])
         start += n
     return parts
+
+
+def tile_order(piece, sub=8, lanes=128):
+    rows, width = piece.shape
+    tiles = piece.reshape(rows // sub, sub, width // lanes, lanes)
+    return jnp.transpose(tiles, (0, 2, 1, 3)).reshape(-1, lanes)
+
+
+def from_tile_order(gathered, shape, sub=8, lanes=128):
+    rows, width = shape
+    owners = gathered.shape[0]
+    tiles = gathered.reshape(owners, rows // sub, width // lanes, sub, lanes)
+    return jnp.transpose(tiles, (0, 1, 3, 2, 4)).reshape(owners * rows, width)
 
 
 def return_maxima(maxima):
@@ -74,7 +87,7 @@
 
     lanes = query_weight.shape[1]
     first = (query_weight, w_key, w_value, w_out.T, rel_table, w_proj)
-    second = (w_up, w_down.T)
+    second = (tile_order(w_up), tile_order(w_down.T))
     first_y = gather_over_y(first, lanes)
     first_parts = gather_over_z(first, lanes, first_y, page_owners)
     pg_dev = pages.shape[0]
@@ -105,8 +118,8 @@
     wk = g_k.reshape(page_owners * w_key.shape[0], cols)
     wv = g_v.reshape(page_owners * w_value.shape[0], cols)
     wo = g_out.reshape(page_owners * w_out.shape[1], w_out.shape[0]).T
-    wu = g_up.reshape(page_owners * w_up.shape[0], w_up.shape[1])
-    wd = g_down.reshape(page_owners * w_down.shape[1], w_down.shape[0]).T
+    wu = from_tile_order(g_up, w_up.shape)
+    wd = from_tile_order(g_down, (w_down.shape[1], w_down.shape[0])).T
     left_rel = g_rel.reshape(page_owners * rel_table.shape[0], rel_table.shape[1])
     g_proj = g_proj.reshape((page_owners,) + w_proj.shape)
 
@@ -171,7 +184,7 @@
     sim = jnp.einsum("sqie,snte->snqit", recv, chosen, preferred_element_type=jnp.float32)
     valid = token_positions[None, None, None, None, :] < lens[:, :, None, None, None]
     both_best = jnp.max(jnp.where(valid, sim, -1e30), axis=-1)
-    picked = jnp.take_along_axis(both_best, which_query[:, :, None, None], axis=2)[:, :, 0]
+    picked = jnp.where(which_query[:, :, None] == 0, both_best[:, :, 0], both_best[:, :, 1])
     returned = return_maxima(picked)
     best = returned.reshape(page_owners * cap, qlen)[index]
     best = best.reshape(qry_dev, ncand, ppc, qlen)

time: 218 us -> 214 us (0.982)
  blocking collectives: 48.3 us -> 69 us
  starting transfers between devices: 37.5 us -> 26.9 us
  waiting for transfers between devices: 48.7 us -> 40.8 us
  local copies, waits for them, and re-layouts: 42.7 us -> 36.2 us
    all_to_all x0 -> x1, blocking collectives: none -> 20.8 us  [body(): lax.all_to_all(codes.reshape(page_owners, cap), DP, split_axis=0, concat_...]
    all_to_all x1 -> x0, starting transfers between devices: 11 us -> none  [body(): lax.all_to_all(codes.reshape(page_owners, cap), DP, split_axis=0, concat_...]
    all_to_all x1 -> x0, waiting for transfers between devices: 8.37 us -> none  [body(): lax.all_to_all(codes.reshape(page_owners, cap), DP, split_axis=0, concat_...]
    reshape x2 -> x0, local copies, waits for them, and re-layouts: 2.95 us -> none  [the longest x1 1.5 us: body(): wd = g_down.reshape(page_owners * w_down.shape[1], w_down.shape[0]).T]
  transfers between devices with their start and end apart: 8 -> 7, of which waited for: 5 -> 4; matrix products, arithmetic and copies ran while one was open for 17% -> 17% of each run, Pallas kernels for 0% -> 0%
where the time goes in v9:
time: 214 us; the launch traced here: 213 us
  blocking collectives  69 us (32%)
  waiting for transfers between devices  40.8 us (19%)
  local copies, waits for them, and re-layouts  36.2 us (17%)
  starting transfers between devices  26.9 us (13%)
  matrix products  22.3 us (10%)
  between operations  14.6 us (7%)
  other arithmetic  2.84 us (1%)
    all_gather x2, blocking collectives, gather_over_y(): return lax.all_gather(flat_pieces, DP[0], axis=0, tiled=False)  26.5 us
    all_to_all x1, blocking collectives, body(): lax.all_to_all(jnp.broadcast_to(both[None], (n_mp,) + both.shape), MP, sp...  21.7 us
    all_to_all x1, blocking collectives, body(): lax.all_to_all(codes.reshape(page_owners, cap), DP, split_axis=0, concat_...  20.8 us
    all_to_all x1, waiting for transfers between devices, body(): recv = lax.all_to_all(sent, DP, split_axis=0, concat_axis=0, tiled=True)  16.4 us
    all_to_all x2, waiting for transfers between devices, sum_to_owner(): got = lax.all_to_all(pieces, MP, split_axis=0, concat_axis=0, tiled=True)  14.6 us
    gather x1, local copies, waits for them, and re-layouts, body(): chosen = pages[where_local]  11.9 us
    all_to_all x1, waiting for transfers between devices, return_maxima(): lax.all_to_all(maxima.astype(jnp.bfloat16), DP, split_axis=0, concat_axis...  9.79 us
    all_to_all x2, starting transfers between devices, sum_to_owner(): got = lax.all_to_all(pieces, MP, split_axis=0, concat_axis=0, tiled=True)  9.61 us
  transfers between devices with their start and end apart: 7, of which 4 were waited for; matrix products, arithmetic and copies ran while one was open for 17% of the time, Pallas kernels for 0%

profile of v9, /device:TPU:2, one launch (start us, length us, event | category | flops | bytes accessed | tf_op | source)
XLA Modules:
  0.0 212.7 jit_solution(5396452781280631140)
XLA Ops:
  8.0 3.6 %concatenate.9 = bf16[272,128]{1,0:T(8,128)(2,1)S(1)} concatenate(bf16[32,128]{1,0:T(8,128)(2,1)} %param.15, bf16[32,128]{1,0:T(8,128)(2,1)} %param.16, bf16[32,128]{1,0:T(8,128)(2,1)} %param.17, bf16[32,128]{1,0:T(8,128)(2,1)} %bitcast.175, bf16[128,128]{1,0:T(8,128)(2,1)S(1)} %reshape.278, bf16[4,128]{1,0:T(4,128)(2,1)} %param.23, bf16[12,128]{1,0:T(8,128)(2,1)S(1)} %broadcast_in_dim.25), dimensions={0} | concatenate | bytes 139264 | tf_op jit(solution)/shard_map/concatenate | solution.py:31
  11.6 13.5 %all-gather = bf16[1088,128]{1,0:T(8,128)(2,1)} all-gather(bf16[272,128]{1,0:T(8,128)(2,1)S(1)} %concatenate.9), channel_id=2, replica_groups=mesh['y'=4,'z'=8,'x'=4,'c'=2] {'y'}, dimensions={0}, use_global_device_ids=true | all-gather | bytes 348160 | tf_op jit(solution)/shard_map/all_gather | solution.py:32
  28.8 20.8 %all_to_all.42 = s32[32,1,8]{2,1,0:T(1,128)S(1)} all-to-all(s32[32,1,8]{2,1,0:T(1,128)S(1)} %bitcast.172), channel_id=1, replica_groups=mesh['y'=4,'z'=8,'x'=4,'c'=2] {'y','z'}, dimensions={0} | all-to-all | bytes 2048 | tf_op jit(solution)/shard_map/all_to_all | solution.py:107
  49.6 2.0 broadcast_in_dim.28
  51.7 4.8 %all-to-all-start.1 = ((bf16[8,2,32,1024]{3,2,1,0:T(8,128)(2,1)}), bf16[8,2,32,1024]{3,2,1,0:T(8,128)(2,1)S(1)}, u32[]{:S(2)}, u32[]{:S(2)}) async-start(bf16[8,2,32,1024]{3,2,1,0:T(8,128)(2,1)} %broadcast_in_dim.28), calls=%async_computation.1 | async-start | bytes 2097152 | tf_op jit(solution)/shard_map/all_to_all | solution.py:127
  56.5 13.0 %all-gather.2 = bf16[1024,128]{1,0:T(8,128)(2,1)} all-gather(bf16[256,128]{1,0:T(8,128)(2,1)S(1)} %pad_maximum_fusion.1), channel_id=4, replica_groups=mesh['y'=4,'z'=8,'x'=4,'c'=2] {'y'}, dimensions={0}, use_global_device_ids=true | all-gather | bytes 327680 | tf_op jit(solution)/shard_map/all_gather | solution.py:32
  71.7 2.1 fusion.120
  74.8 1.5 convolution_convert_fusion.4
  79.1 1.4 fusion.7
  81.3 1.4 fusion.5
  84.1 1.4 convolution_convert_fusion
  85.6 4.8 %all-to-all-start.2 = ((bf16[8,64,1024]{2,1,0:T(8,128)(2,1)}), bf16[8,64,1024]{2,1,0:T(8,128)(2,1)S(1)}, u32[]{:S(2)}, u32[]{:S(2)}) async-start(bf16[8,64,1024]{2,1,0:T(8,128)(2,1)} %bitcast.39), calls=%async_computation.2 | async-start | bytes 2097152 | tf_op jit(solution)/shard_map/all_to_all | solution.py:24
  90.5 1.9 gather_fusion.2
  92.6 11.9 %gather_fusion.1 = bf16[256,128,128]{2,1,0:T(8,128)(2,1)} fusion(bf16[256,128,128]{2,1,0:T(8,128)(2,1)} %param.24, s32[1024]{0:T(1024)S(1)} %pad_clamp_fusion.1), kind=kCustom, calls=%fused_computation.1 | custom fusion | bytes 16778240 | tf_op jit(solution)/shard_map/gather | solution.py:115
  105.8 21.7 %all_to_all.43 = bf16[8,80,1024]{2,1,0:T(8,128)(2,1)S(1)} all-to-all(bf16[8,80,1024]{2,1,0:T(8,128)(2,1)S(1)} %broadcast_in_dim.29), channel_id=1, replica_groups=mesh['y'=4,'z'=8,'x'=4,'c'=2] {'x','c'}, dimensions={0} | all-to-all | bytes 2621440 | tf_op jit(solution)/shard_map/all_to_all | solution.py:163
  127.6 3.1 %fusion.121 = (bf16[32,128,128]{2,1,0:T(8,128)(2,1)}, bf16[32,128,128]{2,1,0:T(8,128)(2,1)}) fusion(bf16[32,256,128]{2,1,0:T(8,128)(2,1)} %bitcast.148), kind=kLoop, calls=%fused_computation.189 | loop fusion | bytes 4194304 | tf_op jit(solution)/shard_map/slice | solution.py:42
  130.7 6.0 %convolution_convert_fusion.1 = bf16[512,1024]{1,0:T(8,128)(2,1)} fusion(bf16[1024,512]{1,0:T(8,128)(2,1)} %bitcast.159, bf16[512,1024]{1,0:T(8,128)(2,1)S(1)} %bitcast.156, bf16[1024,512]{1,0:T(8,128)(2,1)} %bitcast.158), kind=kOutput, calls=%fused_computation.17 | convolution fusion | flops 1091305472 | bytes 4194304 | tf_op jit(solution)/shard_map/dot_general | solution.py:171
  136.7 4.8 %all-to-all-start.4 = ((bf16[8,64,1024]{2,1,0:T(8,128)(2,1)}), bf16[8,64,1024]{2,1,0:T(8,128)(2,1)S(1)}, u32[]{:S(2)}, u32[]{:S(2)}) async-start(bf16[8,64,1024]{2,1,0:T(8,128)(2,1)} %bitcast.155), calls=%async_computation.4 | async-start | bytes 2097152 | tf_op jit(solution)/shard_map/all_to_all | solution.py:24
  141.8 14.2 %all-to-all-done.4 = bf16[8,64,1024]{2,1,0:T(8,128)(2,1)S(1)} async-done(((bf16[8,64,1024]{2,1,0:T(8,128)(2,1)}), bf16[8,64,1024]{2,1,0:T(8,128)(2,1)S(1)}, u32[]{:S(2)}, u32[]{:S(2)}) %all-to-all-start.4) | async-done | bytes 1048608 | tf_op jit(solution)/shard_map/all_to_all | solution.py:24
  158.0 6.7 %all-to-all-start.5 = ((bf16[32,2,32,128]{3,2,1,0:T(8,128)(2,1)}), bf16[32,2,32,128]{3,2,1,0:T(8,128)(2,1)S(1)}, u32[]{:S(2)}, u32[]{:S(2)}) async-start(bf16[32,2,32,128]{3,2,1,0:T(8,128)(2,1)} %broadcast_in_dim.32), calls=%async_computation.5 | async-start | bytes 1048576 | tf_op jit(solution)/shard_map/all_to_all | solution.py:182
  164.9 16.4 %all-to-all-done.5 = bf16[32,2,32,128]{3,2,1,0:T(8,128)(2,1)S(1)} async-done(((bf16[32,2,32,128]{3,2,1,0:T(8,128)(2,1)}), bf16[32,2,32,128]{3,2,1,0:T(8,128)(2,1)S(1)}, u32[]{:S(2)}, u32[]{:S(2)}) %all-to-all-start.5) | async-done | bytes 524320 | tf_op jit(solution)/shard_map/all_to_all | solution.py:182
  181.3 6.7 %select_reduce_fusion = f32[32,8,2,32]{3,2,1,0:T(2,128)S(1)} fusion(pred[32,8,128]{2,1,0:T(8,128)(4,1)S(1)} %iota_compare_fusion.1, bf16[32,8,128,128]{3,2,1,0:T(8,128)(2,1)} %bitcast.143, bf16[32,2,32,128]{3,2,1,0:T(8,128)(2,1)S(1)} %all-to-all-done.5), kind=kOutput, calls=%fused_computation.8 | convolution fusion | flops 541048832 | bytes 9011200 | tf_op jit(solution)/shard_map/sqie,snte->snqit/dot_general | solution.py:184
  189.0 5.7 %all-to-all-start.6 = ((bf16[32,2,128]{2,1,0:T(2,128)(2,1)}), bf16[32,2,128]{2,1,0:T(2,128)(2,1)S(1)}, u32[]{:S(2)}, u32[]{:S(2)}) async-start(bf16[32,2,128]{2,1,0:T(2,128)(2,1)} %reshape.372), calls=%async_computation.6 | async-start | bytes 32768 | tf_op jit(solution)/shard_map/all_to_all | solution.py:61
  194.6 9.8 %all-to-all-done.6 = bf16[32,2,128]{2,1,0:T(2,128)(2,1)S(1)} async-done(((bf16[32,2,128]{2,1,0:T(2,128)(2,1)}), bf16[32,2,128]{2,1,0:T(2,128)(2,1)S(1)}, u32[]{:S(2)}, u32[]{:S(2)}) %all-to-all-start.6) | async-done | bytes 16416 | tf_op jit(solution)/shard_map/all_to_all | solution.py:61
  (103 shorter events, 18.8 us)
Async XLA Ops:
  7.2 19.0 %copy-start = (s32[8192]{0:T(1024)S(1)}, s32[8192]{0:T(1024)}, u32[]{:S(2)}) copy-start(s32[8192]{0:T(1024)} %param.26) | copy-start | bytes 98308
  7.2 62.3 %all-gather.7.cloned.1.call-start = ((), (), s32[]{:S(2)}) async-start(), calls=%async_computation.7 | async-start | bytes 2506752 | tf_op jit(solution)/shard_map/all_gather | solution.py:36
  25.2 31.3 %copy-start.8 = (bf16[512,32]{0,1:T(8,128)(2,1)S(1)}, bf16[512,32]{0,1:T(8,128)(2,1)}, u32[]{:S(2)}) copy-start(bf16[512,32]{0,1:T(8,128)(2,1)} %param.22) | copy-start | bytes 98308
  25.2 31.3 %copy-start.9 = (bf16[32,512]{1,0:T(8,128)(2,1)S(1)}, bf16[32,512]{1,0:T(8,128)(2,1)}, u32[]{:S(2)}) copy-start(bf16[32,512]{1,0:T(8,128)(2,1)} %param.21) | copy-start | bytes 98308
  51.7 24.6 %all-to-all-start.1 = ((bf16[8,2,32,1024]{3,2,1,0:T(8,128)(2,1)}), bf16[8,2,32,1024]{3,2,1,0:T(8,128)(2,1)S(1)}, u32[]{:S(2)}, u32[]{:S(2)}) async-start(bf16[8,2,32,1024]{3,2,1,0:T(8,128)(2,1)} %broadcast_in_dim.28), calls=%async_computation.1 | async-start | bytes 2097152 | tf_op jit(solution)/shard_map/all_to_all | solution.py:127
  56.5 71.1 %all-gather.9.cloned.1.call-start = ((), (), s32[]{:S(2)}) async-start(), calls=%async_computation.8 | async-start | bytes 2359296 | tf_op jit(solution)/shard_map/all_gather | solution.py:36
  74.3 2.0 copy-start.2
  74.8 2.5 %copy-start.5 = (bf16[32,32,128]{2,1,0:T(8,128)(2,1)S(1)}, bf16[32,32,128]{2,1,0:T(8,128)(2,1)}, u32[]{:S(2)}) copy-start(bf16[32,32,128]{2,1,0:T(8,128)(2,1)} %get-tuple-element.16) | copy-start | bytes 786436
  77.9 1.2 copy-start.6
  83.2 1.0 copy-start.4
  84.0 6.5 %copy-start.1 = (s32[256]{0:T(256)S(1)}, s32[256]{0:T(256)}, u32[]{:S(2)}) copy-start(s32[256]{0:T(256)} %param.25) | copy-start | bytes 3076
  85.6 19.3 %all-to-all-start.2 = ((bf16[8,64,1024]{2,1,0:T(8,128)(2,1)}), bf16[8,64,1024]{2,1,0:T(8,128)(2,1)S(1)}, u32[]{:S(2)}, u32[]{:S(2)}) async-start(bf16[8,64,1024]{2,1,0:T(8,128)(2,1)} %bitcast.39), calls=%async_computation.2 | async-start | bytes 2097152 | tf_op jit(solution)/shard_map/all_to_all | solution.py:24
  92.5 12.5 %copy-start.3 = (bf16[2,32,1024]{2,1,0:T(8,128)(2,1)S(1)}, bf16[2,32,1024]{2,1,0:T(8,128)(2,1)}, u32[]{:S(2)}) copy-start(bf16[2,32,1024]{2,1,0:T(8,128)(2,1)} %param.14) | copy-start | bytes 393220
  136.7 19.3 %all-to-all-start.4 = ((bf16[8,64,1024]{2,1,0:T(8,128)(2,1)}), bf16[8,64,1024]{2,1,0:T(8,128)(2,1)S(1)}, u32[]{:S(2)}, u32[]{:S(2)}) async-start(bf16[8,64,1024]{2,1,0:T(8,128)(2,1)} %bitcast.155), calls=%async_computation.4 | async-start | bytes 2097152 | tf_op jit(solution)/shard_map/all_to_all | solution.py:24
  157.0 30.9 %copy-start.7 = (bf16[64,128]{1,0:T(8,128)(2,1)}, bf16[64,128]{1,0:T(8,128)(2,1)S(1)}, u32[]{:S(2)}) copy-start(bf16[64,128]{1,0:T(8,128)(2,1)S(1)} %divide_convert_fusion.4) | copy-start | bytes 49156
  158.0 23.3 %all-to-all-start.5 = ((bf16[32,2,32,128]{3,2,1,0:T(8,128)(2,1)}), bf16[32,2,32,128]{3,2,1,0:T(8,128)(2,1)S(1)}, u32[]{:S(2)}, u32[]{:S(2)}) async-start(bf16[32,2,32,128]{3,2,1,0:T(8,128)(2,1)} %broadcast_in_dim.32), calls=%async_computation.5 | async-start | bytes 1048576 | tf_op jit(solution)/shard_map/all_to_all | solution.py:182
  189.0 15.5 %all-to-all-start.6 = ((bf16[32,2,128]{2,1,0:T(2,128)(2,1)}), bf16[32,2,128]{2,1,0:T(2,128)(2,1)S(1)}, u32[]{:S(2)}, u32[]{:S(2)}) async-start(bf16[32,2,128]{2,1,0:T(2,128)(2,1)} %reshape.372), calls=%async_computation.6 | async-start | bytes 32768 | tf_op jit(solution)/shard_map/all_to_all | solution.py:61
Sparse Core Ops, SparseCore 0:
  25.3 43.8 all-gather.6
  77.4 39.1 all-gather.8

commit v10 on v9

--- a/solution.py
+++ b/solution.py
@@ -86,7 +86,7 @@
     n_mp = lax.axis_size(MP)
 
     lanes = query_weight.shape[1]
-    first = (query_weight, w_key, w_value, w_out.T, rel_table, w_proj)
+    first = (query_weight, w_key, w_value, w_out.T, tile_order(rel_table), w_proj)
     second = (tile_order(w_up), tile_order(w_down.T))
     first_y = gather_over_y(first, lanes)
     first_parts = gather_over_z(first, lanes, first_y, page_owners)
@@ -120,7 +120,7 @@
     wo = g_out.reshape(page_owners * w_out.shape[1], w_out.shape[0]).T
     wu = from_tile_order(g_up, w_up.shape)
     wd = from_tile_order(g_down, (w_down.shape[1], w_down.shape[0])).T
-    left_rel = g_rel.reshape(page_owners * rel_table.shape[0], rel_table.shape[1])
+    left_rel = from_tile_order(g_rel, rel_table.shape)
     g_proj = g_proj.reshape((page_owners,) + w_proj.shape)
 
     spread = jnp.broadcast_to(hidden[None], (n_mp,) + hidden.shape)

time: 214 us -> 211 us (0.986)
  transfers between devices with their start and end apart: 7 -> 7, of which waited for: 4 -> 4; matrix products, arithmetic and copies ran while one was open for 17% -> 16% of each run, Pallas kernels for 0% -> 0%
where the time goes in v10:
time: 211 us; the launch traced here: 210 us
  blocking collectives  69.2 us (33%)
  waiting for transfers between devices  40.6 us (19%)
  local copies, waits for them, and re-layouts  35.1 us (17%)
  starting transfers between devices  26.7 us (13%)
  matrix products  21.4 us (10%)
  between operations  14.5 us (7%)
  other arithmetic  2.84 us (1%)
    all_gather x2, blocking collectives, gather_over_y(): return lax.all_gather(flat_pieces, DP[0], axis=0, tiled=False)  26.5 us
    all_to_all x1, blocking collectives, body(): lax.all_to_all(jnp.broadcast_to(both[None], (n_mp,) + both.shape), MP, sp...  21.9 us
    all_to_all x1, blocking collectives, body(): lax.all_to_all(codes.reshape(page_owners, cap), DP, split_axis=0, concat_...  20.8 us
    all_to_all x1, waiting for transfers between devices, body(): recv = lax.all_to_all(sent, DP, split_axis=0, concat_axis=0, tiled=True)  16.4 us
    all_to_all x2, waiting for transfers between devices, sum_to_owner(): got = lax.all_to_all(pieces, MP, split_axis=0, concat_axis=0, tiled=True)  14.4 us
    gather x1, local copies, waits for them, and re-layouts, body(): chosen = pages[where_local]  12.1 us
    all_to_all x1, waiting for transfers between devices, return_maxima(): lax.all_to_all(maxima.astype(jnp.bfloat16), DP, split_axis=0, concat_axis...  9.79 us
    all_to_all x2, starting transfers between devices, sum_to_owner(): got = lax.all_to_all(pieces, MP, split_axis=0, concat_axis=0, tiled=True)  9.61 us
  transfers between devices with their start and end apart: 7, of which 4 were waited for; matrix products, arithmetic and copies ran while one was open for 16% of the time, Pallas kernels for 0%

profile of v10, /device:TPU:2, one launch (start us, length us, event | category | flops | bytes accessed | tf_op | source)
XLA Modules:
  0.0 210.3 jit_solution(3425976386107217794)
XLA Ops:
  7.2 4.3 %concatenate.9 = bf16[272,128]{1,0:T(8,128)(2,1)S(1)} concatenate(bf16[32,128]{1,0:T(8,128)(2,1)} %param.15, bf16[32,128]{1,0:T(8,128)(2,1)} %param.16, bf16[32,128]{1,0:T(8,128)(2,1)} %param.17, bf16[32,128]{1,0:T(8,128)(2,1)} %bitcast.188, bf16[128,128]{1,0:T(8,128)(2,1)} %bitcast.185, bf16[4,128]{1,0:T(4,128)(2,1)} %param.23, bf16[12,128]{1,0:T(8,128)(2,1)S(1)} %broadcast_in_dim.25), dimensions={0} | concatenate | bytes 139264 | tf_op jit(solution)/shard_map/concatenate | solution.py:31
  11.6 13.5 %all-gather = bf16[1088,128]{1,0:T(8,128)(2,1)} all-gather(bf16[272,128]{1,0:T(8,128)(2,1)S(1)} %concatenate.9), channel_id=2, replica_groups=mesh['y'=4,'z'=8,'x'=4,'c'=2] {'y'}, dimensions={0}, use_global_device_ids=true | all-gather | bytes 348160 | tf_op jit(solution)/shard_map/all_gather | solution.py:32
  28.8 20.8 %all_to_all.42 = s32[32,1,8]{2,1,0:T(1,128)S(1)} all-to-all(s32[32,1,8]{2,1,0:T(1,128)S(1)} %bitcast.184), channel_id=1, replica_groups=mesh['y'=4,'z'=8,'x'=4,'c'=2] {'y','z'}, dimensions={0} | all-to-all | bytes 2048 | tf_op jit(solution)/shard_map/all_to_all | solution.py:107
  49.6 2.0 broadcast_in_dim.28
  51.6 4.8 %all-to-all-start.1 = ((bf16[8,2,32,1024]{3,2,1,0:T(8,128)(2,1)}), bf16[8,2,32,1024]{3,2,1,0:T(8,128)(2,1)S(1)}, u32[]{:S(2)}, u32[]{:S(2)}) async-start(bf16[8,2,32,1024]{3,2,1,0:T(8,128)(2,1)} %broadcast_in_dim.28), calls=%async_computation.1 | async-start | bytes 2097152 | tf_op jit(solution)/shard_map/all_to_all | solution.py:127
  56.5 13.0 %all-gather.2 = bf16[1024,128]{1,0:T(8,128)(2,1)} all-gather(bf16[256,128]{1,0:T(8,128)(2,1)S(1)} %pad_maximum_fusion.1), channel_id=4, replica_groups=mesh['y'=4,'z'=8,'x'=4,'c'=2] {'y'}, dimensions={0}, use_global_device_ids=true | all-gather | bytes 327680 | tf_op jit(solution)/shard_map/all_gather | solution.py:32
  70.3 1.3 slice.60
  71.7 1.3 fusion.120
  76.7 1.4 fusion.7
  78.9 1.4 fusion.5
  81.7 1.4 convolution_convert_fusion
  83.2 4.8 %all-to-all-start.2 = ((bf16[8,64,1024]{2,1,0:T(8,128)(2,1)}), bf16[8,64,1024]{2,1,0:T(8,128)(2,1)S(1)}, u32[]{:S(2)}, u32[]{:S(2)}) async-start(bf16[8,64,1024]{2,1,0:T(8,128)(2,1)} %bitcast.47), calls=%async_computation.2 | async-start | bytes 2097152 | tf_op jit(solution)/shard_map/all_to_all | solution.py:24
  88.1 1.9 gather_fusion.2
  90.2 12.1 %gather_fusion.1 = bf16[256,128,128]{2,1,0:T(8,128)(2,1)} fusion(bf16[256,128,128]{2,1,0:T(8,128)(2,1)} %param.24, s32[1024]{0:T(1024)S(1)} %pad_clamp_fusion.1), kind=kCustom, calls=%fused_computation.1 | custom fusion | bytes 16778240 | tf_op jit(solution)/shard_map/gather | solution.py:115
  103.4 21.9 %all_to_all.43 = bf16[8,80,1024]{2,1,0:T(8,128)(2,1)S(1)} all-to-all(bf16[8,80,1024]{2,1,0:T(8,128)(2,1)S(1)} %broadcast_in_dim.29), channel_id=1, replica_groups=mesh['y'=4,'z'=8,'x'=4,'c'=2] {'x','c'}, dimensions={0} | all-to-all | bytes 2621440 | tf_op jit(solution)/shard_map/all_to_all | solution.py:163
  125.4 3.1 %fusion.121 = (bf16[32,128,128]{2,1,0:T(8,128)(2,1)}, bf16[32,128,128]{2,1,0:T(8,128)(2,1)}) fusion(bf16[32,256,128]{2,1,0:T(8,128)(2,1)} %bitcast.160), kind=kLoop, calls=%fused_computation.189 | loop fusion | bytes 4194304 | tf_op jit(solution)/shard_map/slice | solution.py:42
  128.5 6.0 %convolution_convert_fusion.1 = bf16[512,1024]{1,0:T(8,128)(2,1)} fusion(bf16[1024,512]{1,0:T(8,128)(2,1)} %bitcast.171, bf16[512,1024]{1,0:T(8,128)(2,1)S(1)} %bitcast.168, bf16[1024,512]{1,0:T(8,128)(2,1)} %bitcast.170), kind=kOutput, calls=%fused_computation.17 | convolution fusion | flops 1091305472 | bytes 4194304 | tf_op jit(solution)/shard_map/dot_general | solution.py:171
  134.5 4.8 %all-to-all-start.4 = ((bf16[8,64,1024]{2,1,0:T(8,128)(2,1)}), bf16[8,64,1024]{2,1,0:T(8,128)(2,1)S(1)}, u32[]{:S(2)}, u32[]{:S(2)}) async-start(bf16[8,64,1024]{2,1,0:T(8,128)(2,1)} %bitcast.167), calls=%async_computation.4 | async-start | bytes 2097152 | tf_op jit(solution)/shard_map/all_to_all | solution.py:24
  139.6 14.2 %all-to-all-done.4 = bf16[8,64,1024]{2,1,0:T(8,128)(2,1)S(1)} async-done(((bf16[8,64,1024]{2,1,0:T(8,128)(2,1)}), bf16[8,64,1024]{2,1,0:T(8,128)(2,1)S(1)}, u32[]{:S(2)}, u32[]{:S(2)}) %all-to-all-start.4) | async-done | bytes 1048608 | tf_op jit(solution)/shard_map/all_to_all | solution.py:24
  155.8 6.5 %all-to-all-start.5 = ((bf16[32,2,32,128]{3,2,1,0:T(8,128)(2,1)}), bf16[32,2,32,128]{3,2,1,0:T(8,128)(2,1)S(1)}, u32[]{:S(2)}, u32[]{:S(2)}) async-start(bf16[32,2,32,128]{3,2,1,0:T(8,128)(2,1)} %broadcast_in_dim.32), calls=%async_computation.5 | async-start | bytes 1048576 | tf_op jit(solution)/shard_map/all_to_all | solution.py:182
  162.5 16.4 %all-to-all-done.5 = bf16[32,2,32,128]{3,2,1,0:T(8,128)(2,1)S(1)} async-done(((bf16[32,2,32,128]{3,2,1,0:T(8,128)(2,1)}), bf16[32,2,32,128]{3,2,1,0:T(8,128)(2,1)S(1)}, u32[]{:S(2)}, u32[]{:S(2)}) %all-to-all-start.5) | async-done | bytes 524320 | tf_op jit(solution)/shard_map/all_to_all | solution.py:182
  178.9 6.7 %select_reduce_fusion = f32[32,8,2,32]{3,2,1,0:T(2,128)S(1)} fusion(pred[32,8,128]{2,1,0:T(8,128)(4,1)S(1)} %iota_compare_fusion.1, bf16[32,8,128,128]{3,2,1,0:T(8,128)(2,1)} %bitcast.155, bf16[32,2,32,128]{3,2,1,0:T(8,128)(2,1)S(1)} %all-to-all-done.5), kind=kOutput, calls=%fused_computation.8 | convolution fusion | flops 541048832 | bytes 9011200 | tf_op jit(solution)/shard_map/sqie,snte->snqit/dot_general | solution.py:184
  186.6 5.7 %all-to-all-start.6 = ((bf16[32,2,128]{2,1,0:T(2,128)(2,1)}), bf16[32,2,128]{2,1,0:T(2,128)(2,1)S(1)}, u32[]{:S(2)}, u32[]{:S(2)}) async-start(bf16[32,2,128]{2,1,0:T(2,128)(2,1)} %reshape.380), calls=%async_computation.6 | async-start | bytes 32768 | tf_op jit(solution)/shard_map/all_to_all | solution.py:61
  192.2 9.8 %all-to-all-done.6 = bf16[32,2,128]{2,1,0:T(2,128)(2,1)S(1)} async-done(((bf16[32,2,128]{2,1,0:T(2,128)(2,1)}), bf16[32,2,128]{2,1,0:T(2,128)(2,1)S(1)}, u32[]{:S(2)}, u32[]{:S(2)}) %all-to-all-start.6) | async-done | bytes 16416 | tf_op jit(solution)/shard_map/all_to_all | solution.py:61
  (95 shorter events, 16.5 us)
Async XLA Ops:
  7.2 18.9 %copy-start = (s32[8192]{0:T(1024)S(1)}, s32[8192]{0:T(1024)}, u32[]{:S(2)}) copy-start(s32[8192]{0:T(1024)} %param.26) | copy-start | bytes 98308
  7.2 62.3 %all-gather.7.cloned.1.call-start = ((), (), s32[]{:S(2)}) async-start(), calls=%async_computation.7 | async-start | bytes 2506752 | tf_op jit(solution)/shard_map/all_gather | solution.py:36
  25.2 31.3 %copy-start.5 = (bf16[512,32]{0,1:T(8,128)(2,1)S(1)}, bf16[512,32]{0,1:T(8,128)(2,1)}, u32[]{:S(2)}) copy-start(bf16[512,32]{0,1:T(8,128)(2,1)} %param.22) | copy-start | bytes 98308
  25.2 31.3 %copy-start.6 = (bf16[32,512]{1,0:T(8,128)(2,1)S(1)}, bf16[32,512]{1,0:T(8,128)(2,1)}, u32[]{:S(2)}) copy-start(bf16[32,512]{1,0:T(8,128)(2,1)} %param.21) | copy-start | bytes 98308
  51.6 22.3 %all-to-all-start.1 = ((bf16[8,2,32,1024]{3,2,1,0:T(8,128)(2,1)}), bf16[8,2,32,1024]{3,2,1,0:T(8,128)(2,1)S(1)}, u32[]{:S(2)}, u32[]{:S(2)}) async-start(bf16[8,2,32,1024]{3,2,1,0:T(8,128)(2,1)} %broadcast_in_dim.28), calls=%async_computation.1 | async-start | bytes 2097152 | tf_op jit(solution)/shard_map/all_to_all | solution.py:127
  56.5 69.0 %all-gather.9.cloned.1.call-start = ((), (), s32[]{:S(2)}) async-start(), calls=%async_computation.8 | async-start | bytes 2359296 | tf_op jit(solution)/shard_map/all_gather | solution.py:36
  75.6 1.2 copy-start.3
  81.6 6.5 %copy-start.1 = (s32[256]{0:T(256)S(1)}, s32[256]{0:T(256)}, u32[]{:S(2)}) copy-start(s32[256]{0:T(256)} %param.25) | copy-start | bytes 3076
  83.2 19.3 %all-to-all-start.2 = ((bf16[8,64,1024]{2,1,0:T(8,128)(2,1)}), bf16[8,64,1024]{2,1,0:T(8,128)(2,1)S(1)}, u32[]{:S(2)}, u32[]{:S(2)}) async-start(bf16[8,64,1024]{2,1,0:T(8,128)(2,1)} %bitcast.47), calls=%async_computation.2 | async-start | bytes 2097152 | tf_op jit(solution)/shard_map/all_to_all | solution.py:24
  90.2 12.5 %copy-start.2 = (bf16[2,32,1024]{2,1,0:T(8,128)(2,1)S(1)}, bf16[2,32,1024]{2,1,0:T(8,128)(2,1)}, u32[]{:S(2)}) copy-start(bf16[2,32,1024]{2,1,0:T(8,128)(2,1)} %param.14) | copy-start | bytes 393220
  134.5 19.3 %all-to-all-start.4 = ((bf16[8,64,1024]{2,1,0:T(8,128)(2,1)}), bf16[8,64,1024]{2,1,0:T(8,128)(2,1)S(1)}, u32[]{:S(2)}, u32[]{:S(2)}) async-start(bf16[8,64,1024]{2,1,0:T(8,128)(2,1)} %bitcast.167), calls=%async_computation.4 | async-start | bytes 2097152 | tf_op jit(solution)/shard_map/all_to_all | solution.py:24
  154.8 30.7 %copy-start.4 = (bf16[64,128]{1,0:T(8,128)(2,1)}, bf16[64,128]{1,0:T(8,128)(2,1)S(1)}, u32[]{:S(2)}) copy-start(bf16[64,128]{1,0:T(8,128)(2,1)S(1)} %divide_convert_fusion.4) | copy-start | bytes 49156
  155.8 23.1 %all-to-all-start.5 = ((bf16[32,2,32,128]{3,2,1,0:T(8,128)(2,1)}), bf16[32,2,32,128]{3,2,1,0:T(8,128)(2,1)S(1)}, u32[]{:S(2)}, u32[]{:S(2)}) async-start(bf16[32,2,32,128]{3,2,1,0:T(8,128)(2,1)} %broadcast_in_dim.32), calls=%async_computation.5 | async-start | bytes 1048576 | tf_op jit(solution)/shard_map/all_to_all | solution.py:182
  186.6 15.5 %all-to-all-start.6 = ((bf16[32,2,128]{2,1,0:T(2,128)(2,1)}), bf16[32,2,128]{2,1,0:T(2,128)(2,1)S(1)}, u32[]{:S(2)}, u32[]{:S(2)}) async-start(bf16[32,2,128]{2,1,0:T(2,128)(2,1)} %reshape.380), calls=%async_computation.6 | async-start | bytes 32768 | tf_op jit(solution)/shard_map/all_to_all | solution.py:61
Sparse Core Ops, SparseCore 0:
  25.3 43.8 all-gather.6
  75.1 39.1 all-gather.8

commit v11 on v10

--- a/solution.py
+++ b/solution.py
@@ -105,13 +105,15 @@
     index = dest * cap + place
     codes = jnp.zeros((page_owners * cap,), jnp.int32).at[index].set(query_of * pg_dev + local)
     got = lax.all_to_all(codes.reshape(page_owners, cap), DP, split_axis=0, concat_axis=0, tiled=True)
-    second_y = gather_over_y(second, lanes)
+    second_y = lax.all_gather(jnp.stack(second), DP[0], axis=1, tiled=False)
     first_parts, second_y, got = lax.optimization_barrier((first_parts, second_y, got))
     where_local = got % pg_dev
     which_query = got // pg_dev
 
     g_q, g_k, g_v, g_out, g_rel, g_proj = first_parts
-    g_up, g_down = gather_over_z(second, lanes, second_y, page_owners)
+    second_all = lax.all_gather(second_y, DP[1], axis=2, tiled=False)
+    second_all = second_all.reshape((len(second), page_owners) + second[0].shape)
+    g_up, g_down = second_all[0], second_all[1]
     chosen = pages[where_local]
     lens = page_len[where_local]
     wq = g_q.reshape(page_owners * query_weight.shape[0], cols)

time: 211 us -> 211 us (level)
    all_gather x2 -> x1, blocking collectives: 26.5 us -> 13.5 us  [gather_over_y(): return lax.all_gather(flat_pieces, DP[0], axis=0, tiled=False)]
    all_gather x0 -> x1, blocking collectives: none -> 13 us  [body(): second_y = lax.all_gather(jnp.stack(second), DP[0], axis=1, tiled=False)]
    slice x4 -> x3, local copies, waits for them, and re-layouts: 6.53 us -> 3.43 us  [gather_over_z(): parts.append(gathered[:, start:start + n])]
    slice x0 -> x1, local copies, waits for them, and re-layouts: none -> 2.99 us  [body(): g_up, g_down = (second_all[0], second_all[1])]
where the time goes in v11:
time: 211 us; the launch traced here: 210 us
  blocking collectives  69.1 us (33%)
  waiting for transfers between devices  40.8 us (19%)
  local copies, waits for them, and re-layouts  34.8 us (16%)
  starting transfers between devices  26.9 us (13%)
  matrix products  21.4 us (10%)
  between operations  14.5 us (7%)
  other arithmetic  2.84 us (1%)
    all_to_all x1, blocking collectives, body(): lax.all_to_all(jnp.broadcast_to(both[None], (n_mp,) + both.shape), MP, sp...  21.7 us
    all_to_all x1, blocking collectives, body(): lax.all_to_all(codes.reshape(page_owners, cap), DP, split_axis=0, concat_...  20.8 us
    all_to_all x1, waiting for transfers between devices, body(): recv = lax.all_to_all(sent, DP, split_axis=0, concat_axis=0, tiled=True)  16.4 us
    all_to_all x2, waiting for transfers between devices, sum_to_owner(): got = lax.all_to_all(pieces, MP, split_axis=0, concat_axis=0, tiled=True)  14.5 us
    all_gather x1, blocking collectives, gather_over_y(): return lax.all_gather(flat_pieces, DP[0], axis=0, tiled=False)  13.5 us
    all_gather x1, blocking collectives, body(): second_y = lax.all_gather(jnp.stack(second), DP[0], axis=1, tiled=False)  13 us
    gather x1, local copies, waits for them, and re-layouts, body(): chosen = pages[where_local]  11.9 us
    all_to_all x1, waiting for transfers between devices, return_maxima(): lax.all_to_all(maxima.astype(jnp.bfloat16), DP, split_axis=0, concat_axis...  9.79 us
  transfers between devices with their start and end apart: 7, of which 4 were waited for; matrix products, arithmetic and copies ran while one was open for 16% of the time, Pallas kernels for 0%

profile of v11, /device:TPU:2, one launch (start us, length us, event | category | flops | bytes accessed | tf_op | source)
XLA Modules:
  0.0 210.2 jit_solution(6578791327720365368)
XLA Ops:
  7.2 4.3 %concatenate.6 = bf16[272,128]{1,0:T(8,128)(2,1)S(1)} concatenate(bf16[32,128]{1,0:T(8,128)(2,1)} %param.15, bf16[32,128]{1,0:T(8,128)(2,1)} %param.16, bf16[32,128]{1,0:T(8,128)(2,1)} %param.17, bf16[32,128]{1,0:T(8,128)(2,1)} %bitcast.186, bf16[128,128]{1,0:T(8,128)(2,1)} %bitcast.183, bf16[4,128]{1,0:T(4,128)(2,1)} %param.23, bf16[12,128]{1,0:T(8,128)(2,1)S(1)} %broadcast_in_dim.25), dimensions={0} | concatenate | bytes 139264 | tf_op jit(solution)/shard_map/concatenate | solution.py:31
  11.6 13.5 %all-gather = bf16[1088,128]{1,0:T(8,128)(2,1)} all-gather(bf16[272,128]{1,0:T(8,128)(2,1)S(1)} %concatenate.6), channel_id=2, replica_groups=mesh['y'=4,'z'=8,'x'=4,'c'=2] {'y'}, dimensions={0}, use_global_device_ids=true | all-gather | bytes 348160 | tf_op jit(solution)/shard_map/all_gather | solution.py:32
  28.8 20.8 %all_to_all.42 = s32[32,1,8]{2,1,0:T(1,128)S(1)} all-to-all(s32[32,1,8]{2,1,0:T(1,128)S(1)} %bitcast.182), channel_id=1, replica_groups=mesh['y'=4,'z'=8,'x'=4,'c'=2] {'y','z'}, dimensions={0} | all-to-all | bytes 2048 | tf_op jit(solution)/shard_map/all_to_all | solution.py:107
  49.6 2.0 broadcast_in_dim.28
  51.6 4.8 %all-to-all-start.1 = ((bf16[8,2,32,1024]{3,2,1,0:T(8,128)(2,1)}), bf16[8,2,32,1024]{3,2,1,0:T(8,128)(2,1)S(1)}, u32[]{:S(2)}, u32[]{:S(2)}) async-start(bf16[8,2,32,1024]{3,2,1,0:T(8,128)(2,1)} %broadcast_in_dim.28), calls=%async_computation.1 | async-start | bytes 2097152 | tf_op jit(solution)/shard_map/all_to_all | solution.py:129
  56.5 13.0 %all-gather.2 = bf16[2,512,128]{2,1,0:T(8,128)(2,1)} all-gather(bf16[2,128,128]{2,1,0:T(8,128)(2,1)S(1)} %pad_maximum_fusion.1), channel_id=4, replica_groups=mesh['y'=4,'z'=8,'x'=4,'c'=2] {'y'}, dimensions={1}, use_global_device_ids=true | all-gather | bytes 327680 | tf_op jit(solution)/shard_map/all_gather | solution.py:108
  70.3 1.3 slice.64
  71.7 1.3 fusion.120
  76.7 1.4 fusion.7
  78.9 1.4 fusion.5
  81.7 1.4 convolution_convert_fusion
  83.2 4.8 %all-to-all-start.2 = ((bf16[8,64,1024]{2,1,0:T(8,128)(2,1)}), bf16[8,64,1024]{2,1,0:T(8,128)(2,1)S(1)}, u32[]{:S(2)}, u32[]{:S(2)}) async-start(bf16[8,64,1024]{2,1,0:T(8,128)(2,1)} %bitcast.47), calls=%async_computation.2 | async-start | bytes 2097152 | tf_op jit(solution)/shard_map/all_to_all | solution.py:24
  88.1 1.9 gather_fusion.2
  90.2 11.9 %gather_fusion.1 = bf16[256,128,128]{2,1,0:T(8,128)(2,1)} fusion(bf16[256,128,128]{2,1,0:T(8,128)(2,1)} %param.24, s32[1024]{0:T(1024)S(1)} %pad_clamp_fusion.1), kind=kCustom, calls=%fused_computation.1 | custom fusion | bytes 16778240 | tf_op jit(solution)/shard_map/gather | solution.py:117
  103.4 21.7 %all_to_all.43 = bf16[8,80,1024]{2,1,0:T(8,128)(2,1)S(1)} all-to-all(bf16[8,80,1024]{2,1,0:T(8,128)(2,1)S(1)} %broadcast_in_dim.29), channel_id=1, replica_groups=mesh['y'=4,'z'=8,'x'=4,'c'=2] {'x','c'}, dimensions={0} | all-to-all | bytes 2621440 | tf_op jit(solution)/shard_map/all_to_all | solution.py:165
  125.2 3.0 %fusion.121 = (bf16[1,4,1024,128]{3,2,1,0:T(8,128)(2,1)}, bf16[1,4,1024,128]{3,2,1,0:T(8,128)(2,1)}) fusion(bf16[2,4,1024,128]{3,2,1,0:T(8,128)(2,1)} %all-gather.9.cloned.1.call-done), kind=kLoop, calls=%fused_computation.189 | loop fusion | bytes 4194304 | tf_op jit(solution)/shard_map/slice | solution.py:116
  128.2 6.0 %convolution_convert_fusion.1 = bf16[512,1024]{1,0:T(8,128)(2,1)} fusion(bf16[1024,512]{1,0:T(8,128)(2,1)} %bitcast.169, bf16[512,1024]{1,0:T(8,128)(2,1)S(1)} %bitcast.166, bf16[1024,512]{1,0:T(8,128)(2,1)} %bitcast.168), kind=kOutput, calls=%fused_computation.17 | convolution fusion | flops 1091305472 | bytes 4194304 | tf_op jit(solution)/shard_map/dot_general | solution.py:173
  134.2 4.8 %all-to-all-start.4 = ((bf16[8,64,1024]{2,1,0:T(8,128)(2,1)}), bf16[8,64,1024]{2,1,0:T(8,128)(2,1)S(1)}, u32[]{:S(2)}, u32[]{:S(2)}) async-start(bf16[8,64,1024]{2,1,0:T(8,128)(2,1)} %bitcast.165), calls=%async_computation.4 | async-start | bytes 2097152 | tf_op jit(solution)/shard_map/all_to_all | solution.py:24
  139.3 14.2 %all-to-all-done.4 = bf16[8,64,1024]{2,1,0:T(8,128)(2,1)S(1)} async-done(((bf16[8,64,1024]{2,1,0:T(8,128)(2,1)}), bf16[8,64,1024]{2,1,0:T(8,128)(2,1)S(1)}, u32[]{:S(2)}, u32[]{:S(2)}) %all-to-all-start.4) | async-done | bytes 1048608 | tf_op jit(solution)/shard_map/all_to_all | solution.py:24
  155.5 6.7 %all-to-all-start.5 = ((bf16[32,2,32,128]{3,2,1,0:T(8,128)(2,1)}), bf16[32,2,32,128]{3,2,1,0:T(8,128)(2,1)S(1)}, u32[]{:S(2)}, u32[]{:S(2)}) async-start(bf16[32,2,32,128]{3,2,1,0:T(8,128)(2,1)} %broadcast_in_dim.32), calls=%async_computation.5 | async-start | bytes 1048576 | tf_op jit(solution)/shard_map/all_to_all | solution.py:184
  162.4 16.4 %all-to-all-done.5 = bf16[32,2,32,128]{3,2,1,0:T(8,128)(2,1)S(1)} async-done(((bf16[32,2,32,128]{3,2,1,0:T(8,128)(2,1)}), bf16[32,2,32,128]{3,2,1,0:T(8,128)(2,1)S(1)}, u32[]{:S(2)}, u32[]{:S(2)}) %all-to-all-start.5) | async-done | bytes 524320 | tf_op jit(solution)/shard_map/all_to_all | solution.py:184
  178.8 6.7 %select_reduce_fusion = f32[32,8,2,32]{3,2,1,0:T(2,128)S(1)} fusion(pred[32,8,128]{2,1,0:T(8,128)(4,1)S(1)} %iota_compare_fusion.1, bf16[32,8,128,128]{3,2,1,0:T(8,128)(2,1)} %bitcast.154, bf16[32,2,32,128]{3,2,1,0:T(8,128)(2,1)S(1)} %all-to-all-done.5), kind=kOutput, calls=%fused_computation.8 | convolution fusion | flops 541048832 | bytes 9011200 | tf_op jit(solution)/shard_map/sqie,snte->snqit/dot_general | solution.py:186
  186.5 5.7 %all-to-all-start.6 = ((bf16[32,2,128]{2,1,0:T(2,128)(2,1)}), bf16[32,2,128]{2,1,0:T(2,128)(2,1)S(1)}, u32[]{:S(2)}, u32[]{:S(2)}) async-start(bf16[32,2,128]{2,1,0:T(2,128)(2,1)} %reshape.368), calls=%async_computation.6 | async-start | bytes 32768 | tf_op jit(solution)/shard_map/all_to_all | solution.py:61
  192.1 9.8 %all-to-all-done.6 = bf16[32,2,128]{2,1,0:T(2,128)(2,1)S(1)} async-done(((bf16[32,2,128]{2,1,0:T(2,128)(2,1)}), bf16[32,2,128]{2,1,0:T(2,128)(2,1)S(1)}, u32[]{:S(2)}, u32[]{:S(2)}) %all-to-all-start.6) | async-done | bytes 16416 | tf_op jit(solution)/shard_map/all_to_all | solution.py:61
  (95 shorter events, 16.7 us)
Async XLA Ops:
  7.2 18.9 %copy-start = (s32[8192]{0:T(1024)S(1)}, s32[8192]{0:T(1024)}, u32[]{:S(2)}) copy-start(s32[8192]{0:T(1024)} %param.26) | copy-start | bytes 98308
  7.2 62.3 %all-gather.7.cloned.1.call-start = ((), (), s32[]{:S(2)}) async-start(), calls=%async_computation.7 | async-start | bytes 2506752 | tf_op jit(solution)/shard_map/all_gather | solution.py:36
  25.2 31.3 %copy-start.5 = (bf16[512,32]{0,1:T(8,128)(2,1)S(1)}, bf16[512,32]{0,1:T(8,128)(2,1)}, u32[]{:S(2)}) copy-start(bf16[512,32]{0,1:T(8,128)(2,1)} %param.22) | copy-start | bytes 98308
  25.2 31.3 %copy-start.6 = (bf16[32,512]{1,0:T(8,128)(2,1)S(1)}, bf16[32,512]{1,0:T(8,128)(2,1)}, u32[]{:S(2)}) copy-start(bf16[32,512]{1,0:T(8,128)(2,1)} %param.21) | copy-start | bytes 98308
  51.6 22.3 %all-to-all-start.1 = ((bf16[8,2,32,1024]{3,2,1,0:T(8,128)(2,1)}), bf16[8,2,32,1024]{3,2,1,0:T(8,128)(2,1)S(1)}, u32[]{:S(2)}, u32[]{:S(2)}) async-start(bf16[8,2,32,1024]{3,2,1,0:T(8,128)(2,1)} %broadcast_in_dim.28), calls=%async_computation.1 | async-start | bytes 2097152 | tf_op jit(solution)/shard_map/all_to_all | solution.py:129
  56.5 68.8 %all-gather.9.cloned.1.call-start = ((), (), s32[]{:S(2)}) async-start(), calls=%async_computation.8 | async-start | bytes 2359296 | tf_op jit(solution)/shard_map/all_gather | solution.py:114
  75.6 1.2 copy-start.3
  81.6 6.5 %copy-start.1 = (s32[256]{0:T(256)S(1)}, s32[256]{0:T(256)}, u32[]{:S(2)}) copy-start(s32[256]{0:T(256)} %param.25) | copy-start | bytes 3076
  83.2 19.3 %all-to-all-start.2 = ((bf16[8,64,1024]{2,1,0:T(8,128)(2,1)}), bf16[8,64,1024]{2,1,0:T(8,128)(2,1)S(1)}, u32[]{:S(2)}, u32[]{:S(2)}) async-start(bf16[8,64,1024]{2,1,0:T(8,128)(2,1)} %bitcast.47), calls=%async_computation.2 | async-start | bytes 2097152 | tf_op jit(solution)/shard_map/all_to_all | solution.py:24
  90.2 12.5 %copy-start.2 = (bf16[2,32,1024]{2,1,0:T(8,128)(2,1)S(1)}, bf16[2,32,1024]{2,1,0:T(8,128)(2,1)}, u32[]{:S(2)}) copy-start(bf16[2,32,1024]{2,1,0:T(8,128)(2,1)} %param.14) | copy-start | bytes 393220
  134.2 19.3 %all-to-all-start.4 = ((bf16[8,64,1024]{2,1,0:T(8,128)(2,1)}), bf16[8,64,1024]{2,1,0:T(8,128)(2,1)S(1)}, u32[]{:S(2)}, u32[]{:S(2)}) async-start(bf16[8,64,1024]{2,1,0:T(8,128)(2,1)} %bitcast.165), calls=%async_computation.4 | async-start | bytes 2097152 | tf_op jit(solution)/shard_map/all_to_all | solution.py:24
  154.5 30.9 %copy-start.4 = (bf16[64,128]{1,0:T(8,128)(2,1)}, bf16[64,128]{1,0:T(8,128)(2,1)S(1)}, u32[]{:S(2)}) copy-start(bf16[64,128]{1,0:T(8,128)(2,1)S(1)} %divide_convert_fusion.4) | copy-start | bytes 49156
  155.5 23.3 %all-to-all-start.5 = ((bf16[32,2,32,128]{3,2,1,0:T(8,128)(2,1)}), bf16[32,2,32,128]{3,2,1,0:T(8,128)(2,1)S(1)}, u32[]{:S(2)}, u32[]{:S(2)}) async-start(bf16[32,2,32,128]{3,2,1,0:T(8,128)(2,1)} %broadcast_in_dim.32), calls=%async_computation.5 | async-start | bytes 1048576 | tf_op jit(solution)/shard_map/all_to_all | solution.py:184
  186.5 15.5 %all-to-all-start.6 = ((bf16[32,2,128]{2,1,0:T(2,128)(2,1)}), bf16[32,2,128]{2,1,0:T(2,128)(2,1)S(1)}, u32[]{:S(2)}, u32[]{:S(2)}) async-start(bf16[32,2,128]{2,1,0:T(2,128)(2,1)} %reshape.368), calls=%async_computation.6 | async-start | bytes 32768 | tf_op jit(solution)/shard_map/all_to_all | solution.py:61
Sparse Core Ops, SparseCore 0:
  25.3 43.8 all-gather.6
  75.1 39.1 all-gather.8

commit v12 on v11

--- a/solution.py
+++ b/solution.py
@@ -22,7 +22,7 @@
 def sum_to_owner(terms, n_mp):
     pieces = terms.astype(jnp.bfloat16).reshape((n_mp, terms.shape[0] // n_mp) + terms.shape[1:])
     got = lax.all_to_all(pieces, MP, split_axis=0, concat_axis=0, tiled=True)
-    return jnp.sum(got.astype(jnp.float32), axis=0).astype(jnp.bfloat16).astype(jnp.float32)
+    return jnp.sum(got.astype(jnp.float32), axis=0)
 
 
 def gather_over_y(pieces, lanes):

time: 211 us -> 211 us (level)
  no operation moved by 1% of the time
where the time goes in v12:
time: 211 us; the launch traced here: 210 us
  blocking collectives  69 us (33%)
  waiting for transfers between devices  40.8 us (19%)
  local copies, waits for them, and re-layouts  34.8 us (16%)
  starting transfers between devices  26.9 us (13%)
  matrix products  21.4 us (10%)
  between operations  14.5 us (7%)
  other arithmetic  2.81 us (1%)
    all_to_all x1, blocking collectives, body(): lax.all_to_all(jnp.broadcast_to(both[None], (n_mp,) + both.shape), MP, sp...  21.7 us
    all_to_all x1, blocking collectives, body(): lax.all_to_all(codes.reshape(page_owners, cap), DP, split_axis=0, concat_...  20.8 us
    all_to_all x1, waiting for transfers between devices, body(): recv = lax.all_to_all(sent, DP, split_axis=0, concat_axis=0, tiled=True)  16.4 us
    all_to_all x2, waiting for transfers between devices, sum_to_owner(): got = lax.all_to_all(pieces, MP, split_axis=0, concat_axis=0, tiled=True)  14.5 us
    all_gather x1, blocking collectives, gather_over_y(): return lax.all_gather(flat_pieces, DP[0], axis=0, tiled=False)  13.5 us
    all_gather x1, blocking collectives, body(): second_y = lax.all_gather(jnp.stack(second), DP[0], axis=1, tiled=False)  13 us
    gather x1, local copies, waits for them, and re-layouts, body(): chosen = pages[where_local]  11.9 us
    all_to_all x1, waiting for transfers between devices, return_maxima(): lax.all_to_all(maxima.astype(jnp.bfloat16), DP, split_axis=0, concat_axis...  9.79 us
  transfers between devices with their start and end apart: 7, of which 4 were waited for; matrix products, arithmetic and copies ran while one was open for 16% of the time, Pallas kernels for 0%

profile of v12, /device:TPU:2, one launch (start us, length us, event | category | flops | bytes accessed | tf_op | source)
XLA Modules:
  0.0 210.2 jit_solution(14906710079511475075)
XLA Ops:
  7.2 4.3 %concatenate.6 = bf16[272,128]{1,0:T(8,128)(2,1)S(1)} concatenate(bf16[32,128]{1,0:T(8,128)(2,1)} %param.15, bf16[32,128]{1,0:T(8,128)(2,1)} %param.16, bf16[32,128]{1,0:T(8,128)(2,1)} %param.17, bf16[32,128]{1,0:T(8,128)(2,1)} %bitcast.186, bf16[128,128]{1,0:T(8,128)(2,1)} %bitcast.183, bf16[4,128]{1,0:T(4,128)(2,1)} %param.23, bf16[12,128]{1,0:T(8,128)(2,1)S(1)} %broadcast_in_dim.25), dimensions={0} | concatenate | bytes 139264 | tf_op jit(solution)/shard_map/concatenate | solution.py:31
  11.6 13.5 %all-gather = bf16[1088,128]{1,0:T(8,128)(2,1)} all-gather(bf16[272,128]{1,0:T(8,128)(2,1)S(1)} %concatenate.6), channel_id=2, replica_groups=mesh['y'=4,'z'=8,'x'=4,'c'=2] {'y'}, dimensions={0}, use_global_device_ids=true | all-gather | bytes 348160 | tf_op jit(solution)/shard_map/all_gather | solution.py:32
  28.8 20.8 %all_to_all.42 = s32[32,1,8]{2,1,0:T(1,128)S(1)} all-to-all(s32[32,1,8]{2,1,0:T(1,128)S(1)} %bitcast.182), channel_id=1, replica_groups=mesh['y'=4,'z'=8,'x'=4,'c'=2] {'y','z'}, dimensions={0} | all-to-all | bytes 2048 | tf_op jit(solution)/shard_map/all_to_all | solution.py:107
  49.6 2.0 broadcast_in_dim.28
  51.6 4.8 %all-to-all-start.1 = ((bf16[8,2,32,1024]{3,2,1,0:T(8,128)(2,1)}), bf16[8,2,32,1024]{3,2,1,0:T(8,128)(2,1)S(1)}, u32[]{:S(2)}, u32[]{:S(2)}) async-start(bf16[8,2,32,1024]{3,2,1,0:T(8,128)(2,1)} %broadcast_in_dim.28), calls=%async_computation.1 | async-start | bytes 2097152 | tf_op jit(solution)/shard_map/all_to_all | solution.py:129
  56.5 13.0 %all-gather.2 = bf16[2,512,128]{2,1,0:T(8,128)(2,1)} all-gather(bf16[2,128,128]{2,1,0:T(8,128)(2,1)S(1)} %pad_maximum_fusion.1), channel_id=4, replica_groups=mesh['y'=4,'z'=8,'x'=4,'c'=2] {'y'}, dimensions={1}, use_global_device_ids=true | all-gather | bytes 327680 | tf_op jit(solution)/shard_map/all_gather | solution.py:108
  70.3 1.3 slice.64
  71.7 1.3 fusion.119
  76.7 1.4 fusion.7
  78.9 1.4 fusion.5
  81.7 1.4 convolution_convert_fusion
  83.2 4.8 %all-to-all-start.2 = ((bf16[8,64,1024]{2,1,0:T(8,128)(2,1)}), bf16[8,64,1024]{2,1,0:T(8,128)(2,1)S(1)}, u32[]{:S(2)}, u32[]{:S(2)}) async-start(bf16[8,64,1024]{2,1,0:T(8,128)(2,1)} %bitcast.47), calls=%async_computation.2 | async-start | bytes 2097152 | tf_op jit(solution)/shard_map/all_to_all | solution.py:24
  88.1 1.9 gather_fusion.2
  90.2 11.9 %gather_fusion.1 = bf16[256,128,128]{2,1,0:T(8,128)(2,1)} fusion(bf16[256,128,128]{2,1,0:T(8,128)(2,1)} %param.24, s32[1024]{0:T(1024)S(1)} %pad_clamp_fusion.1), kind=kCustom, calls=%fused_computation.1 | custom fusion | bytes 16778240 | tf_op jit(solution)/shard_map/gather | solution.py:117
  103.4 21.7 %all_to_all.43 = bf16[8,80,1024]{2,1,0:T(8,128)(2,1)S(1)} all-to-all(bf16[8,80,1024]{2,1,0:T(8,128)(2,1)S(1)} %broadcast_in_dim.29), channel_id=1, replica_groups=mesh['y'=4,'z'=8,'x'=4,'c'=2] {'x','c'}, dimensions={0} | all-to-all | bytes 2621440 | tf_op jit(solution)/shard_map/all_to_all | solution.py:165
  125.2 3.0 %fusion.120 = (bf16[1,4,1024,128]{3,2,1,0:T(8,128)(2,1)}, bf16[1,4,1024,128]{3,2,1,0:T(8,128)(2,1)}) fusion(bf16[2,4,1024,128]{3,2,1,0:T(8,128)(2,1)} %all-gather.9.cloned.1.call-done), kind=kLoop, calls=%fused_computation.190 | loop fusion | bytes 4194304 | tf_op jit(solution)/shard_map/slice | solution.py:116
  128.2 6.0 %convolution_convert_fusion.1 = bf16[512,1024]{1,0:T(8,128)(2,1)} fusion(bf16[1024,512]{1,0:T(8,128)(2,1)} %bitcast.169, bf16[512,1024]{1,0:T(8,128)(2,1)S(1)} %bitcast.166, bf16[1024,512]{1,0:T(8,128)(2,1)} %bitcast.168), kind=kOutput, calls=%fused_computation.19 | convolution fusion | flops 1091305472 | bytes 4194304 | tf_op jit(solution)/shard_map/dot_general | solution.py:173
  134.2 4.8 %all-to-all-start.4 = ((bf16[8,64,1024]{2,1,0:T(8,128)(2,1)}), bf16[8,64,1024]{2,1,0:T(8,128)(2,1)S(1)}, u32[]{:S(2)}, u32[]{:S(2)}) async-start(bf16[8,64,1024]{2,1,0:T(8,128)(2,1)} %bitcast.165), calls=%async_computation.4 | async-start | bytes 2097152 | tf_op jit(solution)/shard_map/all_to_all | solution.py:24
  139.3 14.2 %all-to-all-done.4 = bf16[8,64,1024]{2,1,0:T(8,128)(2,1)S(1)} async-done(((bf16[8,64,1024]{2,1,0:T(8,128)(2,1)}), bf16[8,64,1024]{2,1,0:T(8,128)(2,1)S(1)}, u32[]{:S(2)}, u32[]{:S(2)}) %all-to-all-start.4) | async-done | bytes 1048608 | tf_op jit(solution)/shard_map/all_to_all | solution.py:24
  155.5 6.7 %all-to-all-start.5 = ((bf16[32,2,32,128]{3,2,1,0:T(8,128)(2,1)}), bf16[32,2,32,128]{3,2,1,0:T(8,128)(2,1)S(1)}, u32[]{:S(2)}, u32[]{:S(2)}) async-start(bf16[32,2,32,128]{3,2,1,0:T(8,128)(2,1)} %broadcast_in_dim.32), calls=%async_computation.5 | async-start | bytes 1048576 | tf_op jit(solution)/shard_map/all_to_all | solution.py:184
  162.3 16.4 %all-to-all-done.5 = bf16[32,2,32,128]{3,2,1,0:T(8,128)(2,1)S(1)} async-done(((bf16[32,2,32,128]{3,2,1,0:T(8,128)(2,1)}), bf16[32,2,32,128]{3,2,1,0:T(8,128)(2,1)S(1)}, u32[]{:S(2)}, u32[]{:S(2)}) %all-to-all-start.5) | async-done | bytes 524320 | tf_op jit(solution)/shard_map/all_to_all | solution.py:184
  178.7 6.7 %select_reduce_fusion = f32[32,8,2,32]{3,2,1,0:T(2,128)S(1)} fusion(pred[32,8,128]{2,1,0:T(8,128)(4,1)S(1)} %iota_compare_fusion.1, bf16[32,8,128,128]{3,2,1,0:T(8,128)(2,1)} %bitcast.153, bf16[32,2,32,128]{3,2,1,0:T(8,128)(2,1)S(1)} %all-to-all-done.5), kind=kOutput, calls=%fused_computation.8 | convolution fusion | flops 541048832 | bytes 9011200 | tf_op jit(solution)/shard_map/sqie,snte->snqit/dot_general | solution.py:186
  186.4 5.7 %all-to-all-start.6 = ((bf16[32,2,128]{2,1,0:T(2,128)(2,1)}), bf16[32,2,128]{2,1,0:T(2,128)(2,1)S(1)}, u32[]{:S(2)}, u32[]{:S(2)}) async-start(bf16[32,2,128]{2,1,0:T(2,128)(2,1)} %reshape.365), calls=%async_computation.6 | async-start | bytes 32768 | tf_op jit(solution)/shard_map/all_to_all | solution.py:61
  192.1 9.8 %all-to-all-done.6 = bf16[32,2,128]{2,1,0:T(2,128)(2,1)S(1)} async-done(((bf16[32,2,128]{2,1,0:T(2,128)(2,1)}), bf16[32,2,128]{2,1,0:T(2,128)(2,1)S(1)}, u32[]{:S(2)}, u32[]{:S(2)}) %all-to-all-start.6) | async-done | bytes 16416 | tf_op jit(solution)/shard_map/all_to_all | solution.py:61
  (95 shorter events, 16.7 us)
Async XLA Ops:
  7.2 18.9 %copy-start = (s32[8192]{0:T(1024)S(1)}, s32[8192]{0:T(1024)}, u32[]{:S(2)}) copy-start(s32[8192]{0:T(1024)} %param.26) | copy-start | bytes 98308
  7.2 62.3 %all-gather.7.cloned.1.call-start = ((), (), s32[]{:S(2)}) async-start(), calls=%async_computation.7 | async-start | bytes 2506752 | tf_op jit(solution)/shard_map/all_gather | solution.py:36
  25.2 31.3 %copy-start.5 = (bf16[512,32]{0,1:T(8,128)(2,1)S(1)}, bf16[512,32]{0,1:T(8,128)(2,1)}, u32[]{:S(2)}) copy-start(bf16[512,32]{0,1:T(8,128)(2,1)} %param.22) | copy-start | bytes 98308
  25.2 31.3 %copy-start.6 = (bf16[32,512]{1,0:T(8,128)(2,1)S(1)}, bf16[32,512]{1,0:T(8,128)(2,1)}, u32[]{:S(2)}) copy-start(bf16[32,512]{1,0:T(8,128)(2,1)} %param.21) | copy-start | bytes 98308
  51.6 22.3 %all-to-all-start.1 = ((bf16[8,2,32,1024]{3,2,1,0:T(8,128)(2,1)}), bf16[8,2,32,1024]{3,2,1,0:T(8,128)(2,1)S(1)}, u32[]{:S(2)}, u32[]{:S(2)}) async-start(bf16[8,2,32,1024]{3,2,1,0:T(8,128)(2,1)} %broadcast_in_dim.28), calls=%async_computation.1 | async-start | bytes 2097152 | tf_op jit(solution)/shard_map/all_to_all | solution.py:129
  56.5 68.8 %all-gather.9.cloned.1.call-start = ((), (), s32[]{:S(2)}) async-start(), calls=%async_computation.8 | async-start | bytes 2359296 | tf_op jit(solution)/shard_map/all_gather | solution.py:114
  75.6 1.2 copy-start.3
  81.6 6.5 %copy-start.1 = (s32[256]{0:T(256)S(1)}, s32[256]{0:T(256)}, u32[]{:S(2)}) copy-start(s32[256]{0:T(256)} %param.25) | copy-start | bytes 3076
  83.2 19.3 %all-to-all-start.2 = ((bf16[8,64,1024]{2,1,0:T(8,128)(2,1)}), bf16[8,64,1024]{2,1,0:T(8,128)(2,1)S(1)}, u32[]{:S(2)}, u32[]{:S(2)}) async-start(bf16[8,64,1024]{2,1,0:T(8,128)(2,1)} %bitcast.47), calls=%async_computation.2 | async-start | bytes 2097152 | tf_op jit(solution)/shard_map/all_to_all | solution.py:24
  90.2 12.5 %copy-start.2 = (bf16[2,32,1024]{2,1,0:T(8,128)(2,1)S(1)}, bf16[2,32,1024]{2,1,0:T(8,128)(2,1)}, u32[]{:S(2)}) copy-start(bf16[2,32,1024]{2,1,0:T(8,128)(2,1)} %param.14) | copy-start | bytes 393220
  134.2 19.3 %all-to-all-start.4 = ((bf16[8,64,1024]{2,1,0:T(8,128)(2,1)}), bf16[8,64,1024]{2,1,0:T(8,128)(2,1)S(1)}, u32[]{:S(2)}, u32[]{:S(2)}) async-start(bf16[8,64,1024]{2,1,0:T(8,128)(2,1)} %bitcast.165), calls=%async_computation.4 | async-start | bytes 2097152 | tf_op jit(solution)/shard_map/all_to_all | solution.py:24
  154.5 30.9 %copy-start.4 = (bf16[64,128]{1,0:T(8,128)(2,1)}, bf16[64,128]{1,0:T(8,128)(2,1)S(1)}, u32[]{:S(2)}) copy-start(bf16[64,128]{1,0:T(8,128)(2,1)S(1)} %divide_convert_fusion.4) | copy-start | bytes 49156
  155.5 23.3 %all-to-all-start.5 = ((bf16[32,2,32,128]{3,2,1,0:T(8,128)(2,1)}), bf16[32,2,32,128]{3,2,1,0:T(8,128)(2,1)S(1)}, u32[]{:S(2)}, u32[]{:S(2)}) async-start(bf16[32,2,32,128]{3,2,1,0:T(8,128)(2,1)} %broadcast_in_dim.32), calls=%async_computation.5 | async-start | bytes 1048576 | tf_op jit(solution)/shard_map/all_to_all | solution.py:184
  186.4 15.5 %all-to-all-start.6 = ((bf16[32,2,128]{2,1,0:T(2,128)(2,1)}), bf16[32,2,128]{2,1,0:T(2,128)(2,1)S(1)}, u32[]{:S(2)}, u32[]{:S(2)}) async-start(bf16[32,2,128]{2,1,0:T(2,128)(2,1)} %reshape.365), calls=%async_computation.6 | async-start | bytes 32768 | tf_op jit(solution)/shard_map/all_to_all | solution.py:61
Sparse Core Ops, SparseCore 0:
  25.3 43.8 all-gather.6
  75.1 39.1 all-gather.8
